TPU v7x, 512 devices: a whole 4x8x8 slice. The times are simulated.
512 devices in a mesh: ctx: 16 (over y, x_hi), tp: 32 (over z, x_lo, core).
Axes of the slice: x: 4 (x_hi: 2, x_lo: 2; x = x_hi * 2 + x_lo), y: 8, z: 8, core: 2. Of those that a mesh axis runs over, the one named last changes fastest.
Arguments:
- resid_in: bfloat16 [2048, 4096], P('ctx', 'tp'), may hold values from -6 to 6
- feats: bfloat16 [2048, 3, 4096], P('ctx', None, 'tp'), may hold values from -6 to 6
- short_filter: float32 [3, 3, 4096], P(None, None, 'tp'), may hold values from -3.5 to 3.5
- residues: float32 [4096, 16], P('tp'), may hold values from -4 to 4
- rates: float32 [4096, 16], P('tp'), may hold values from 0.00014648438 to 0.03
- out_weight: bfloat16 [4096, 4096], P('tp'), may hold values from -0.1875 to 0.1875
- norm_gain: float32 [4096], replicated, may hold values from 0.1 to 1.9
- attn_weight: bfloat16 [4096, 3, 4096], P(None, None, 'tp'), may hold values from -1 to 1
Outputs:
- hyena_out: bfloat16 [2048, 4096], P('ctx', 'tp')
- context: bfloat16 [2048, 4096], P('ctx', 'tp')
All inputs are finite; a program needn't handle non-finite values.
Results may differ from a plain program's by a relative error of at most 0.01.
Values may be sent and summed in bfloat16 or wider, within the bound.
No kernel may reach another device: no remote copies, remote signals or barrier semaphores. Data moves between devices by JAX's collectives and lax.ppermute only.
A program may use at most 192 MiB of HBM per device.

v0:
```python
import math

import jax
import jax.numpy as jnp
from jax import lax
from jax.sharding import PartitionSpec as P

HEAD_DIM = 128


eps_norm = 1e-05
rope_base = 10000.0
mask_fill = -1e30
highest = lax.Precision.HIGHEST


def shifted(value, axis, steps):
    count = lax.axis_size(axis)
    initial, last = (max(0, -steps), min(count, count - steps))
    return lax.ppermute(value, axis, [(source, source + steps) for source in range(initial, last)])


def toeplitz_lower(filter_taps):
    chan_count, block_size = filter_taps.shape
    padded = jnp.concatenate(
        [jnp.zeros((chan_count, block_size - 1), jnp.float32), filter_taps], axis=1
    )
    flipped = padded[:, ::-1]
    tiled = jnp.tile(flipped, (1, block_size))
    offset = block_size - 1
    window = tiled[:, offset : offset + block_size * (2 * block_size - 2)]
    return window.reshape(chan_count, block_size, 2 * block_size - 2)[:, :, :block_size]


def modal_conv(signal, residues, rates, start_state):
    chan_count, length = signal.shape
    block_size = math.gcd(length, 128)
    block_count = length // block_size
    weight = residues * jnp.sqrt(1.0 - jnp.exp(-2.0 * rates))
    lag_steps = jnp.arange(block_size, dtype=jnp.float32)
    powers = jnp.exp(-rates[:, :, None] * lag_steps)
    filter_taps = jnp.sum(weight[:, :, None] * powers, axis=1)
    toeplitz = toeplitz_lower(filter_taps)
    blocks = signal.reshape(chan_count, block_count, block_size)
    inner_part = jnp.einsum("cij,cnj->cni", toeplitz, blocks, precision=highest)
    tail_powers = jnp.exp(-rates[:, :, None] * (block_size - lag_steps))
    end_states = jnp.einsum("cnj,cmj->cnm", blocks, tail_powers, precision=highest)
    block_steps = jnp.arange(block_count, dtype=jnp.float32)
    gap_count = block_steps[:, None] - 1.0 - block_steps[None, :]
    live_mask = gap_count >= 0.0
    carry_mat = jnp.where(
        live_mask, jnp.exp(-rates[:, :, None, None] * block_size * jnp.maximum(gap_count, 0.0)), 0.0
    )
    states = jnp.einsum("cmnk,ckm->cnm", carry_mat, end_states, precision=highest)
    states = (
        states
        + jnp.exp(-rates[:, None, :] * block_size * block_steps[None, :, None])
        * start_state[:, None, :]
    )
    cross_part = jnp.einsum("cnm,cmi->cni", states * weight[:, None, :], powers, precision=highest)
    return (inner_part + cross_part).reshape(chan_count, length)


def short_mix(feats, short_filter):
    row_count = feats.shape[0]
    prior_feats = shifted(feats[-2:], "ctx", 1)
    joined = jnp.concatenate([prior_feats, feats], axis=0).astype(jnp.float32)
    return (
        short_filter[0] * joined[2:]
        + short_filter[1] * joined[1 : row_count + 1]
        + short_filter[2] * joined[:row_count]
    )


def rotary_turn(vectors, positions):
    half_dim = vectors.shape[-1] // 2
    frequency = rope_base ** (-jnp.arange(half_dim, dtype=jnp.float32) * 2.0 / vectors.shape[-1])
    angles = positions.astype(jnp.float32)[:, None] * frequency[None, :]
    cosine = jnp.cos(angles)[:, None, :]
    sine_part = jnp.sin(angles)[:, None, :]
    first_half = vectors[..., :half_dim]
    second = vectors[..., half_dim:]
    return jnp.concatenate(
        [first_half * cosine - second * sine_part, second * cosine + first_half * sine_part],
        axis=-1,
    )


def attend_tile(running, query_rows, query_pos, key_block, value_block, key_start):
    run_peak, denom, accumulated = running
    block_size = key_block.shape[0]
    score_scale = 1.0 / math.sqrt(key_block.shape[2])
    key_pos = key_start + jnp.arange(block_size, dtype=jnp.int32)
    scores = (
        jnp.einsum("shd,khd->hsk", query_rows, key_block, preferred_element_type=jnp.float32)
        * score_scale
    )
    allowed = (query_pos[:, None] >= key_pos[None, :])[None]
    masked = jnp.where(allowed, scores, mask_fill)
    new_peak = jnp.maximum(run_peak, jnp.max(masked, axis=2))
    weights = jnp.where(allowed, jnp.exp(masked - new_peak[:, :, None]), 0.0)
    factor = jnp.exp(run_peak - new_peak)
    denom = denom * factor + jnp.sum(weights, axis=2)
    accumulated = accumulated * factor[:, :, None] + jnp.einsum(
        "hsk,khd->hsd",
        weights.astype(jnp.bfloat16),
        value_block,
        preferred_element_type=jnp.float32,
    )
    return (new_peak, denom, accumulated)


def empty_state(head_count, rows):
    return (
        jnp.full((head_count, rows), mask_fill, jnp.float32),
        jnp.zeros((head_count, rows), jnp.float32),
        jnp.zeros((head_count, rows, HEAD_DIM), jnp.float32),
    )


def finish_rows(state):
    run_peak, denom, accumulated = state
    heads_out = accumulated / denom[:, :, None]
    rows = heads_out.shape[1]
    return (
        heads_out.transpose(1, 0, 2)
        .reshape(rows, heads_out.shape[0] * heads_out.shape[2])
        .astype(jnp.bfloat16)
    )


def per_device(resid_in, feats, short_filter, residues, rates, out_weight, norm_gain, attn_weight):
    row_count, chan_count = resid_in.shape
    width_all = out_weight.shape[1]
    short_out = short_mix(feats, short_filter)
    product = (short_out[:, 1] * short_out[:, 2]).astype(jnp.bfloat16)
    panel_rows = lax.all_to_all(product.T, "ctx", split_axis=0, concat_axis=1, tiled=True)
    panel_count = chan_count // lax.axis_size("ctx")
    panel_start = lax.axis_index("ctx") * panel_count
    panel_res = lax.dynamic_slice_in_dim(residues, panel_start, panel_count, 0)
    panel_rates = lax.dynamic_slice_in_dim(rates, panel_start, panel_count, 0)
    panel_conv = modal_conv(
        panel_rows.astype(jnp.float32), panel_res, panel_rates, jnp.zeros_like(panel_rates)
    )
    returned = lax.all_to_all(panel_conv, "ctx", split_axis=1, concat_axis=0, tiled=True)
    conv_out = returned.T
    gated = (short_out[:, 0] * conv_out).astype(jnp.bfloat16)
    own_share = lax.psum_scatter(
        lax.dot_general(
            out_weight, gated, (((0,), (1,)), ((), ())), preferred_element_type=jnp.float32
        ),
        "tp",
        scatter_dimension=0,
        tiled=True,
    )
    hyena_out = (resid_in.astype(jnp.float32) + own_share.T).astype(jnp.bfloat16)
    full_rows = lax.all_gather(hyena_out, "tp", axis=1, tiled=True)
    wide = full_rows.astype(jnp.float32)
    mean_square = jnp.mean(wide * wide, axis=1, keepdims=True)
    normed = (wide * lax.rsqrt(mean_square + eps_norm) * norm_gain).astype(jnp.bfloat16)
    projected = jnp.dot(
        normed, attn_weight.reshape(width_all, 3 * chan_count), preferred_element_type=jnp.float32
    ).reshape(row_count, 3, chan_count)
    head_count = chan_count // HEAD_DIM
    ctx_index = lax.axis_index("ctx")
    first_pos = ctx_index * row_count
    positions = first_pos + jnp.arange(row_count, dtype=jnp.int32)
    queries = rotary_turn(
        projected[:, 0].reshape(row_count, head_count, HEAD_DIM), positions
    ).astype(jnp.bfloat16)
    keys_all = rotary_turn(
        projected[:, 1].reshape(row_count, head_count, HEAD_DIM), positions
    ).astype(jnp.bfloat16)
    values = projected[:, 2].astype(jnp.bfloat16)
    key_pieces = (keys_all.reshape(row_count, chan_count), values)
    initial = empty_state(head_count, row_count)
    key_rows = lax.all_gather(key_pieces[0], "ctx", axis=0, tiled=True)
    value_rows = lax.all_gather(key_pieces[1], "ctx", axis=0, tiled=True)
    key_total = key_rows.shape[0]
    tiles_block_size = math.gcd(key_total, 1024)
    block_count = key_total // tiles_block_size
    key_blocks = key_rows.reshape(block_count, tiles_block_size, head_count, HEAD_DIM)
    value_blocks = value_rows.reshape(block_count, tiles_block_size, head_count, HEAD_DIM)
    key_blocks, value_blocks, block_ids, block_size = (
        key_blocks,
        value_blocks,
        jnp.arange(block_count, dtype=jnp.int32),
        tiles_block_size,
    )

    def one_tile(carried, slot_item):
        key_block, value_block, block_index = slot_item
        key_start = block_index * block_size
        updated = attend_tile(carried, queries, positions, key_block, value_block, key_start)
        return (updated, None)

    result, _ = lax.scan(one_tile, initial, (key_blocks, value_blocks, block_ids))
    context = finish_rows(result)
    return (hyena_out, context)


def solution(mesh):
    in_specs = (
        P("ctx", "tp"),
        P("ctx", None, "tp"),
        P(None, None, "tp"),
        P("tp", None),
        P("tp", None),
        P("tp", None),
        P(),
        P(None, None, "tp"),
    )
    out_specs = (P("ctx", "tp"), P("ctx", "tp"))
    return jax.shard_map(
        per_device, mesh=mesh, in_specs=in_specs, out_specs=out_specs, check_vma=False
    )
```

profile of v0, /device:TPU:6, one launch (start us, length us, event | category | flops | bytes accessed | tf_op | source)
XLA Modules:
  0.0 341.2 jit_solution(16704651836069771264)
XLA Ops:
  7.2 0.8 slice.59
  8.1 4.3 %collective-permute-start = (bf16[2,3,128]{0,2,1:T(8,128)(2,1)S(1)}, bf16[2,3,128]{0,2,1:T(8,128)(2,1)S(1)}, u32[]{:S(2)}, u32[]{:S(2)}) collective-permute-start(bf16[2,3,128]{0,2,1:T(8,128)(2,1)S(1)} %copy.44), channel_id=1, source_target_pairs={{0,32},{32,64},{64,96},{96,128},{128,160},{160,192},{192,224},{224... | collective-permute-start | bytes 4616 | tf_op jit(solution)/shard_map/ppermute | solution.py:20
  12.6 0.8 constant_dynamic-slice_fusion
  13.6 0.7 slice_bitcast_fusion.3
  14.4 1.0 copy.45
  15.8 0.6 tile.10
  16.4 0.3 slice.81
  16.8 1.6 reshape.257
  18.5 0.3 fusion.34
  18.9 0.6 fusion.65
  19.5 9.2 %all-to-all-start = ((bf16[16,8,128]{2,1,0:T(8,128)(2,1)}), bf16[16,8,128]{2,1,0:T(8,128)(2,1)S(1)}, u32[]{:S(2)}, u32[]{:S(2)}) async-start(bf16[16,8,128]{2,1,0:T(8,128)(2,1)} %fusion.65), calls=%async_computation | async-start | bytes 65536 | tf_op jit(solution)/shard_map/all_to_all | solution.py:137
  28.7 7.4 %all-to-all-done = bf16[16,8,128]{2,1,0:T(8,128)(2,1)S(1)} async-done(((bf16[16,8,128]{2,1,0:T(8,128)(2,1)}), bf16[16,8,128]{2,1,0:T(8,128)(2,1)S(1)}, u32[]{:S(2)}, u32[]{:S(2)}) %all-to-all-start) | async-done | bytes 32800 | tf_op jit(solution)/shard_map/all_to_all | solution.py:137
  36.4 0.6 multiply_reduce_fusion
  37.1 0.5 fusion.32
  37.9 13.1 %all_to_all.32 = f32[8,16,128]{2,0,1:T(8,128)S(1)} all-to-all(f32[8,16,128]{2,0,1:T(8,128)S(1)} %copy.49), channel_id=1, replica_groups=mesh['ctx'=16,'tp'=32] {'ctx'}, dimensions={1} | all-to-all | bytes 131072 | tf_op jit(solution)/shard_map/all_to_all | solution.py:145
  51.1 1.8 convolution_bitcast_fusion.1
  53.0 117.8 %reduce-scatter.2.cloned.1.call-done = f32[128,128]{0,1:T(8,128)} async-done(((f32[4096,128]{0,1:T(8,128)}), f32[128,128]{0,1:T(8,128)}) %reduce-scatter.2.cloned.1.call-update) | async-done | bytes 65552 | tf_op jit(solution)/shard_map/reduce_scatter | solution.py:148
  170.8 1.5 fusion.39
  172.3 4.7 %copy.50 = bf16[4096,3,128]{0,2,1:T(8,128)(2,1)} copy(bf16[4096,3,128]{2,0,1:T(8,128)(2,1)} %param.17) | data formatting | bytes 6291456 | tf_op args[7]
  177.1 63.0 %all-gather.3.cloned.1.call-done = bf16[128,4096]{1,0:T(8,128)(2,1)} async-done(((bf16[128,128]{1,0:T(8,128)(2,1)}), bf16[128,4096]{1,0:T(8,128)(2,1)}) %all-gather.3.cloned.1.call-update) | async-done | bytes 1048592 | tf_op jit(solution)/shard_map/all_gather | solution.py:157
  240.1 1.5 fusion.25
  241.6 3.3 fusion.23
  245.3 40.2 %all_gather.10 = bf16[2048,128]{0,1:T(8,128)(2,1)S(1)} all-gather(bf16[128,128]{0,1:T(8,128)(2,1)S(1)} %pad_maximum_fusion), channel_id=1, replica_groups=mesh['ctx'=16,'tp'=32] {'ctx'}, dimensions={0}, use_global_device_ids=true | all-gather | bytes 557056 | tf_op jit(solution)/shard_map/all_gather | solution.py:177
  285.8 42.9 %all-gather = bf16[2048,1,128]{0,2,1:T(8,128)(2,1)S(1)} all-gather(bf16[128,1,128]{0,2,1:T(8,128)(2,1)S(1)} %slice.136), channel_id=2, replica_groups=mesh['ctx'=16,'tp'=32] {'ctx'}, dimensions={0}, use_global_device_ids=true | all-gather | bytes 557056 | tf_op jit(solution)/shard_map/all_gather | solution.py:178
  329.0 4.6 %while.15 = (s32[]{:T(128)}, f32[1,128]{1,0:T(1,128)S(1)}, f32[1,128]{1,0:T(1,128)S(1)}, f32[1,128,128]{2,1,0:T(8,128)S(1)}, s32[2]{0:T(128)S(1)}, /*index=5*/bf...) while((s32[]{:T(128)}, f32[1,128]{1,0:T(1,128)S(1)}, ...), condition=%wide.region_6.7_spmd.clone, body=%wide.region_3.6_spmd.clone.sunk | while | flops 68732800 | bytes 2287785 | solution.py:197
  329.0 0.6 dynamic_slice.39
  330.3 0.3 fusion.93
  330.6 0.4 fusion.97
  331.3 0.6 dynamic_slice.39
  332.6 0.3 fusion.93
  332.9 0.4 fusion.97
  333.6 0.7 fusion.74
  (56 shorter events, 3.4 us)
Async XLA Ops:
  7.2 43.9 %copy-start = (bf16[128,4096]{1,0:T(8,128)(2,1)S(1)}, bf16[128,4096]{1,0:T(8,128)(2,1)}, u32[]{:S(2)}) copy-start(bf16[128,4096]{1,0:T(8,128)(2,1)} %param.15) | copy-start | bytes 3145732
  8.1 10.2 %collective-permute-start = (bf16[2,3,128]{0,2,1:T(8,128)(2,1)S(1)}, bf16[2,3,128]{0,2,1:T(8,128)(2,1)S(1)}, u32[]{:S(2)}, u32[]{:S(2)}) collective-permute-start(bf16[2,3,128]{0,2,1:T(8,128)(2,1)S(1)} %copy.44), channel_id=1, source_target_pairs={{0,32},{32,64},{64,96},{96,128},{128,160},{160,192},{192,224},{224... | collective-permute-start | bytes 4616 | tf_op jit(solution)/shard_map/ppermute | solution.py:20
  19.5 16.6 %all-to-all-start = ((bf16[16,8,128]{2,1,0:T(8,128)(2,1)}), bf16[16,8,128]{2,1,0:T(8,128)(2,1)S(1)}, u32[]{:S(2)}, u32[]{:S(2)}) async-start(bf16[16,8,128]{2,1,0:T(8,128)(2,1)} %fusion.65), calls=%async_computation | async-start | bytes 65536 | tf_op jit(solution)/shard_map/all_to_all | solution.py:137
  28.7 142.1 %reduce-scatter.2.cloned.1.call-start = ((), (), s32[]{:S(2)}) async-start(), calls=%async_computation.3 | async-start | bytes 2162688 | tf_op jit(solution)/shard_map/reduce_scatter | solution.py:148
  51.1 119.7 %copy-start.1 = (bf16[128,128]{1,0:T(8,128)(2,1)S(1)}, bf16[128,128]{1,0:T(8,128)(2,1)}, u32[]{:S(2)}) copy-start(bf16[128,128]{1,0:T(8,128)(2,1)} %param.10) | copy-start | bytes 98308
  52.9 187.2 %all-gather.3.cloned.1.call-start = ((), (), s32[]{:S(2)}) async-start(), calls=%async_computation.4 | async-start | bytes 1081344 | tf_op jit(solution)/shard_map/all_gather | solution.py:157
  172.3 69.3 %copy-start.2 = (f32[4096]{0:T(1024)S(1)}, f32[4096]{0:T(1024)}, u32[]{:S(2)}) copy-start(f32[4096]{0:T(1024)} %param.16) | copy-start | bytes 49156
Sparse Core Ops, SparseCore 0:
  53.0 117.7 reduce-scatter.1
  173.6 66.4 all-gather.2
where the time goes:
time: 342 us; the launch traced here: 341 us
  waiting for transfers between devices  188 us (55%)
  blocking collectives  96.3 us (28%)
  between operations  14.3 us (4%)
  starting transfers between devices  13.6 us (4%)
  local copies, waits for them, and re-layouts  13.3 us (4%)
  matrix products  7.62 us (2%)
  other arithmetic  6.39 us (2%)
    reduce_scatter x1, waiting for transfers between devices, per_device(): lax.psum_scatter(lax.dot_general(out_weight, gated, (((0,), (1,)), ((), (...  118 us
    all_gather x1, waiting for transfers between devices, per_device(): full_rows = lax.all_gather(hyena_out, 'tp', axis=1, tiled=True)  63 us
    all_gather x1, blocking collectives, per_device(): value_rows = lax.all_gather(key_pieces[1], 'ctx', axis=0, tiled=True)  42.9 us
    all_gather x1, blocking collectives, per_device(): key_rows = lax.all_gather(key_pieces[0], 'ctx', axis=0, tiled=True)  40.2 us
    all_to_all x1, blocking collectives, per_device(): lax.all_to_all(panel_conv, 'ctx', split_axis=1, concat_axis=0, tiled=True)  13.1 us
    all_to_all x1, starting transfers between devices, per_device(): lax.all_to_all(product.T, 'ctx', split_axis=0, concat_axis=1, tiled=True)  9.18 us
    all_to_all x1, waiting for transfers between devices, per_device(): lax.all_to_all(product.T, 'ctx', split_axis=0, concat_axis=1, tiled=True)  7.39 us
  transfers between devices with their start and end apart: 4, of which 3 were waited for; matrix products, arithmetic and copies ran while one was open for 3% of the time, Pallas kernels for 0%

commit v1 on v0

--- a/solution.py
+++ b/solution.py
@@ -18,6 +18,12 @@
     count = lax.axis_size(axis)
     initial, last = (max(0, -steps), min(count, count - steps))
     return lax.ppermute(value, axis, [(source, source + steps) for source in range(initial, last)])
+
+
+def gather_by_exchange(block, axis, concat_axis=1):
+    count = lax.axis_size(axis)
+    copies = jnp.broadcast_to(block[None], (count,) + block.shape)
+    return lax.all_to_all(copies, axis, split_axis=0, concat_axis=concat_axis, tiled=False)
 
 
 def toeplitz_lower(filter_taps):
@@ -145,16 +151,16 @@
     returned = lax.all_to_all(panel_conv, "ctx", split_axis=1, concat_axis=0, tiled=True)
     conv_out = returned.T
     gated = (short_out[:, 0] * conv_out).astype(jnp.bfloat16)
-    own_share = lax.psum_scatter(
-        lax.dot_general(
-            out_weight, gated, (((0,), (1,)), ((), ())), preferred_element_type=jnp.float32
-        ),
-        "tp",
-        scatter_dimension=0,
-        tiled=True,
+    tp_count = lax.axis_size("tp")
+    partials = lax.dot_general(
+        out_weight, gated, (((0,), (1,)), ((), ())), preferred_element_type=jnp.float32
+    ).astype(jnp.bfloat16)
+    received = lax.all_to_all(partials, "tp", split_axis=0, concat_axis=0, tiled=True)
+    own_share = jnp.sum(
+        received.reshape(tp_count, chan_count, row_count).astype(jnp.float32), axis=0
     )
     hyena_out = (resid_in.astype(jnp.float32) + own_share.T).astype(jnp.bfloat16)
-    full_rows = lax.all_gather(hyena_out, "tp", axis=1, tiled=True)
+    full_rows = gather_by_exchange(hyena_out, "tp").reshape(row_count, width_all)
     wide = full_rows.astype(jnp.float32)
     mean_square = jnp.mean(wide * wide, axis=1, keepdims=True)
     normed = (wide * lax.rsqrt(mean_square + eps_norm) * norm_gain).astype(jnp.bfloat16)
@@ -174,8 +180,11 @@
     values = projected[:, 2].astype(jnp.bfloat16)
     key_pieces = (keys_all.reshape(row_count, chan_count), values)
     initial = empty_state(head_count, row_count)
-    key_rows = lax.all_gather(key_pieces[0], "ctx", axis=0, tiled=True)
-    value_rows = lax.all_gather(key_pieces[1], "ctx", axis=0, tiled=True)
+    joined_kv = jnp.concatenate(key_pieces, axis=1)
+    gathered_kv = gather_by_exchange(joined_kv, "ctx", concat_axis=0)
+    gathered_kv = gathered_kv.reshape(lax.axis_size("ctx") * row_count, 2 * chan_count)
+    key_rows = gathered_kv[:, :chan_count]
+    value_rows = gathered_kv[:, chan_count:]
     key_total = key_rows.shape[0]
     tiles_block_size = math.gcd(key_total, 1024)
     block_count = key_total // tiles_block_size

time: 342 us -> 168 us (0.49)
  waiting for transfers between devices: 188 us -> 59.6 us
  blocking collectives: 96.3 us -> 53.8 us
  between operations: 14.3 us -> 0.92 us
  starting transfers between devices: 13.6 us -> 23.9 us
  matrix products: 7.62 us -> 3.99 us
  local copies, waits for them, and re-layouts: 13.3 us -> 16.9 us
    reduce_scatter x1 -> x0, waiting for transfers between devices: 118 us -> none  [per_device(): lax.psum_scatter(lax.dot_general(out_weight, gated, (((0,), (1,)), ((), (...]
    all_gather x2 -> x0, blocking collectives: 83.1 us -> none  [the longest x1 42.9 us: per_device(): value_rows = lax.all_gather(key_pieces[1], 'ctx', axis=0, tiled=True)]
    all_gather x1 -> x0, waiting for transfers between devices: 63 us -> none  [per_device(): full_rows = lax.all_gather(hyena_out, 'tp', axis=1, tiled=True)]
    all_to_all x0 -> x2, waiting for transfers between devices: none -> 52.2 us  [gather_by_exchange(): lax.all_to_all(copies, axis, split_axis=0, concat_axis=concat_axis, tiled...]
    all_to_all x0 -> x1, blocking collectives: none -> 40.7 us  [per_device(): lax.all_to_all(partials, 'tp', split_axis=0, concat_axis=0, tiled=True)]
    all_to_all x0 -> x2, starting transfers between devices: none -> 10.4 us  [gather_by_exchange(): lax.all_to_all(copies, axis, split_axis=0, concat_axis=concat_axis, tiled...]
    unnamed x16 -> x18, local copies, waits for them, and re-layouts: 6.83 us -> 6.87 us
  transfers between devices with their start and end apart: 4 -> 4, of which waited for: 3 -> 3; matrix products, arithmetic and copies ran while one was open for 3% -> 6% of each run, Pallas kernels for 0% -> 0%
where the time goes in v1:
time: 168 us; the launch traced here: 165 us
  waiting for transfers between devices  59.6 us (35%)
  blocking collectives  53.8 us (32%)
  starting transfers between devices  23.9 us (14%)
  local copies, waits for them, and re-layouts  16.9 us (10%)
  other arithmetic  4.83 us (3%)
  matrix products  3.99 us (2%)
    all_to_all x2, waiting for transfers between devices, gather_by_exchange(): lax.all_to_all(copies, axis, split_axis=0, concat_axis=concat_axis, tiled...  52.2 us
    all_to_all x1, blocking collectives, per_device(): lax.all_to_all(partials, 'tp', split_axis=0, concat_axis=0, tiled=True)  40.7 us
    all_to_all x1, blocking collectives, per_device(): lax.all_to_all(panel_conv, 'ctx', split_axis=1, concat_axis=0, tiled=True)  13.1 us
    all_to_all x2, starting transfers between devices, gather_by_exchange(): lax.all_to_all(copies, axis, split_axis=0, concat_axis=concat_axis, tiled...  10.4 us
    all_to_all x1, starting transfers between devices, per_device(): lax.all_to_all(product.T, 'ctx', split_axis=0, concat_axis=1, tiled=True)  9.18 us
    all_to_all x1, waiting for transfers between devices, per_device(): lax.all_to_all(product.T, 'ctx', split_axis=0, concat_axis=1, tiled=True)  7.43 us
    unnamed x18, local copies, waits for them, and re-layouts  6.87 us
    ppermute x1, starting transfers between devices, shifted(): lax.ppermute(value, axis, [(source, source + steps) for source in range(i...  4.33 us
  transfers between devices with their start and end apart: 4, of which 3 were waited for; matrix products, arithmetic and copies ran while one was open for 6% of the time, Pallas kernels for 0%

profile of v1, /device:TPU:6, one launch (start us, length us, event | category | flops | bytes accessed | tf_op | source)
XLA Modules:
  0.0 165.3 jit_solution(11550427073858953379)
XLA Ops:
  0.6 0.8 slice.65
  1.6 4.3 %collective-permute-start = (bf16[2,3,128]{0,2,1:T(8,128)(2,1)S(1)}, bf16[2,3,128]{0,2,1:T(8,128)(2,1)S(1)}, u32[]{:S(2)}, u32[]{:S(2)}) collective-permute-start(bf16[2,3,128]{0,2,1:T(8,128)(2,1)S(1)} %copy.63), channel_id=1, source_target_pairs={{0,32},{32,64},{64,96},{96,128},{128,160},{160,192},{192,224},{224... | collective-permute-start | bytes 4616 | tf_op jit(solution)/shard_map/ppermute | solution.py:20
  6.1 0.8 constant_dynamic-slice_fusion
  7.0 0.7 slice_bitcast_fusion.3
  7.9 1.0 copy.64
  9.3 0.6 tile.10
  10.2 1.6 reshape.284
  12.3 0.6 fusion.62
  12.9 9.2 %all-to-all-start = ((bf16[16,8,128]{2,1,0:T(8,128)(2,1)}), bf16[16,8,128]{2,1,0:T(8,128)(2,1)S(1)}, u32[]{:S(2)}, u32[]{:S(2)}) async-start(bf16[16,8,128]{2,1,0:T(8,128)(2,1)} %fusion.62), calls=%async_computation | async-start | bytes 65536 | tf_op jit(solution)/shard_map/all_to_all | solution.py:143
  22.1 7.4 %all-to-all-done = bf16[16,8,128]{2,1,0:T(8,128)(2,1)S(1)} async-done(((bf16[16,8,128]{2,1,0:T(8,128)(2,1)}), bf16[16,8,128]{2,1,0:T(8,128)(2,1)S(1)}, u32[]{:S(2)}, u32[]{:S(2)}) %all-to-all-start) | async-done | bytes 32800 | tf_op jit(solution)/shard_map/all_to_all | solution.py:143
  29.9 0.6 multiply_reduce_fusion
  30.6 0.5 fusion.29
  31.4 13.1 %all_to_all.55 = f32[8,16,128]{2,0,1:T(8,128)S(1)} all-to-all(f32[8,16,128]{2,0,1:T(8,128)S(1)} %copy.68), channel_id=1, replica_groups=mesh['ctx'=16,'tp'=32] {'ctx'}, dimensions={1} | all-to-all | bytes 131072 | tf_op jit(solution)/shard_map/all_to_all | solution.py:151
  44.5 0.5 fusion.28
  45.3 40.7 %all_to_all.56 = bf16[32,128,128]{1,2,0:T(8,128)(2,1)S(1)} all-to-all(bf16[32,128,128]{1,2,0:T(8,128)(2,1)S(1)} %bitcast.133), channel_id=1, replica_groups=mesh['ctx'=16,'tp'=32] {'tp'}, dimensions={0} | all-to-all | bytes 2097152 | tf_op jit(solution)/shard_map/all_to_all | solution.py:158
  86.2 1.2 broadcast_in_dim_broadcast_in_dim.2
  87.4 4.0 %all-to-all-start.3 = ((bf16[32,128,1,128]{3,1,2,0:T(8,128)(2,1)}), bf16[32,128,1,128]{3,1,2,0:T(8,128)(2,1)S(1)}, u32[]{:S(2)}, u32[]{:S(2)}) async-start(bf16[32,128,1,128]{3,1,2,0:T(8,128)(2,1)} %broadcast_in_dim_broadcast_in_dim.2), calls=%async_computation.3 | async-start | bytes 2097152 | tf_op jit(solution)/shard_map/all_to_all | solution.py:26
  91.4 4.7 %copy.71 = bf16[4096,3,128]{0,2,1:T(8,128)(2,1)} copy(bf16[4096,3,128]{2,0,1:T(8,128)(2,1)} %param.17) | data formatting | bytes 6291456 | tf_op args[7]
  96.1 24.3 %all-to-all-done.3 = bf16[32,128,1,128]{3,1,2,0:T(8,128)(2,1)S(1)} async-done(((bf16[32,128,1,128]{3,1,2,0:T(8,128)(2,1)}), bf16[32,128,1,128]{3,1,2,0:T(8,128)(2,1)S(1)}, u32[]{:S(2)}, u32[]{:S(2)}) %all-to-all-start.3) | async-done | bytes 1048608 | tf_op jit(solution)/shard_map/all_to_all | solution.py:26
  120.4 0.7 copy.70
  121.1 0.6 fusion.25
  121.6 0.7 fusion.27
  122.4 0.6 copy-done.1
  123.0 1.0 fusion.23
  124.3 1.1 broadcast_in_dim.27
  125.4 6.4 %all-to-all-start.4 = ((bf16[16,128,256]{2,1,0:T(8,128)(2,1)}), bf16[16,128,256]{2,1,0:T(8,128)(2,1)S(1)}, u32[]{:S(2)}, u32[]{:S(2)}) async-start(bf16[16,128,256]{2,1,0:T(8,128)(2,1)} %broadcast_in_dim.27), calls=%async_computation.4 | async-start | bytes 2097152 | tf_op jit(solution)/shard_map/all_to_all | solution.py:26
  131.9 27.9 %all-to-all-done.4 = bf16[16,128,256]{2,1,0:T(8,128)(2,1)S(1)} async-done(((bf16[16,128,256]{2,1,0:T(8,128)(2,1)}), bf16[16,128,256]{2,1,0:T(8,128)(2,1)S(1)}, u32[]{:S(2)}, u32[]{:S(2)}) %all-to-all-start.4) | async-done | bytes 1048608 | tf_op jit(solution)/shard_map/all_to_all | solution.py:26
  159.9 4.7 %while.15 = (s32[]{:T(128)}, f32[1,128]{1,0:T(1,128)S(1)}, f32[1,128]{1,0:T(1,128)S(1)}, f32[1,128,128]{2,1,0:T(8,128)S(1)}, s32[2]{0:T(128)S(1)}, /*index=5*/bf...) while((s32[]{:T(128)}, f32[1,128]{1,0:T(1,128)S(1)}, ...), condition=%wide.region_6.7_spmd.clone, body=%wide.region_3.6_spmd.clone.sunk | while | flops 68732800 | bytes 2287785 | solution.py:206
  159.9 0.7 dynamic_slice.39
  161.6 0.4 fusion.97
  162.3 0.7 dynamic_slice.39
  164.6 0.7 fusion.72
  (63 shorter events, 5.1 us)
Async XLA Ops:
  0.6 43.9 %copy-start = (bf16[128,4096]{1,0:T(8,128)(2,1)S(1)}, bf16[128,4096]{1,0:T(8,128)(2,1)}, u32[]{:S(2)}) copy-start(bf16[128,4096]{1,0:T(8,128)(2,1)} %param.15) | copy-start | bytes 3145732
  1.6 10.2 %collective-permute-start = (bf16[2,3,128]{0,2,1:T(8,128)(2,1)S(1)}, bf16[2,3,128]{0,2,1:T(8,128)(2,1)S(1)}, u32[]{:S(2)}, u32[]{:S(2)}) collective-permute-start(bf16[2,3,128]{0,2,1:T(8,128)(2,1)S(1)} %copy.63), channel_id=1, source_target_pairs={{0,32},{32,64},{64,96},{96,128},{128,160},{160,192},{192,224},{224... | collective-permute-start | bytes 4616 | tf_op jit(solution)/shard_map/ppermute | solution.py:20
  12.9 16.6 %all-to-all-start = ((bf16[16,8,128]{2,1,0:T(8,128)(2,1)}), bf16[16,8,128]{2,1,0:T(8,128)(2,1)S(1)}, u32[]{:S(2)}, u32[]{:S(2)}) async-start(bf16[16,8,128]{2,1,0:T(8,128)(2,1)} %fusion.62), calls=%async_computation | async-start | bytes 65536 | tf_op jit(solution)/shard_map/all_to_all | solution.py:143
  45.3 40.8 %copy-start.3 = (bf16[128,128]{1,0:T(8,128)(2,1)S(1)}, bf16[128,128]{1,0:T(8,128)(2,1)}, u32[]{:S(2)}) copy-start(bf16[128,128]{1,0:T(8,128)(2,1)} %param.10) | copy-start | bytes 98308
  86.2 9.9 %copy-start.2 = (bf16[128,128]{1,0:T(8,128)(2,1)}, bf16[128,128]{1,0:T(8,128)(2,1)S(1)}, u32[]{:S(2)}) copy-start(bf16[128,128]{1,0:T(8,128)(2,1)S(1)} %fusion.36) | copy-start | bytes 98308
  87.4 33.0 %all-to-all-start.3 = ((bf16[32,128,1,128]{3,1,2,0:T(8,128)(2,1)}), bf16[32,128,1,128]{3,1,2,0:T(8,128)(2,1)S(1)}, u32[]{:S(2)}, u32[]{:S(2)}) async-start(bf16[32,128,1,128]{3,1,2,0:T(8,128)(2,1)} %broadcast_in_dim_broadcast_in_dim.2), calls=%async_computation.3 | async-start | bytes 2097152 | tf_op jit(solution)/shard_map/all_to_all | solution.py:26
  96.1 25.6 %copy-start.4 = (f32[4096]{0:T(1024)S(1)}, f32[4096]{0:T(1024)}, u32[]{:S(2)}) copy-start(f32[4096]{0:T(1024)} %param.16) | copy-start | bytes 49156
  121.1 1.9 %copy-start.1 = (bf16[4096,3,128]{0,2,1:T(8,128)(2,1)S(1)}, bf16[4096,3,128]{0,2,1:T(8,128)(2,1)}, u32[]{:S(2)}) copy-start(bf16[4096,3,128]{0,2,1:T(8,128)(2,1)} %copy.71) | copy-start | bytes 9437188
  125.4 34.5 %all-to-all-start.4 = ((bf16[16,128,256]{2,1,0:T(8,128)(2,1)}), bf16[16,128,256]{2,1,0:T(8,128)(2,1)S(1)}, u32[]{:S(2)}, u32[]{:S(2)}) async-start(bf16[16,128,256]{2,1,0:T(8,128)(2,1)} %broadcast_in_dim.27), calls=%async_computation.4 | async-start | bytes 2097152 | tf_op jit(solution)/shard_map/all_to_all | solution.py:26

commit v2 on v1

--- a/solution.py
+++ b/solution.py
@@ -140,16 +140,20 @@
     width_all = out_weight.shape[1]
     short_out = short_mix(feats, short_filter)
     product = (short_out[:, 1] * short_out[:, 2]).astype(jnp.bfloat16)
-    panel_rows = lax.all_to_all(product.T, "ctx", split_axis=0, concat_axis=1, tiled=True)
-    panel_count = chan_count // lax.axis_size("ctx")
-    panel_start = lax.axis_index("ctx") * panel_count
-    panel_res = lax.dynamic_slice_in_dim(residues, panel_start, panel_count, 0)
-    panel_rates = lax.dynamic_slice_in_dim(rates, panel_start, panel_count, 0)
-    panel_conv = modal_conv(
-        panel_rows.astype(jnp.float32), panel_res, panel_rates, jnp.zeros_like(panel_rates)
-    )
-    returned = lax.all_to_all(panel_conv, "ctx", split_axis=1, concat_axis=0, tiled=True)
-    conv_out = returned.T
+    signal = product.T.astype(jnp.float32)
+    lag_steps = jnp.arange(row_count, dtype=jnp.float32)
+    tail_powers = jnp.exp(-rates[:, :, None] * (row_count - lag_steps))
+    end_state = jnp.einsum("ct,cmt->cm", signal, tail_powers, precision=highest)
+    gathered_states = gather_by_exchange(end_state, "ctx", concat_axis=0)
+    shard_steps = jnp.arange(lax.axis_size("ctx"), dtype=jnp.float32)
+    gap_count = lax.axis_index("ctx").astype(jnp.float32) - 1.0 - shard_steps
+    decay = jnp.where(
+        (gap_count >= 0.0)[:, None, None],
+        jnp.exp(-rates[None] * row_count * jnp.maximum(gap_count, 0.0)[:, None, None]),
+        0.0,
+    )
+    start_state = jnp.sum(decay * gathered_states, axis=0)
+    conv_out = modal_conv(signal, residues, rates, start_state).T
     gated = (short_out[:, 0] * conv_out).astype(jnp.bfloat16)
     tp_count = lax.axis_size("tp")
     partials = lax.dot_general(

time: 168 us -> 227 us (1.35)
  local copies, waits for them, and re-layouts: 16.9 us -> 79 us
  blocking collectives: 53.8 us -> 40.7 us
  other arithmetic: 4.83 us -> 12.7 us
    reshape x1, local copies, waits for them, and re-layouts: 1.61 us -> 28.5 us  [toeplitz_lower(): window.reshape(chan_count, block_size, 2 * block_size - 2)]
    another operation x2, local copies, waits for them, and re-layouts: 0.69 us -> 24.3 us  [toeplitz_lower(): tiled = jnp.tile(flipped, (1, block_size))]
    all_to_all x1 -> x0, blocking collectives: 13.1 us -> none  [per_device(): lax.all_to_all(panel_conv, 'ctx', split_axis=1, concat_axis=0, tiled=True)]
    slice x1, local copies, waits for them, and re-layouts: 0.33 us -> 12.8 us  [toeplitz_lower(): window = tiled[:, offset:offset + block_size * (2 * block_size - 2)]]
    all_to_all x2 -> x3, starting transfers between devices: 10.4 us -> 20.9 us  [gather_by_exchange(): lax.all_to_all(copies, axis, split_axis=0, concat_axis=concat_axis, tiled...]
    all_to_all x1 -> x0, starting transfers between devices: 9.18 us -> none  [per_device(): lax.all_to_all(product.T, 'ctx', split_axis=0, concat_axis=1, tiled=True)]
    all_to_all x2 -> x3, waiting for transfers between devices: 52.2 us -> 60.6 us  [gather_by_exchange(): lax.all_to_all(copies, axis, split_axis=0, concat_axis=concat_axis, tiled...]
    all_to_all x1 -> x0, waiting for transfers between devices: 7.43 us -> none  [per_device(): lax.all_to_all(product.T, 'ctx', split_axis=0, concat_axis=1, tiled=True)]
  transfers between devices with their start and end apart: 4 -> 4, of which waited for: 3 -> 4; matrix products, arithmetic and copies ran while one was open for 6% -> 3% of each run, Pallas kernels for 0% -> 0%
where the time goes in v2:
time: 227 us; the launch traced here: 225 us
  local copies, waits for them, and re-layouts  79 us (35%)
  waiting for transfers between devices  61.7 us (27%)
  blocking collectives  40.7 us (18%)
  starting transfers between devices  25.2 us (11%)
  other arithmetic  12.7 us (6%)
  matrix products  2.9 us (1%)
    all_to_all x3, waiting for transfers between devices, gather_by_exchange(): lax.all_to_all(copies, axis, split_axis=0, concat_axis=concat_axis, tiled...  60.6 us
    all_to_all x1, blocking collectives, per_device(): lax.all_to_all(partials, 'tp', split_axis=0, concat_axis=0, tiled=True)  40.7 us
    reshape x1, local copies, waits for them, and re-layouts, toeplitz_lower(): window.reshape(chan_count, block_size, 2 * block_size - 2)  28.5 us
    another operation x2, local copies, waits for them, and re-layouts, toeplitz_lower(): tiled = jnp.tile(flipped, (1, block_size))  24.3 us
    all_to_all x3, starting transfers between devices, gather_by_exchange(): lax.all_to_all(copies, axis, split_axis=0, concat_axis=concat_axis, tiled...  20.9 us
    slice x1, local copies, waits for them, and re-layouts, toeplitz_lower(): window = tiled[:, offset:offset + block_size * (2 * block_size - 2)]  12.8 us
    unnamed x7, other arithmetic  7.25 us
    unnamed x16, local copies, waits for them, and re-layouts  5.9 us
  transfers between devices with their start and end apart: 4, of which 4 were waited for; matrix products, arithmetic and copies ran while one was open for 3% of the time, Pallas kernels for 0%

profile of v2, /device:TPU:6, one launch (start us, length us, event | category | flops | bytes accessed | tf_op | source)
XLA Modules:
  0.0 224.5 jit_solution(11898122627901697243)
XLA Ops:
  0.6 0.8 slice.65
  1.4 4.3 %collective-permute-start = (bf16[2,3,128]{2,0,1:T(2,128)(2,1)S(1)}, bf16[2,3,128]{2,0,1:T(2,128)(2,1)S(1)}, u32[]{:S(2)}, u32[]{:S(2)}) collective-permute-start(bf16[2,3,128]{2,0,1:T(2,128)(2,1)S(1)} %slice.65), channel_id=1, source_target_pairs={{0,32},{32,64},{64,96},{96,128},{128,160},{160,192},{192,224},{224... | collective-permute-start | bytes 4616 | tf_op jit(solution)/shard_map/ppermute | solution.py:20
  5.8 0.7 slice_bitcast_fusion.4
  6.5 0.7 broadcast_multiply_fusion
  7.3 1.1 collective-permute-done
  8.4 0.9 maximum_convert_fusion
  9.5 0.6 multiply_reduce_fusion.1
  10.2 0.7 broadcast_in_dim.34
  10.9 10.6 %all-to-all-start = ((f32[16,128,16]{1,2,0:T(8,128)}), f32[16,128,16]{1,2,0:T(8,128)S(1)}, u32[]{:S(2)}, u32[]{:S(2)}) async-start(f32[16,128,16]{1,2,0:T(8,128)} %broadcast_in_dim.34), calls=%async_computation | async-start | bytes 262144 | tf_op jit(solution)/shard_map/all_to_all | solution.py:26
  21.5 8.4 %all-to-all-done = f32[16,128,16]{1,2,0:T(8,128)S(1)} async-done(((f32[16,128,16]{1,2,0:T(8,128)}), f32[16,128,16]{1,2,0:T(8,128)S(1)}, u32[]{:S(2)}, u32[]{:S(2)}) %all-to-all-start) | async-done | bytes 131104 | tf_op jit(solution)/shard_map/all_to_all | solution.py:26
  30.0 0.7 add_multiply_fusion
  31.0 1.0 multiply_reduce_fusion
  32.4 7.0 %tile.4 = f32[128,128,255]{2,1,0:T(8,128)} broadcast(f32[128,255]{1,0:T(8,128)S(1)} %slice.154), dimensions={0,2} | broadcast | bytes 16842240 | tf_op jit(solution)/shard_map/tile | solution.py:35
  39.4 17.3 %tile.10 = f32[128,32640]{1,0:T(8,128)} reshape(f32[128,128,255]{2,1,0:T(8,128)} %tile.4) | data formatting | bytes 33423360 | tf_op jit(solution)/shard_map/tile | solution.py:35
  56.7 12.8 %slice.89 = f32[128,32512]{1,0:T(8,128)} slice(f32[128,32640]{1,0:T(8,128)} %tile.10), slice={[0:128], [127:32639]} | slice | bytes 33292288 | tf_op jit(solution)/shard_map/slice | solution.py:37
  69.5 28.5 %reshape.284 = f32[128,128,254]{2,1,0:T(8,128)} reshape(f32[128,32512]{1,0:T(8,128)} %slice.89) | data formatting | bytes 33292288 | tf_op jit(solution)/shard_map/reshape | solution.py:38
  98.0 5.6 %fusion.24 = f32[128,128]{1,0:T(8,128)S(1)} fusion(f32[128,128,254]{2,1,0:T(8,128)} %reshape.284, f32[128,128]{1,0:T(8,128)S(1)} %copy.69), kind=kLoop, calls=%fused_computation.33 | loop fusion | flops 4177920 | bytes 8519680
  104.6 40.7 %all_to_all.28 = bf16[32,128,128]{1,2,0:T(8,128)(2,1)S(1)} all-to-all(bf16[32,128,128]{1,2,0:T(8,128)(2,1)S(1)} %bitcast.123), channel_id=1, replica_groups=mesh['ctx'=16,'tp'=32] {'tp'}, dimensions={0} | all-to-all | bytes 2097152 | tf_op jit(solution)/shard_map/all_to_all | solution.py:162
  145.4 1.2 broadcast_in_dim_broadcast_in_dim.2
  146.6 4.0 %all-to-all-start.2 = ((bf16[32,128,1,128]{3,1,2,0:T(8,128)(2,1)}), bf16[32,128,1,128]{3,1,2,0:T(8,128)(2,1)S(1)}, u32[]{:S(2)}, u32[]{:S(2)}) async-start(bf16[32,128,1,128]{3,1,2,0:T(8,128)(2,1)} %broadcast_in_dim_broadcast_in_dim.2), calls=%async_computation.2 | async-start | bytes 2097152 | tf_op jit(solution)/shard_map/all_to_all | solution.py:26
  150.7 4.7 %copy.47 = bf16[4096,3,128]{0,2,1:T(8,128)(2,1)} copy(bf16[4096,3,128]{2,0,1:T(8,128)(2,1)} %param.17) | data formatting | bytes 6291456 | tf_op args[7]
  155.4 24.3 %all-to-all-done.2 = bf16[32,128,1,128]{3,1,2,0:T(8,128)(2,1)S(1)} async-done(((bf16[32,128,1,128]{3,1,2,0:T(8,128)(2,1)}), bf16[32,128,1,128]{3,1,2,0:T(8,128)(2,1)S(1)}, u32[]{:S(2)}, u32[]{:S(2)}) %all-to-all-start.2) | async-done | bytes 1048608 | tf_op jit(solution)/shard_map/all_to_all | solution.py:26
  179.7 0.7 copy.46
  180.9 0.7 fusion.29
  182.2 1.0 fusion.25
  183.6 1.1 broadcast_in_dim.38
  184.7 6.2 %all-to-all-start.3 = ((bf16[16,128,256]{2,1,0:T(8,128)(2,1)}), bf16[16,128,256]{2,1,0:T(8,128)(2,1)S(1)}, u32[]{:S(2)}, u32[]{:S(2)}) async-start(bf16[16,128,256]{2,1,0:T(8,128)(2,1)} %broadcast_in_dim.38), calls=%async_computation.3 | async-start | bytes 2097152 | tf_op jit(solution)/shard_map/all_to_all | solution.py:26
  191.0 27.9 %all-to-all-done.3 = bf16[16,128,256]{2,1,0:T(8,128)(2,1)S(1)} async-done(((bf16[16,128,256]{2,1,0:T(8,128)(2,1)}), bf16[16,128,256]{2,1,0:T(8,128)(2,1)S(1)}, u32[]{:S(2)}, u32[]{:S(2)}) %all-to-all-start.3) | async-done | bytes 1048608 | tf_op jit(solution)/shard_map/all_to_all | solution.py:26
  219.0 4.8 %while.15 = (s32[]{:T(128)}, f32[1,128]{1,0:T(1,128)S(1)}, f32[1,128]{1,0:T(1,128)S(1)}, f32[1,128,128]{2,1,0:T(8,128)S(1)}, s32[2]{0:T(128)S(1)}, /*index=5*/bf...) while((s32[]{:T(128)}, f32[1,128]{1,0:T(1,128)S(1)}, ...), condition=%wide.region_7.8_spmd.clone, body=%wide.region_4.7_spmd.clone.sunk | while | flops 68732800 | bytes 2287785 | solution.py:210
  219.0 0.7 dynamic_slice.29
  221.4 0.7 dynamic_slice.29
  223.8 0.7 fusion.57
  (61 shorter events, 5.8 us)
Async XLA Ops:
  0.6 103.2 %copy-start = (bf16[128,4096]{1,0:T(8,128)(2,1)S(1)}, bf16[128,4096]{1,0:T(8,128)(2,1)}, u32[]{:S(2)}) copy-start(bf16[128,4096]{1,0:T(8,128)(2,1)} %param.15) | copy-start | bytes 3145732
  1.4 7.0 %collective-permute-start = (bf16[2,3,128]{2,0,1:T(2,128)(2,1)S(1)}, bf16[2,3,128]{2,0,1:T(2,128)(2,1)S(1)}, u32[]{:S(2)}, u32[]{:S(2)}) collective-permute-start(bf16[2,3,128]{2,0,1:T(2,128)(2,1)S(1)} %slice.65), channel_id=1, source_target_pairs={{0,32},{32,64},{64,96},{96,128},{128,160},{160,192},{192,224},{224... | collective-permute-start | bytes 4616 | tf_op jit(solution)/shard_map/ppermute | solution.py:20
  10.9 19.1 %all-to-all-start = ((f32[16,128,16]{1,2,0:T(8,128)}), f32[16,128,16]{1,2,0:T(8,128)S(1)}, u32[]{:S(2)}, u32[]{:S(2)}) async-start(f32[16,128,16]{1,2,0:T(8,128)} %broadcast_in_dim.34), calls=%async_computation | async-start | bytes 262144 | tf_op jit(solution)/shard_map/all_to_all | solution.py:26
  104.3 41.1 %copy-start.3 = (bf16[128,128]{1,0:T(8,128)(2,1)S(1)}, bf16[128,128]{1,0:T(8,128)(2,1)}, u32[]{:S(2)}) copy-start(bf16[128,128]{1,0:T(8,128)(2,1)} %param.10) | copy-start | bytes 98308
  145.4 9.9 %copy-start.2 = (bf16[128,128]{1,0:T(8,128)(2,1)}, bf16[128,128]{1,0:T(8,128)(2,1)S(1)}, u32[]{:S(2)}) copy-start(bf16[128,128]{1,0:T(8,128)(2,1)S(1)} %fusion.36) | copy-start | bytes 98308
  146.6 33.0 %all-to-all-start.2 = ((bf16[32,128,1,128]{3,1,2,0:T(8,128)(2,1)}), bf16[32,128,1,128]{3,1,2,0:T(8,128)(2,1)S(1)}, u32[]{:S(2)}, u32[]{:S(2)}) async-start(bf16[32,128,1,128]{3,1,2,0:T(8,128)(2,1)} %broadcast_in_dim_broadcast_in_dim.2), calls=%async_computation.2 | async-start | bytes 2097152 | tf_op jit(solution)/shard_map/all_to_all | solution.py:26
  155.3 25.6 %copy-start.4 = (f32[4096]{0:T(1024)S(1)}, f32[4096]{0:T(1024)}, u32[]{:S(2)}) copy-start(f32[4096]{0:T(1024)} %param.16) | copy-start | bytes 49156
  180.3 1.9 copy-start.1
  184.7 34.3 %all-to-all-start.3 = ((bf16[16,128,256]{2,1,0:T(8,128)(2,1)}), bf16[16,128,256]{2,1,0:T(8,128)(2,1)S(1)}, u32[]{:S(2)}, u32[]{:S(2)}) async-start(bf16[16,128,256]{2,1,0:T(8,128)(2,1)} %broadcast_in_dim.38), calls=%async_computation.3 | async-start | bytes 2097152 | tf_op jit(solution)/shard_map/all_to_all | solution.py:26

commit v3 on v2

--- a/solution.py
+++ b/solution.py
@@ -38,9 +38,9 @@
     return window.reshape(chan_count, block_size, 2 * block_size - 2)[:, :, :block_size]
 
 
-def modal_conv(signal, residues, rates, start_state):
+def modal_conv(signal, residues, rates, start_state, block_limit=128):
     chan_count, length = signal.shape
-    block_size = math.gcd(length, 128)
+    block_size = math.gcd(length, block_limit)
     block_count = length // block_size
     weight = residues * jnp.sqrt(1.0 - jnp.exp(-2.0 * rates))
     lag_steps = jnp.arange(block_size, dtype=jnp.float32)
@@ -153,7 +153,7 @@
         0.0,
     )
     start_state = jnp.sum(decay * gathered_states, axis=0)
-    conv_out = modal_conv(signal, residues, rates, start_state).T
+    conv_out = modal_conv(signal, residues, rates, start_state, block_limit=16).T
     gated = (short_out[:, 0] * conv_out).astype(jnp.bfloat16)
     tp_count = lax.axis_size("tp")
     partials = lax.dot_general(

time: 227 us -> 159 us (0.70)
  local copies, waits for them, and re-layouts: 79 us -> 15.9 us
  other arithmetic: 12.7 us -> 7.36 us
  matrix products: 2.9 us -> 7 us
    reshape x1, local copies, waits for them, and re-layouts: 28.5 us -> 0.02 us  [toeplitz_lower(): window.reshape(chan_count, block_size, 2 * block_size - 2)]
    another operation x2, local copies, waits for them, and re-layouts: 24.3 us -> 0.07 us  [toeplitz_lower(): tiled = jnp.tile(flipped, (1, block_size))]
    slice x1, local copies, waits for them, and re-layouts: 12.8 us -> 0.02 us  [toeplitz_lower(): window = tiled[:, offset:offset + block_size * (2 * block_size - 2)]]
    unnamed x7 -> x6, other arithmetic: 7.25 us -> 0.96 us
    dot_general x0 -> x3, matrix products: none -> 4.09 us  [the longest x1 2.07 us: modal_conv(): jnp.einsum('cnm,cmi->cni', states * weight[:, None, :], powers, precision...]
    unnamed x16 -> x19, local copies, waits for them, and re-layouts: 5.9 us -> 6.84 us
  transfers between devices with their start and end apart: 4 -> 4, of which waited for: 4 -> 3; matrix products, arithmetic and copies ran while one was open for 3% -> 6% of each run, Pallas kernels for 0% -> 0%
where the time goes in v3:
time: 159 us; the launch traced here: 157 us
  waiting for transfers between devices  59.8 us (38%)
  blocking collectives  40.7 us (26%)
  starting transfers between devices  23.7 us (15%)
  local copies, waits for them, and re-layouts  15.9 us (10%)
  other arithmetic  7.36 us (5%)
  matrix products  7 us (4%)
    all_to_all x3, waiting for transfers between devices, gather_by_exchange(): lax.all_to_all(copies, axis, split_axis=0, concat_axis=concat_axis, tiled...  59.7 us
    all_to_all x1, blocking collectives, per_device(): lax.all_to_all(partials, 'tp', split_axis=0, concat_axis=0, tiled=True)  40.7 us
    all_to_all x3, starting transfers between devices, gather_by_exchange(): lax.all_to_all(copies, axis, split_axis=0, concat_axis=concat_axis, tiled...  19.4 us
    unnamed x19, local copies, waits for them, and re-layouts  6.84 us
    ppermute x1, starting transfers between devices, shifted(): lax.ppermute(value, axis, [(source, source + steps) for source in range(i...  4.31 us
  transfers between devices with their start and end apart: 4, of which 3 were waited for; matrix products, arithmetic and copies ran while one was open for 6% of the time, Pallas kernels for 0%

profile of v3, /device:TPU:6, one launch (start us, length us, event | category | flops | bytes accessed | tf_op | source)
XLA Modules:
  0.0 156.9 jit_solution(14472627002190005286)
XLA Ops:
  0.7 0.8 slice.65
  1.5 4.3 %collective-permute-start = (bf16[2,3,128]{2,0,1:T(2,128)(2,1)S(1)}, bf16[2,3,128]{2,0,1:T(2,128)(2,1)S(1)}, u32[]{:S(2)}, u32[]{:S(2)}) collective-permute-start(bf16[2,3,128]{2,0,1:T(2,128)(2,1)S(1)} %slice.65), channel_id=1, source_target_pairs={{0,32},{32,64},{64,96},{96,128},{128,160},{160,192},{192,224},{224... | collective-permute-start | bytes 4616 | tf_op jit(solution)/shard_map/ppermute | solution.py:20
  6.0 0.7 slice_bitcast_fusion.3
  6.7 0.7 broadcast_multiply_fusion
  7.6 0.6 multiply_reduce_fusion.1
  9.2 0.7 copy.98
  10.0 0.6 copy-done.2
  10.9 1.1 convolution_bitcast_fusion.1
  12.8 0.6 multiply_reduce_fusion
  13.5 0.7 broadcast_in_dim.40
  14.2 9.2 %all-to-all-start = ((f32[16,128,16]{1,2,0:T(8,128)}), f32[16,128,16]{1,2,0:T(8,128)}, u32[]{:S(2)}, u32[]{:S(2)}) async-start(f32[16,128,16]{1,2,0:T(8,128)} %broadcast_in_dim.40), calls=%async_computation | async-start | bytes 262144 | tf_op jit(solution)/shard_map/all_to_all | solution.py:26
  23.4 0.9 fusion.76
  24.3 7.6 %all-to-all-done = f32[16,128,16]{1,2,0:T(8,128)} async-done(((f32[16,128,16]{1,2,0:T(8,128)}), f32[16,128,16]{1,2,0:T(8,128)}, u32[]{:S(2)}, u32[]{:S(2)}) %all-to-all-start) | async-done | bytes 131104 | tf_op jit(solution)/shard_map/all_to_all | solution.py:26
  31.9 1.0 multiply_reduce_fusion.3
  33.0 2.1 %convolution_add_fusion = f32[128,8,16]{2,1,0:T(8,128)S(1)} fusion(f32[128,8,16]{2,1,0:T(8,128)S(1)} %fusion.76, f32[128,16,8]{1,2,0:T(8,128)S(1)} %copy.118, f32[128,16]{1,0:T(8,128)S(1)} %copy.93, f32[128,16]{1,0:T(8,128)S(1)} %copy.92, f32[128,16]{1,0:T(8,128)S(1)} %copy.100, f32[128,16]{1,0:T(8,128)} %copy.98), kind=kOutput, calls=%fused_computation.41 | convolution fusion | flops 3260416 | bytes 229376 | tf_op jit(solution)/shard_map/cnm,cmi->cni/dot_general | solution.py:66
  35.3 0.9 fusion.47
  36.9 40.7 %all_to_all.28 = bf16[32,128,128]{1,2,0:T(8,128)(2,1)S(1)} all-to-all(bf16[32,128,128]{1,2,0:T(8,128)(2,1)S(1)} %bitcast.133), channel_id=1, replica_groups=mesh['ctx'=16,'tp'=32] {'tp'}, dimensions={0} | all-to-all | bytes 2097152 | tf_op jit(solution)/shard_map/all_to_all | solution.py:162
  77.7 1.2 broadcast_in_dim_broadcast_in_dim.2
  79.0 4.0 %all-to-all-start.2 = ((bf16[32,128,1,128]{3,1,2,0:T(8,128)(2,1)}), bf16[32,128,1,128]{3,1,2,0:T(8,128)(2,1)S(1)}, u32[]{:S(2)}, u32[]{:S(2)}) async-start(bf16[32,128,1,128]{3,1,2,0:T(8,128)(2,1)} %broadcast_in_dim_broadcast_in_dim.2), calls=%async_computation.2 | async-start | bytes 2097152 | tf_op jit(solution)/shard_map/all_to_all | solution.py:26
  83.0 4.7 %copy.105 = bf16[4096,3,128]{0,2,1:T(8,128)(2,1)} copy(bf16[4096,3,128]{2,0,1:T(8,128)(2,1)} %param.17) | data formatting | bytes 6291456 | tf_op args[7]
  87.7 24.3 %all-to-all-done.2 = bf16[32,128,1,128]{3,1,2,0:T(8,128)(2,1)S(1)} async-done(((bf16[32,128,1,128]{3,1,2,0:T(8,128)(2,1)}), bf16[32,128,1,128]{3,1,2,0:T(8,128)(2,1)S(1)}, u32[]{:S(2)}, u32[]{:S(2)}) %all-to-all-start.2) | async-done | bytes 1048608 | tf_op jit(solution)/shard_map/all_to_all | solution.py:26
  112.0 0.7 copy.104
  113.2 0.7 fusion.27
  113.9 0.6 copy-done.1
  114.5 1.0 fusion.23
  115.9 1.1 broadcast_in_dim.44
  117.0 6.2 %all-to-all-start.3 = ((bf16[16,128,256]{2,1,0:T(8,128)(2,1)}), bf16[16,128,256]{2,1,0:T(8,128)(2,1)S(1)}, u32[]{:S(2)}, u32[]{:S(2)}) async-start(bf16[16,128,256]{2,1,0:T(8,128)(2,1)} %broadcast_in_dim.44), calls=%async_computation.3 | async-start | bytes 2097152 | tf_op jit(solution)/shard_map/all_to_all | solution.py:26
  123.4 27.9 %all-to-all-done.3 = bf16[16,128,256]{2,1,0:T(8,128)(2,1)S(1)} async-done(((bf16[16,128,256]{2,1,0:T(8,128)(2,1)}), bf16[16,128,256]{2,1,0:T(8,128)(2,1)S(1)}, u32[]{:S(2)}, u32[]{:S(2)}) %all-to-all-start.3) | async-done | bytes 1048608 | tf_op jit(solution)/shard_map/all_to_all | solution.py:26
  151.3 4.8 %while.15 = (s32[]{:T(128)}, f32[1,128]{1,0:T(1,128)S(1)}, f32[1,128]{1,0:T(1,128)S(1)}, f32[1,128,128]{2,1,0:T(8,128)S(1)}, s32[2]{0:T(128)S(1)}, /*index=5*/bf...) while((s32[]{:T(128)}, f32[1,128]{1,0:T(1,128)S(1)}, ...), condition=%wide.region_7.8_spmd.clone, body=%wide.region_4.7_spmd.clone.sunk | while | flops 68732800 | bytes 2287785 | solution.py:210
  151.3 0.7 dynamic_slice.29
  153.7 0.7 dynamic_slice.29
  156.1 0.7 fusion.66
  (77 shorter events, 6.7 us)
Async XLA Ops:
  0.6 35.5 %copy-start = (bf16[128,4096]{1,0:T(8,128)(2,1)S(1)}, bf16[128,4096]{1,0:T(8,128)(2,1)}, u32[]{:S(2)}) copy-start(bf16[128,4096]{1,0:T(8,128)(2,1)} %param.15) | copy-start | bytes 3145732
  0.6 9.2 %copy-start.4 = (bf16[128,3,128]{2,0,1:T(8,128)(2,1)S(1)}, bf16[128,3,128]{2,0,1:T(8,128)(2,1)}, u32[]{:S(2)}) copy-start(bf16[128,3,128]{2,0,1:T(8,128)(2,1)} %param.11) | copy-start | bytes 294916
  1.5 8.4 %collective-permute-start = (bf16[2,3,128]{2,0,1:T(2,128)(2,1)S(1)}, bf16[2,3,128]{2,0,1:T(2,128)(2,1)S(1)}, u32[]{:S(2)}, u32[]{:S(2)}) collective-permute-start(bf16[2,3,128]{2,0,1:T(2,128)(2,1)S(1)} %slice.65), channel_id=1, source_target_pairs={{0,32},{32,64},{64,96},{96,128},{128,160},{160,192},{192,224},{224... | collective-permute-start | bytes 4616 | tf_op jit(solution)/shard_map/ppermute | solution.py:20
  10.0 0.7 copy-start.2
  14.2 17.7 %all-to-all-start = ((f32[16,128,16]{1,2,0:T(8,128)}), f32[16,128,16]{1,2,0:T(8,128)}, u32[]{:S(2)}, u32[]{:S(2)}) async-start(f32[16,128,16]{1,2,0:T(8,128)} %broadcast_in_dim.40), calls=%async_computation | async-start | bytes 262144 | tf_op jit(solution)/shard_map/all_to_all | solution.py:26
  36.9 40.8 %copy-start.5 = (bf16[128,128]{1,0:T(8,128)(2,1)S(1)}, bf16[128,128]{1,0:T(8,128)(2,1)}, u32[]{:S(2)}) copy-start(bf16[128,128]{1,0:T(8,128)(2,1)} %param.10) | copy-start | bytes 98308
  77.7 9.9 %copy-start.3 = (bf16[128,128]{1,0:T(8,128)(2,1)}, bf16[128,128]{1,0:T(8,128)(2,1)S(1)}, u32[]{:S(2)}) copy-start(bf16[128,128]{1,0:T(8,128)(2,1)S(1)} %fusion.48) | copy-start | bytes 98308
  79.0 33.0 %all-to-all-start.2 = ((bf16[32,128,1,128]{3,1,2,0:T(8,128)(2,1)}), bf16[32,128,1,128]{3,1,2,0:T(8,128)(2,1)S(1)}, u32[]{:S(2)}, u32[]{:S(2)}) async-start(bf16[32,128,1,128]{3,1,2,0:T(8,128)(2,1)} %broadcast_in_dim_broadcast_in_dim.2), calls=%async_computation.2 | async-start | bytes 2097152 | tf_op jit(solution)/shard_map/all_to_all | solution.py:26
  87.7 25.6 %copy-start.6 = (f32[4096]{0:T(1024)S(1)}, f32[4096]{0:T(1024)}, u32[]{:S(2)}) copy-start(f32[4096]{0:T(1024)} %param.16) | copy-start | bytes 49156
  112.6 1.9 %copy-start.1 = (bf16[4096,3,128]{0,2,1:T(8,128)(2,1)S(1)}, bf16[4096,3,128]{0,2,1:T(8,128)(2,1)}, u32[]{:S(2)}) copy-start(bf16[4096,3,128]{0,2,1:T(8,128)(2,1)} %copy.105) | copy-start | bytes 9437188
  117.0 34.2 %all-to-all-start.3 = ((bf16[16,128,256]{2,1,0:T(8,128)(2,1)}), bf16[16,128,256]{2,1,0:T(8,128)(2,1)S(1)}, u32[]{:S(2)}, u32[]{:S(2)}) async-start(bf16[16,128,256]{2,1,0:T(8,128)(2,1)} %broadcast_in_dim.44), calls=%async_computation.3 | async-start | bytes 2097152 | tf_op jit(solution)/shard_map/all_to_all | solution.py:26

commit v4 on v3

--- a/solution.py
+++ b/solution.py
@@ -12,12 +12,6 @@
 rope_base = 10000.0
 mask_fill = -1e30
 highest = lax.Precision.HIGHEST
-
-
-def shifted(value, axis, steps):
-    count = lax.axis_size(axis)
-    initial, last = (max(0, -steps), min(count, count - steps))
-    return lax.ppermute(value, axis, [(source, source + steps) for source in range(initial, last)])
 
 
 def gather_by_exchange(block, axis, concat_axis=1):
@@ -67,10 +61,8 @@
     return (inner_part + cross_part).reshape(chan_count, length)
 
 
-def short_mix(feats, short_filter):
-    row_count = feats.shape[0]
-    prior_feats = shifted(feats[-2:], "ctx", 1)
-    joined = jnp.concatenate([prior_feats, feats], axis=0).astype(jnp.float32)
+def short_conv(joined, short_filter):
+    row_count = joined.shape[0] - 2
     return (
         short_filter[0] * joined[2:]
         + short_filter[1] * joined[1 : row_count + 1]
@@ -92,61 +84,46 @@
     )
 
 
-def attend_tile(running, query_rows, query_pos, key_block, value_block, key_start):
-    run_peak, denom, accumulated = running
-    block_size = key_block.shape[0]
-    score_scale = 1.0 / math.sqrt(key_block.shape[2])
-    key_pos = key_start + jnp.arange(block_size, dtype=jnp.int32)
-    scores = (
-        jnp.einsum("shd,khd->hsk", query_rows, key_block, preferred_element_type=jnp.float32)
-        * score_scale
-    )
-    allowed = (query_pos[:, None] >= key_pos[None, :])[None]
-    masked = jnp.where(allowed, scores, mask_fill)
-    new_peak = jnp.maximum(run_peak, jnp.max(masked, axis=2))
-    weights = jnp.where(allowed, jnp.exp(masked - new_peak[:, :, None]), 0.0)
-    factor = jnp.exp(run_peak - new_peak)
-    denom = denom * factor + jnp.sum(weights, axis=2)
-    accumulated = accumulated * factor[:, :, None] + jnp.einsum(
-        "hsk,khd->hsd",
-        weights.astype(jnp.bfloat16),
-        value_block,
-        preferred_element_type=jnp.float32,
-    )
-    return (new_peak, denom, accumulated)
-
-
-def empty_state(head_count, rows):
-    return (
-        jnp.full((head_count, rows), mask_fill, jnp.float32),
-        jnp.zeros((head_count, rows), jnp.float32),
-        jnp.zeros((head_count, rows, HEAD_DIM), jnp.float32),
-    )
-
-
-def finish_rows(state):
-    run_peak, denom, accumulated = state
-    heads_out = accumulated / denom[:, :, None]
-    rows = heads_out.shape[1]
-    return (
-        heads_out.transpose(1, 0, 2)
-        .reshape(rows, heads_out.shape[0] * heads_out.shape[2])
-        .astype(jnp.bfloat16)
-    )
-
-
 def per_device(resid_in, feats, short_filter, residues, rates, out_weight, norm_gain, attn_weight):
     row_count, chan_count = resid_in.shape
     width_all = out_weight.shape[1]
-    short_out = short_mix(feats, short_filter)
+    feats_wide = feats.astype(jnp.float32)
+    ctx_count = lax.axis_size("ctx")
+    ctx_index = lax.axis_index("ctx")
+    lag_steps = jnp.arange(row_count, dtype=jnp.float32)
+    tail_powers = jnp.exp(-rates[:, :, None] * (row_count - lag_steps))
+    no_prior = jnp.zeros((2,) + feats_wide.shape[1:], jnp.float32)
+    blind = short_conv(jnp.concatenate([no_prior, feats_wide], axis=0), short_filter)
+    blind_product = (blind[:, 1] * blind[:, 2]).astype(jnp.bfloat16).T.astype(jnp.float32)
+    late_state = jnp.einsum(
+        "ct,cmt->cm", blind_product[:, 2:], tail_powers[:, :, 2:], precision=highest
+    )
+    mode_count = late_state.shape[1]
+    head_rows = feats_wide[:2, 1:, :].reshape(4, chan_count).T
+    tail_rows = feats_wide[-2:].reshape(6, chan_count).T
+    payload = jnp.concatenate([late_state, head_rows, tail_rows], axis=1)
+    received = gather_by_exchange(payload, "ctx", concat_axis=0)
+    late_all = received[:, :, :mode_count]
+    head_all = received[:, :, mode_count : mode_count + 4].reshape(ctx_count, chan_count, 2, 2)
+    head_all = head_all.transpose(0, 2, 3, 1)
+    tail_all = received[:, :, mode_count + 4 :].reshape(ctx_count, chan_count, 2, 3)
+    tail_all = tail_all.transpose(0, 2, 3, 1)
+    prev_tail = jnp.concatenate([jnp.zeros_like(tail_all[:1]), tail_all[:-1]], axis=0)
+    edge_joined = jnp.concatenate([prev_tail[:, :, 1:], head_all], axis=1)
+    taps = short_filter[:, 1:, :]
+    edge_short = taps[0] * edge_joined[:, 2:] + taps[1] * edge_joined[:, 1:3] + taps[2] * edge_joined[:, :2]
+    edge_product = (edge_short[:, :, 0] * edge_short[:, :, 1]).astype(jnp.bfloat16).astype(jnp.float32)
+    gathered_states = (
+        late_all
+        + edge_product[:, 0, :, None] * tail_powers[None, :, :, 0]
+        + edge_product[:, 1, :, None] * tail_powers[None, :, :, 1]
+    )
+    own_prior = lax.dynamic_index_in_dim(prev_tail, ctx_index, 0, keepdims=False)
+    short_out = short_conv(jnp.concatenate([own_prior, feats_wide], axis=0), short_filter)
     product = (short_out[:, 1] * short_out[:, 2]).astype(jnp.bfloat16)
     signal = product.T.astype(jnp.float32)
-    lag_steps = jnp.arange(row_count, dtype=jnp.float32)
-    tail_powers = jnp.exp(-rates[:, :, None] * (row_count - lag_steps))
-    end_state = jnp.einsum("ct,cmt->cm", signal, tail_powers, precision=highest)
-    gathered_states = gather_by_exchange(end_state, "ctx", concat_axis=0)
-    shard_steps = jnp.arange(lax.axis_size("ctx"), dtype=jnp.float32)
-    gap_count = lax.axis_index("ctx").astype(jnp.float32) - 1.0 - shard_steps
+    shard_steps = jnp.arange(ctx_count, dtype=jnp.float32)
+    gap_count = ctx_index.astype(jnp.float32) - 1.0 - shard_steps
     decay = jnp.where(
         (gap_count >= 0.0)[:, None, None],
         jnp.exp(-rates[None] * row_count * jnp.maximum(gap_count, 0.0)[:, None, None]),
@@ -172,7 +149,6 @@
         normed, attn_weight.reshape(width_all, 3 * chan_count), preferred_element_type=jnp.float32
     ).reshape(row_count, 3, chan_count)
     head_count = chan_count // HEAD_DIM
-    ctx_index = lax.axis_index("ctx")
     first_pos = ctx_index * row_count
     positions = first_pos + jnp.arange(row_count, dtype=jnp.int32)
     queries = rotary_turn(
@@ -182,33 +158,26 @@
         projected[:, 1].reshape(row_count, head_count, HEAD_DIM), positions
     ).astype(jnp.bfloat16)
     values = projected[:, 2].astype(jnp.bfloat16)
-    key_pieces = (keys_all.reshape(row_count, chan_count), values)
-    initial = empty_state(head_count, row_count)
-    joined_kv = jnp.concatenate(key_pieces, axis=1)
+    joined_kv = jnp.concatenate([keys_all.reshape(row_count, chan_count), values], axis=1)
     gathered_kv = gather_by_exchange(joined_kv, "ctx", concat_axis=0)
-    gathered_kv = gathered_kv.reshape(lax.axis_size("ctx") * row_count, 2 * chan_count)
-    key_rows = gathered_kv[:, :chan_count]
-    value_rows = gathered_kv[:, chan_count:]
-    key_total = key_rows.shape[0]
-    tiles_block_size = math.gcd(key_total, 1024)
-    block_count = key_total // tiles_block_size
-    key_blocks = key_rows.reshape(block_count, tiles_block_size, head_count, HEAD_DIM)
-    value_blocks = value_rows.reshape(block_count, tiles_block_size, head_count, HEAD_DIM)
-    key_blocks, value_blocks, block_ids, block_size = (
-        key_blocks,
-        value_blocks,
-        jnp.arange(block_count, dtype=jnp.int32),
-        tiles_block_size,
+    gathered_kv = gathered_kv.reshape(ctx_count * row_count, 2 * chan_count)
+    key_total = gathered_kv.shape[0]
+    key_rows = gathered_kv[:, :chan_count].reshape(key_total, head_count, HEAD_DIM)
+    value_rows = gathered_kv[:, chan_count:].reshape(key_total, head_count, HEAD_DIM)
+    key_pos = jnp.arange(key_total, dtype=jnp.int32)
+    scores = jnp.einsum(
+        "shd,khd->hsk", queries, key_rows, preferred_element_type=jnp.float32
+    ) * (1.0 / math.sqrt(HEAD_DIM))
+    allowed = (positions[:, None] >= key_pos[None, :])[None]
+    masked = jnp.where(allowed, scores, mask_fill)
+    run_peak = jnp.max(masked, axis=2, keepdims=True)
+    probs = jnp.where(allowed, jnp.exp(masked - run_peak), 0.0)
+    denom = jnp.sum(probs, axis=2, keepdims=True)
+    summed = jnp.einsum(
+        "hsk,khd->hsd", probs.astype(jnp.bfloat16), value_rows, preferred_element_type=jnp.float32
     )
-
-    def one_tile(carried, slot_item):
-        key_block, value_block, block_index = slot_item
-        key_start = block_index * block_size
-        updated = attend_tile(carried, queries, positions, key_block, value_block, key_start)
-        return (updated, None)
-
-    result, _ = lax.scan(one_tile, initial, (key_blocks, value_blocks, block_ids))
-    context = finish_rows(result)
+    heads_out = summed / denom
+    context = heads_out.transpose(1, 0, 2).reshape(row_count, chan_count).astype(jnp.bfloat16)
     return (hyena_out, context)
 
 

time: 159 us -> 158 us (level)
  waiting for transfers between devices: 59.8 us -> 54.5 us
  other arithmetic: 7.36 us -> 11.9 us
  local copies, waits for them, and re-layouts: 15.9 us -> 19.2 us
  starting transfers between devices: 23.7 us -> 21.2 us
    all_to_all x3, waiting for transfers between devices: 59.7 us -> 54.5 us  [gather_by_exchange(): lax.all_to_all(copies, axis, split_axis=0, concat_axis=concat_axis, tiled...]
    ppermute x1 -> x0, starting transfers between devices: 4.31 us -> none  [shifted(): lax.ppermute(value, axis, [(source, source + steps) for source in range(i...]
    slice x2 -> x7, local copies, waits for them, and re-layouts: 0.88 us -> 3.17 us  [the longest x1 0.91 us: per_device(): received[:, :, mode_count + 4:].reshape(ctx_count, chan_count, 2, 3)]
    all_to_all x3, starting transfers between devices: 19.4 us -> 21.2 us  [gather_by_exchange(): lax.all_to_all(copies, axis, split_axis=0, concat_axis=concat_axis, tiled...]
    unnamed x19 -> x29, local copies, waits for them, and re-layouts: 6.84 us -> 7.44 us
  transfers between devices with their start and end apart: 4 -> 3, of which waited for: 3 -> 3; matrix products, arithmetic and copies ran while one was open for 6% -> 8% of each run, Pallas kernels for 0% -> 0%
where the time goes in v4:
time: 158 us; the launch traced here: 155 us
  waiting for transfers between devices  54.5 us (34%)
  blocking collectives  40.7 us (26%)
  starting transfers between devices  21.2 us (13%)
  local copies, waits for them, and re-layouts  19.2 us (12%)
  other arithmetic  11.9 us (8%)
  matrix products  6.68 us (4%)
    all_to_all x3, waiting for transfers between devices, gather_by_exchange(): lax.all_to_all(copies, axis, split_axis=0, concat_axis=concat_axis, tiled...  54.5 us
    all_to_all x1, blocking collectives, per_device(): lax.all_to_all(partials, 'tp', split_axis=0, concat_axis=0, tiled=True)  40.7 us
    all_to_all x3, starting transfers between devices, gather_by_exchange(): lax.all_to_all(copies, axis, split_axis=0, concat_axis=concat_axis, tiled...  21.2 us
    unnamed x29, local copies, waits for them, and re-layouts  7.44 us
  transfers between devices with their start and end apart: 3, of which 3 were waited for; matrix products, arithmetic and copies ran while one was open for 8% of the time, Pallas kernels for 0%

profile of v4, /device:TPU:6, one launch (start us, length us, event | category | flops | bytes accessed | tf_op | source)
XLA Modules:
  0.0 155.2 jit_solution(8739979440762104626)
XLA Ops:
  0.7 1.0 convert_element_type.94
  1.7 0.7 slice.179
  2.4 0.7 slice.178
  3.1 0.7 slice_bitcast_fusion.8
  4.4 0.7 broadcast_multiply_fusion
  5.6 0.7 broadcast_in_dim.28
  6.3 10.1 %all-to-all-start = ((f32[16,128,26]{1,2,0:T(8,128)}), f32[16,128,26]{1,2,0:T(8,128)}, u32[]{:S(2)}, u32[]{:S(2)}) async-start(f32[16,128,26]{1,2,0:T(8,128)} %broadcast_in_dim.28), calls=%async_computation | async-start | bytes 524288 | tf_op jit(solution)/shard_map/all_to_all | solution.py:20
  20.4 0.7 slice.188
  21.1 1.4 copy.126
  22.6 1.3 fusion.81
  24.5 2.5 %all-to-all-done = f32[16,128,26]{1,2,0:T(8,128)} async-done(((f32[16,128,26]{1,2,0:T(8,128)}), f32[16,128,26]{1,2,0:T(8,128)}, u32[]{:S(2)}, u32[]{:S(2)}) %all-to-all-start) | async-done | bytes 213024 | tf_op jit(solution)/shard_map/all_to_all | solution.py:20
  27.0 0.9 slice.180
  28.0 0.8 slice.190
  28.8 0.7 fusion.69
  29.5 1.0 fusion.43
  30.6 0.7 copy.101
  31.3 0.7 fusion.39
  32.3 1.7 %convolution_bitcast_fusion = f32[128,16,8]{1,2,0:T(8,128)S(1)} fusion(bf16[128,8,16]{2,1,0:T(8,128)(2,1)S(1)} %copy.96, f32[16]{0:T(128)} %iota_subtract_fusion.2, f32[128,16]{1,0:T(8,128)S(1)} %copy.93), kind=kOutput, calls=%fused_computation.13 | convolution fusion | flops 3178496 | bytes 106560 | tf_op jit(solution)/shard_map/cnj,cmj->cnm/dot_general | solution.py:47
  34.2 1.0 multiply_reduce_fusion.1
  35.4 0.9 fusion.88
  36.4 1.2 convolution_add_fusion
  38.6 40.7 %all_to_all.28 = bf16[32,128,128]{1,2,0:T(8,128)(2,1)S(1)} all-to-all(bf16[32,128,128]{1,2,0:T(8,128)(2,1)S(1)} %bitcast.121), channel_id=1, replica_groups=mesh['ctx'=16,'tp'=32] {'tp'}, dimensions={0} | all-to-all | bytes 2097152 | tf_op jit(solution)/shard_map/all_to_all | solution.py:139
  79.4 1.2 broadcast_in_dim_broadcast_in_dim.2
  80.6 4.0 %all-to-all-start.2 = ((bf16[32,128,1,128]{3,1,2,0:T(8,128)(2,1)}), bf16[32,128,1,128]{3,1,2,0:T(8,128)(2,1)S(1)}, u32[]{:S(2)}, u32[]{:S(2)}) async-start(bf16[32,128,1,128]{3,1,2,0:T(8,128)(2,1)} %broadcast_in_dim_broadcast_in_dim.2), calls=%async_computation.2 | async-start | bytes 2097152 | tf_op jit(solution)/shard_map/all_to_all | solution.py:20
  84.6 4.7 %copy.106 = bf16[4096,3,128]{0,2,1:T(8,128)(2,1)} copy(bf16[4096,3,128]{2,0,1:T(8,128)(2,1)} %param.15) | data formatting | bytes 6291456 | tf_op args[7]
  89.4 24.3 %all-to-all-done.2 = bf16[32,128,1,128]{3,1,2,0:T(8,128)(2,1)S(1)} async-done(((bf16[32,128,1,128]{3,1,2,0:T(8,128)(2,1)}), bf16[32,128,1,128]{3,1,2,0:T(8,128)(2,1)S(1)}, u32[]{:S(2)}, u32[]{:S(2)}) %all-to-all-start.2) | async-done | bytes 1048608 | tf_op jit(solution)/shard_map/all_to_all | solution.py:20
  114.9 0.7 fusion.5
  116.2 1.0 fusion
  117.6 1.1 broadcast_in_dim.35
  118.6 7.1 %all-to-all-start.3 = ((bf16[16,128,256]{2,1,0:T(8,128)(2,1)}), bf16[16,128,256]{2,1,0:T(8,128)(2,1)S(1)}, u32[]{:S(2)}, u32[]{:S(2)}) async-start(bf16[16,128,256]{2,1,0:T(8,128)(2,1)} %broadcast_in_dim.35), calls=%async_computation.3 | async-start | bytes 2097152 | tf_op jit(solution)/shard_map/all_to_all | solution.py:20
  125.8 27.7 %all-to-all-done.3 = bf16[16,128,256]{2,1,0:T(8,128)(2,1)S(1)} async-done(((bf16[16,128,256]{2,1,0:T(8,128)(2,1)}), bf16[16,128,256]{2,1,0:T(8,128)(2,1)S(1)}, u32[]{:S(2)}, u32[]{:S(2)}) %all-to-all-start.3) | async-done | bytes 1048608 | tf_op jit(solution)/shard_map/all_to_all | solution.py:20
  154.2 1.0 fusion.7
  (81 shorter events, 10.5 us)
Async XLA Ops:
  0.6 37.2 %copy-start = (bf16[128,4096]{1,0:T(8,128)(2,1)S(1)}, bf16[128,4096]{1,0:T(8,128)(2,1)}, u32[]{:S(2)}) copy-start(bf16[128,4096]{1,0:T(8,128)(2,1)} %param.13) | copy-start | bytes 3145732
  0.6 15.7 %copy-start.9 = (f32[3,3,128]{2,1,0:T(4,128)S(1)}, f32[3,3,128]{2,1,0:T(4,128)}, u32[]{:S(2)}) copy-start(f32[3,3,128]{2,1,0:T(4,128)} %param.10) | copy-start | bytes 13828
  3.8 0.6 copy-start.5
  3.8 0.6 copy-start.6
  3.8 0.6 copy-start.7
  6.3 20.7 %all-to-all-start = ((f32[16,128,26]{1,2,0:T(8,128)}), f32[16,128,26]{1,2,0:T(8,128)}, u32[]{:S(2)}, u32[]{:S(2)}) async-start(f32[16,128,26]{1,2,0:T(8,128)} %broadcast_in_dim.28), calls=%async_computation | async-start | bytes 524288 | tf_op jit(solution)/shard_map/all_to_all | solution.py:20
  18.7 0.7 copy-start.11
  31.3 2.9 %copy-start.10 = (f32[8,8]{1,0:T(8,128)S(1)}, f32[8,8]{1,0:T(8,128)}, u32[]{:S(2)}) copy-start(f32[8,8]{1,0:T(8,128)} %fusion.80) | copy-start | bytes 772
  32.3 4.1 %copy-start.2 = (f32[128,16]{1,0:T(8,128)S(1)}, f32[128,16]{1,0:T(8,128)}, u32[]{:S(2)}) copy-start(f32[128,16]{1,0:T(8,128)} %copy.101) | copy-start | bytes 24580
  38.6 40.8 %copy-start.4 = (bf16[128,128]{1,0:T(8,128)(2,1)S(1)}, bf16[128,128]{1,0:T(8,128)(2,1)}, u32[]{:S(2)}) copy-start(bf16[128,128]{1,0:T(8,128)(2,1)} %param.8) | copy-start | bytes 98308
  79.4 9.9 %copy-start.3 = (bf16[128,128]{1,0:T(8,128)(2,1)}, bf16[128,128]{1,0:T(8,128)(2,1)S(1)}, u32[]{:S(2)}) copy-start(bf16[128,128]{1,0:T(8,128)(2,1)S(1)} %fusion.48) | copy-start | bytes 98308
  80.6 33.0 %all-to-all-start.2 = ((bf16[32,128,1,128]{3,1,2,0:T(8,128)(2,1)}), bf16[32,128,1,128]{3,1,2,0:T(8,128)(2,1)S(1)}, u32[]{:S(2)}, u32[]{:S(2)}) async-start(bf16[32,128,1,128]{3,1,2,0:T(8,128)(2,1)} %broadcast_in_dim_broadcast_in_dim.2), calls=%async_computation.2 | async-start | bytes 2097152 | tf_op jit(solution)/shard_map/all_to_all | solution.py:20
  89.4 25.5 %copy-start.8 = (f32[4096]{0:T(1024)S(1)}, f32[4096]{0:T(1024)}, u32[]{:S(2)}) copy-start(f32[4096]{0:T(1024)} %param.14) | copy-start | bytes 49156
  114.3 1.9 %copy-start.1 = (bf16[4096,3,128]{0,2,1:T(8,128)(2,1)S(1)}, bf16[4096,3,128]{0,2,1:T(8,128)(2,1)}, u32[]{:S(2)}) copy-start(bf16[4096,3,128]{0,2,1:T(8,128)(2,1)} %copy.106) | copy-start | bytes 9437188
  118.6 34.8 %all-to-all-start.3 = ((bf16[16,128,256]{2,1,0:T(8,128)(2,1)}), bf16[16,128,256]{2,1,0:T(8,128)(2,1)S(1)}, u32[]{:S(2)}, u32[]{:S(2)}) async-start(bf16[16,128,256]{2,1,0:T(8,128)(2,1)} %broadcast_in_dim.35), calls=%async_computation.3 | async-start | bytes 2097152 | tf_op jit(solution)/shard_map/all_to_all | solution.py:20

commit v5 on v4

--- a/solution.py
+++ b/solution.py
@@ -12,6 +12,12 @@
 rope_base = 10000.0
 mask_fill = -1e30
 highest = lax.Precision.HIGHEST
+
+
+def shifted(value, axis, steps):
+    count = lax.axis_size(axis)
+    initial, last = (max(0, -steps), min(count, count - steps))
+    return lax.ppermute(value, axis, [(source, source + steps) for source in range(initial, last)])
 
 
 def gather_by_exchange(block, axis, concat_axis=1):
@@ -118,7 +124,7 @@
         + edge_product[:, 0, :, None] * tail_powers[None, :, :, 0]
         + edge_product[:, 1, :, None] * tail_powers[None, :, :, 1]
     )
-    own_prior = lax.dynamic_index_in_dim(prev_tail, ctx_index, 0, keepdims=False)
+    own_prior = shifted(feats_wide[-2:], "ctx", 1)
     short_out = short_conv(jnp.concatenate([own_prior, feats_wide], axis=0), short_filter)
     product = (short_out[:, 1] * short_out[:, 2]).astype(jnp.bfloat16)
     signal = product.T.astype(jnp.float32)
@@ -135,11 +141,19 @@
     tp_count = lax.axis_size("tp")
     partials = lax.dot_general(
         out_weight, gated, (((0,), (1,)), ((), ())), preferred_element_type=jnp.float32
-    ).astype(jnp.bfloat16)
-    received = lax.all_to_all(partials, "tp", split_axis=0, concat_axis=0, tiled=True)
-    own_share = jnp.sum(
-        received.reshape(tp_count, chan_count, row_count).astype(jnp.float32), axis=0
-    )
+    ).reshape(tp_count // 2, 2, chan_count, row_count)
+    core = lax.axis_index("tp") % 2
+    kept = lax.dynamic_index_in_dim(partials, core, 1, keepdims=False)
+    given = lax.dynamic_index_in_dim(partials, 1 - core, 1, keepdims=False)
+    from_sibling = lax.ppermute(
+        given.astype(jnp.bfloat16), "tp", [(i, i ^ 1) for i in range(tp_count)]
+    )
+    chip_sum = (kept + from_sibling.astype(jnp.float32)).astype(jnp.bfloat16)
+    same_core = [[2 * i + c for i in range(tp_count // 2)] for c in range(2)]
+    received = lax.all_to_all(
+        chip_sum, "tp", split_axis=0, concat_axis=0, axis_index_groups=same_core
+    )
+    own_share = jnp.sum(received.astype(jnp.float32), axis=0)
     hyena_out = (resid_in.astype(jnp.float32) + own_share.T).astype(jnp.bfloat16)
     full_rows = gather_by_exchange(hyena_out, "tp").reshape(row_count, width_all)
     wide = full_rows.astype(jnp.float32)

time: 158 us -> 175 us (1.11)
  blocking collectives: 40.7 us -> 0 us
  waiting for transfers between devices: 54.5 us -> 75.1 us
  starting transfers between devices: 21.2 us -> 38.9 us
  local copies, waits for them, and re-layouts: 19.2 us -> 33.3 us
  other arithmetic: 11.9 us -> 14.7 us
  matrix products: 6.68 us -> 9.11 us
    all_to_all x1 -> x0, blocking collectives: 40.7 us -> none  [per_device(): lax.all_to_all(partials, 'tp', split_axis=0, concat_axis=0, tiled=True)]
    all_to_all x0 -> x1, waiting for transfers between devices: none -> 17 us  [per_device(): lax.all_to_all(chip_sum, 'tp', split_axis=0, concat_axis=0, axis_index_gr...]
    all_to_all x0 -> x1, starting transfers between devices: none -> 11.8 us  [per_device(): lax.all_to_all(chip_sum, 'tp', split_axis=0, concat_axis=0, axis_index_gr...]
    dynamic_slice x2 -> x3, local copies, waits for them, and re-layouts: 0.02 us -> 6.43 us  [the longest x2 4.39 us: per_device(): kept = lax.dynamic_index_in_dim(partials, core, 1, keepdims=False)]
    ppermute x0 -> x2, starting transfers between devices: none -> 6.22 us  [the longest x1 4.31 us: shifted(): lax.ppermute(value, axis, [(source, source + steps) for source in range(i...]
    all_to_all x3, waiting for transfers between devices: 54.5 us -> 58.2 us  [gather_by_exchange(): lax.all_to_all(copies, axis, split_axis=0, concat_axis=concat_axis, tiled...]
    reshape x0 -> x1, local copies, waits for them, and re-layouts: none -> 3.03 us  [per_device(): partials = lax.dot_general(out_weight, gated, (((0,), (1,)), ((), ())), p...]
    unnamed x29 -> x32, local copies, waits for them, and re-layouts: 7.44 us -> 10.3 us
  transfers between devices with their start and end apart: 3 -> 6, of which waited for: 3 -> 4; matrix products, arithmetic and copies ran while one was open for 8% -> 15% of each run, Pallas kernels for 0% -> 0%
where the time goes in v5:
time: 175 us; the launch traced here: 172 us
  waiting for transfers between devices  75.1 us (43%)
  starting transfers between devices  38.9 us (22%)
  local copies, waits for them, and re-layouts  33.3 us (19%)
  other arithmetic  14.7 us (8%)
  matrix products  9.11 us (5%)
    all_to_all x3, waiting for transfers between devices, gather_by_exchange(): lax.all_to_all(copies, axis, split_axis=0, concat_axis=concat_axis, tiled...  58.2 us
    all_to_all x3, starting transfers between devices, gather_by_exchange(): lax.all_to_all(copies, axis, split_axis=0, concat_axis=concat_axis, tiled...  20.9 us
    all_to_all x1, waiting for transfers between devices, per_device(): lax.all_to_all(chip_sum, 'tp', split_axis=0, concat_axis=0, axis_index_gr...  17 us
    all_to_all x1, starting transfers between devices, per_device(): lax.all_to_all(chip_sum, 'tp', split_axis=0, concat_axis=0, axis_index_gr...  11.8 us
    unnamed x32, local copies, waits for them, and re-layouts  10.3 us
    dynamic_slice x2, local copies, waits for them, and re-layouts, per_device(): kept = lax.dynamic_index_in_dim(partials, core, 1, keepdims=False)  4.39 us
    ppermute x1, starting transfers between devices, shifted(): lax.ppermute(value, axis, [(source, source + steps) for source in range(i...  4.31 us
  transfers between devices with their start and end apart: 6, of which 4 were waited for; matrix products, arithmetic and copies ran while one was open for 15% of the time, Pallas kernels for 0%

profile of v5, /device:TPU:6, one launch (start us, length us, event | category | flops | bytes accessed | tf_op | source)
XLA Modules:
  0.0 172.2 jit_solution(16412222092038246043)
XLA Ops:
  1.4 4.3 %collective-permute-start = (f32[2,3,128]{2,0,1:T(2,128)S(1)}, f32[2,3,128]{2,0,1:T(2,128)S(1)}, u32[]{:S(2)}, u32[]{:S(2)}) collective-permute-start(f32[2,3,128]{2,0,1:T(2,128)S(1)} %slice.175), channel_id=1, source_target_pairs={{0,32},{32,64},{64,96},{96,128},{128,160},{160,192},{192,224},{224... | collective-permute-start | bytes 9224 | tf_op jit(solution)/shard_map/ppermute | solution.py:20
  5.8 1.3 slice_bitcast_fusion.8
  7.1 1.3 slice_bitcast_fusion.11
  13.8 0.9 convert_element_type.100
  21.3 9.2 %all-to-all-start = ((f32[16,128,26]{1,2,0:T(8,128)}), f32[16,128,26]{1,2,0:T(8,128)}, u32[]{:S(2)}, u32[]{:S(2)}) async-start(f32[16,128,26]{1,2,0:T(8,128)} %broadcast_in_dim.34), calls=%async_computation | async-start | bytes 524288 | tf_op jit(solution)/shard_map/all_to_all | solution.py:26
  30.7 1.9 %convolution_bitcast_fusion.1 = f32[128,16,8]{1,2,0:T(8,128)S(1)} fusion(bf16[128,8,16]{2,1,0:T(8,128)(2,1)S(1)} %copy.89, f32[16]{0:T(128)} %iota_subtract_fusion.3, f32[128,16]{1,0:T(8,128)} %copy-done.3), kind=kOutput, calls=%fused_computation.11 | convolution fusion | flops 3178496 | bytes 106560 | tf_op jit(solution)/shard_map/cnj,cmj->cnm/dot_general | solution.py:53
  32.8 1.0 multiply_reduce_fusion.1
  34.1 0.9 fusion.88
  35.0 5.9 %all-to-all-done = f32[16,128,26]{1,2,0:T(8,128)} async-done(((f32[16,128,26]{1,2,0:T(8,128)}), f32[16,128,26]{1,2,0:T(8,128)}, u32[]{:S(2)}, u32[]{:S(2)}) %all-to-all-start) | async-done | bytes 213024 | tf_op jit(solution)/shard_map/all_to_all | solution.py:26
  40.9 0.9 slice.190
  43.4 1.0 fusion.43
  44.6 2.1 %convolution_add_fusion = f32[128,8,16]{2,1,0:T(8,128)S(1)} fusion(f32[128,8,16]{2,1,0:T(8,128)S(1)} %fusion.88, f32[128,16,8]{1,2,0:T(8,128)S(1)} %copy.115, f32[128,16]{1,0:T(8,128)S(1)} %copy-done.4, f32[128,16]{1,0:T(8,128)S(1)} %copy-done.6, f32[128,16]{1,0:T(8,128)S(1)} %copy.97, f32[128,16]{1,0:T(8,128)} %copy.91), kind=kOutput, calls=%fused_computation.10 | convolution fusion | flops 3260416 | bytes 229376 | tf_op jit(solution)/shard_map/cnm,cmi->cni/dot_general | solution.py:66
  46.8 0.9 fusion.47
  47.7 1.8 %convolution_bitcast_fusion = f32[4096,128]{0,1:T(8,128)} fusion(bf16[128,128]{1,0:T(8,128)(2,1)S(1)} %fusion.47, bf16[128,4096]{1,0:T(8,128)(2,1)S(1)} %copy-done), kind=kOutput, calls=%fused_computation | convolution fusion | flops 134217728 | bytes 3178496 | tf_op jit(solution)/shard_map/dot_general | solution.py:142
  49.5 3.0 %reshape.299 = f32[16,2,128,128]{2,1,0,3:T(2,128)S(1)} reshape(f32[4096,128]{0,1:T(8,128)} %convolution_bitcast_fusion) | data formatting | bytes 4194304 | tf_op jit(solution)/shard_map/reshape | solution.py:144
  52.5 2.0 %constant_dynamic-slice_fusion = bf16[16,1,128,128]{2,1,0,3:T(2,128)(2,1)} fusion(f32[16,2,128,128]{2,1,0,3:T(2,128)S(1)} %reshape.299, s32[]{:T(128)S(6)} %select_n.35), kind=kLoop, calls=%fused_computation.134 | loop fusion | bytes 1048580 | tf_op jit(solution)/shard_map/jit(dynamic_index_in_dim)/dynamic_slice | solution.py:147
  54.6 3.5 %copy.127 = bf16[16,1,128,128]{3,2,0,1:T(8,128)(2,1)} copy(bf16[16,1,128,128]{2,1,0,3:T(2,128)(2,1)} %constant_dynamic-slice_fusion) | data formatting | bytes 1048576
  58.1 1.9 %collective-permute-start.1 = (bf16[16,128,128]{2,1,0:T(8,128)(2,1)}, bf16[16,128,128]{2,1,0:T(8,128)(2,1)}, u32[]{:S(2)}, u32[]{:S(2)}) collective-permute-start(bf16[16,128,128]{2,1,0:T(8,128)(2,1)} %bitcast.126), channel_id=1, source_target_pairs={{0,1},{1,0},{2,3},{3,2},{4,5},{5,4},{6,7},{7,6},{8,9},{9,8},{10,11... | collective-permute-start | bytes 1572872 | tf_op jit(solution)/shard_map/ppermute | solution.py:148
  60.0 2.1 %constant_dynamic-slice_fusion.1 = f32[16,1,128,128]{2,1,0,3:T(1,128)} fusion(f32[16,2,128,128]{2,1,0,3:T(2,128)S(1)} %reshape.299, s32[]{:T(128)S(6)} %select_n.34), kind=kLoop, calls=%fused_computation.135 | loop fusion | bytes 2097156 | tf_op jit(solution)/shard_map/jit(dynamic_index_in_dim)/dynamic_slice | solution.py:146
  62.0 2.3 %copy.100 = f32[16,1,128,128]{3,2,0,1:T(8,128)S(1)} copy(f32[16,1,128,128]{2,1,0,3:T(1,128)} %constant_dynamic-slice_fusion.1) | data formatting | bytes 2097152 | tf_op jit(solution)/shard_map/jit(dynamic_index_in_dim)/dynamic_slice | solution.py:146
  64.4 2.0 %fusion.7 = bf16[16,128,128]{2,1,0:T(8,128)(2,1)} fusion(f32[16,1,128,128]{3,2,0,1:T(8,128)S(1)} %copy.100, bf16[16,128,128]{2,1,0:T(8,128)(2,1)} %collective-permute-done.1), kind=kLoop, calls=%fused_computation.15 | loop fusion | flops 786432 | bytes 2097152 | tf_op jit(solution)/shard_map/convert_element_type | solution.py:151
  66.4 11.8 %all-to-all-start.1 = ((bf16[16,128,128]{2,1,0:T(8,128)(2,1)}), bf16[16,128,128]{2,1,0:T(8,128)(2,1)S(1)}, u32[]{:S(2)}, u32[]{:S(2)}) async-start(bf16[16,128,128]{2,1,0:T(8,128)(2,1)} %fusion.7), calls=%async_computation.1 | async-start | bytes 1048576 | tf_op jit(solution)/shard_map/all_to_all | solution.py:153
  78.3 17.0 %all-to-all-done.1 = bf16[16,128,128]{2,1,0:T(8,128)(2,1)S(1)} async-done(((bf16[16,128,128]{2,1,0:T(8,128)(2,1)}), bf16[16,128,128]{2,1,0:T(8,128)(2,1)S(1)}, u32[]{:S(2)}, u32[]{:S(2)}) %all-to-all-start.1) | async-done | bytes 524320 | tf_op jit(solution)/shard_map/all_to_all | solution.py:153
  95.5 1.2 broadcast_in_dim_broadcast_in_dim.2
  96.7 5.2 %all-to-all-start.2 = ((bf16[32,128,1,128]{3,1,2,0:T(8,128)(2,1)}), bf16[32,128,1,128]{3,1,2,0:T(8,128)(2,1)S(1)}, u32[]{:S(2)}, u32[]{:S(2)}) async-start(bf16[32,128,1,128]{3,1,2,0:T(8,128)(2,1)} %broadcast_in_dim_broadcast_in_dim.2), calls=%async_computation.2 | async-start | bytes 2097152 | tf_op jit(solution)/shard_map/all_to_all | solution.py:26
  101.9 4.7 %copy.104 = bf16[4096,3,128]{0,2,1:T(8,128)(2,1)} copy(bf16[4096,3,128]{2,0,1:T(8,128)(2,1)} %param.15) | data formatting | bytes 6291456 | tf_op args[7]
  106.6 24.3 %all-to-all-done.2 = bf16[32,128,1,128]{3,1,2,0:T(8,128)(2,1)S(1)} async-done(((bf16[32,128,1,128]{3,1,2,0:T(8,128)(2,1)}), bf16[32,128,1,128]{3,1,2,0:T(8,128)(2,1)S(1)}, u32[]{:S(2)}, u32[]{:S(2)}) %all-to-all-start.2) | async-done | bytes 1048608 | tf_op jit(solution)/shard_map/all_to_all | solution.py:26
  133.4 1.0 fusion
  134.8 1.1 broadcast_in_dim.35
  135.9 6.6 %all-to-all-start.3 = ((bf16[16,128,256]{2,1,0:T(8,128)(2,1)}), bf16[16,128,256]{2,1,0:T(8,128)(2,1)S(1)}, u32[]{:S(2)}, u32[]{:S(2)}) async-start(bf16[16,128,256]{2,1,0:T(8,128)(2,1)} %broadcast_in_dim.35), calls=%async_computation.3 | async-start | bytes 2097152 | tf_op jit(solution)/shard_map/all_to_all | solution.py:26
  142.5 28.0 %all-to-all-done.3 = bf16[16,128,256]{2,1,0:T(8,128)(2,1)S(1)} async-done(((bf16[16,128,256]{2,1,0:T(8,128)(2,1)}), bf16[16,128,256]{2,1,0:T(8,128)(2,1)S(1)}, u32[]{:S(2)}, u32[]{:S(2)}) %all-to-all-start.3) | async-done | bytes 1048608 | tf_op jit(solution)/shard_map/all_to_all | solution.py:26
  171.2 1.0 fusion.6
  (90 shorter events, 19.1 us)
Async XLA Ops:
  0.6 47.1 %copy-start = (bf16[128,4096]{1,0:T(8,128)(2,1)S(1)}, bf16[128,4096]{1,0:T(8,128)(2,1)}, u32[]{:S(2)}) copy-start(bf16[128,4096]{1,0:T(8,128)(2,1)} %param.13) | copy-start | bytes 3145732
  1.4 16.8 %collective-permute-start = (f32[2,3,128]{2,0,1:T(2,128)S(1)}, f32[2,3,128]{2,0,1:T(2,128)S(1)}, u32[]{:S(2)}, u32[]{:S(2)}) collective-permute-start(f32[2,3,128]{2,0,1:T(2,128)S(1)} %slice.175), channel_id=1, source_target_pairs={{0,32},{32,64},{64,96},{96,128},{128,160},{160,192},{192,224},{224... | collective-permute-start | bytes 9224 | tf_op jit(solution)/shard_map/ppermute | solution.py:20
  11.5 5.9 %copy-start.9 = (f32[128,16]{0,1:T(8,128)}, f32[128,16]{0,1:T(8,128)S(1)}, u32[]{:S(2)}) copy-start(f32[128,16]{0,1:T(8,128)S(1)} %get-tuple-element.19) | copy-start | bytes 24580
  11.6 5.1 %copy-start.3 = (f32[128,16]{1,0:T(8,128)}, f32[128,16]{1,0:T(8,128)S(1)}, u32[]{:S(2)}) copy-start(f32[128,16]{1,0:T(8,128)S(1)} %copy.86) | copy-start | bytes 24580
  12.6 4.2 %copy-start.5 = (f32[128,16]{1,0:T(8,128)}, f32[128,16]{1,0:T(8,128)S(1)}, u32[]{:S(2)}) copy-start(f32[128,16]{1,0:T(8,128)S(1)} %copy.85) | copy-start | bytes 24580
  18.2 0.6 copy-start.11
  19.6 10.9 %copy-start.2 = (f32[128,3,128]{2,0,1:T(8,128)}, f32[128,3,128]{2,0,1:T(8,128)S(1)}, u32[]{:S(2)}) copy-start(f32[128,3,128]{2,0,1:T(8,128)S(1)} %get-tuple-element.11) | copy-start | bytes 589828
  21.3 19.6 %all-to-all-start = ((f32[16,128,26]{1,2,0:T(8,128)}), f32[16,128,26]{1,2,0:T(8,128)}, u32[]{:S(2)}, u32[]{:S(2)}) async-start(f32[16,128,26]{1,2,0:T(8,128)} %broadcast_in_dim.34), calls=%async_computation | async-start | bytes 524288 | tf_op jit(solution)/shard_map/all_to_all | solution.py:26
  32.6 11.9 %copy-start.4 = (f32[128,16]{1,0:T(8,128)S(1)}, f32[128,16]{1,0:T(8,128)}, u32[]{:S(2)}) copy-start(f32[128,16]{1,0:T(8,128)} %copy-done.3) | copy-start | bytes 24580
  32.6 11.9 %copy-start.6 = (f32[128,16]{1,0:T(8,128)S(1)}, f32[128,16]{1,0:T(8,128)}, u32[]{:S(2)}) copy-start(f32[128,16]{1,0:T(8,128)} %copy-done.5) | copy-start | bytes 24580
  58.1 6.3 %collective-permute-start.1 = (bf16[16,128,128]{2,1,0:T(8,128)(2,1)}, bf16[16,128,128]{2,1,0:T(8,128)(2,1)}, u32[]{:S(2)}, u32[]{:S(2)}) collective-permute-start(bf16[16,128,128]{2,1,0:T(8,128)(2,1)} %bitcast.126), channel_id=1, source_target_pairs={{0,1},{1,0},{2,3},{3,2},{4,5},{5,4},{6,7},{7,6},{8,9},{9,8},{10,11... | collective-permute-start | bytes 1572872 | tf_op jit(solution)/shard_map/ppermute | solution.py:148
  64.4 13.8 %copy-start.8 = (bf16[128,128]{1,0:T(8,128)(2,1)S(1)}, bf16[128,128]{1,0:T(8,128)(2,1)}, u32[]{:S(2)}) copy-start(bf16[128,128]{1,0:T(8,128)(2,1)} %param.8) | copy-start | bytes 98308
  66.4 28.9 %all-to-all-start.1 = ((bf16[16,128,128]{2,1,0:T(8,128)(2,1)}), bf16[16,128,128]{2,1,0:T(8,128)(2,1)S(1)}, u32[]{:S(2)}, u32[]{:S(2)}) async-start(bf16[16,128,128]{2,1,0:T(8,128)(2,1)} %fusion.7), calls=%async_computation.1 | async-start | bytes 1048576 | tf_op jit(solution)/shard_map/all_to_all | solution.py:153
  95.5 11.1 %copy-start.7 = (bf16[128,128]{1,0:T(8,128)(2,1)}, bf16[128,128]{1,0:T(8,128)(2,1)S(1)}, u32[]{:S(2)}) copy-start(bf16[128,128]{1,0:T(8,128)(2,1)S(1)} %copy.107) | copy-start | bytes 98308
  96.7 34.2 %all-to-all-start.2 = ((bf16[32,128,1,128]{3,1,2,0:T(8,128)(2,1)}), bf16[32,128,1,128]{3,1,2,0:T(8,128)(2,1)S(1)}, u32[]{:S(2)}, u32[]{:S(2)}) async-start(bf16[32,128,1,128]{3,1,2,0:T(8,128)(2,1)} %broadcast_in_dim_broadcast_in_dim.2), calls=%async_computation.2 | async-start | bytes 2097152 | tf_op jit(solution)/shard_map/all_to_all | solution.py:26
  106.6 25.6 %copy-start.10 = (f32[4096]{0:T(1024)S(1)}, f32[4096]{0:T(1024)}, u32[]{:S(2)}) copy-start(f32[4096]{0:T(1024)} %param.14) | copy-start | bytes 49156
  131.6 1.9 %copy-start.1 = (bf16[4096,3,128]{0,2,1:T(8,128)(2,1)S(1)}, bf16[4096,3,128]{0,2,1:T(8,128)(2,1)}, u32[]{:S(2)}) copy-start(bf16[4096,3,128]{0,2,1:T(8,128)(2,1)} %copy.104) | copy-start | bytes 9437188
  135.9 34.6 %all-to-all-start.3 = ((bf16[16,128,256]{2,1,0:T(8,128)(2,1)}), bf16[16,128,256]{2,1,0:T(8,128)(2,1)S(1)}, u32[]{:S(2)}, u32[]{:S(2)}) async-start(bf16[16,128,256]{2,1,0:T(8,128)(2,1)} %broadcast_in_dim.35), calls=%async_computation.3 | async-start | bytes 2097152 | tf_op jit(solution)/shard_map/all_to_all | solution.py:26

commit v6 on v4

--- a/solution.py
+++ b/solution.py
@@ -118,10 +118,6 @@
         + edge_product[:, 0, :, None] * tail_powers[None, :, :, 0]
         + edge_product[:, 1, :, None] * tail_powers[None, :, :, 1]
     )
-    own_prior = lax.dynamic_index_in_dim(prev_tail, ctx_index, 0, keepdims=False)
-    short_out = short_conv(jnp.concatenate([own_prior, feats_wide], axis=0), short_filter)
-    product = (short_out[:, 1] * short_out[:, 2]).astype(jnp.bfloat16)
-    signal = product.T.astype(jnp.float32)
     shard_steps = jnp.arange(ctx_count, dtype=jnp.float32)
     gap_count = ctx_index.astype(jnp.float32) - 1.0 - shard_steps
     decay = jnp.where(
@@ -130,8 +126,23 @@
         0.0,
     )
     start_state = jnp.sum(decay * gathered_states, axis=0)
-    conv_out = modal_conv(signal, residues, rates, start_state, block_limit=16).T
-    gated = (short_out[:, 0] * conv_out).astype(jnp.bfloat16)
+    conv_blind = modal_conv(
+        blind_product, residues, rates, jnp.zeros_like(rates), block_limit=16
+    )
+    weight = residues * jnp.sqrt(1.0 - jnp.exp(-2.0 * rates))
+    full_powers = jnp.exp(-rates[:, :, None] * lag_steps)
+    long_taps = jnp.sum(weight[:, :, None] * full_powers, axis=1)
+    later_taps = jnp.concatenate([jnp.zeros_like(long_taps[:, :1]), long_taps[:, :-1]], axis=1)
+    own_prior = lax.dynamic_index_in_dim(prev_tail, ctx_index, 0, keepdims=False)
+    own_edge = short_conv(jnp.concatenate([own_prior, feats_wide[:2]], axis=0), short_filter)
+    own_edge_product = (own_edge[:, 1] * own_edge[:, 2]).astype(jnp.bfloat16).astype(jnp.float32)
+    delta = own_edge_product - blind_product[:, :2].T
+    start_part = jnp.sum((weight * start_state)[:, :, None] * full_powers, axis=1)
+    conv_out = (
+        conv_blind + start_part + long_taps * delta[0][:, None] + later_taps * delta[1][:, None]
+    ).T
+    short_query = jnp.concatenate([own_edge[:, 0], blind[2:, 0]], axis=0)
+    gated = (short_query * conv_out).astype(jnp.bfloat16)
     tp_count = lax.axis_size("tp")
     partials = lax.dot_general(
         out_weight, gated, (((0,), (1,)), ((), ())), preferred_element_type=jnp.float32

time: 158 us -> 154 us (0.975)
  waiting for transfers between devices: 54.5 us -> 59 us
  other arithmetic: 11.9 us -> 8.15 us
  local copies, waits for them, and re-layouts: 19.2 us -> 16 us
    all_to_all x3, waiting for transfers between devices: 54.5 us -> 59 us  [gather_by_exchange(): lax.all_to_all(copies, axis, split_axis=0, concat_axis=concat_axis, tiled...]
    unnamed x29 -> x33, local copies, waits for them, and re-layouts: 7.44 us -> 6.55 us
  transfers between devices with their start and end apart: 3 -> 3, of which waited for: 3 -> 3; matrix products, arithmetic and copies ran while one was open for 8% -> 6% of each run, Pallas kernels for 0% -> 0%
where the time goes in v6:
time: 154 us; the launch traced here: 152 us
  waiting for transfers between devices  59 us (38%)
  blocking collectives  40.7 us (26%)
  starting transfers between devices  20.6 us (13%)
  local copies, waits for them, and re-layouts  16 us (10%)
  other arithmetic  8.15 us (5%)
  matrix products  6.08 us (4%)
    all_to_all x3, waiting for transfers between devices, gather_by_exchange(): lax.all_to_all(copies, axis, split_axis=0, concat_axis=concat_axis, tiled...  59 us
    all_to_all x1, blocking collectives, per_device(): lax.all_to_all(partials, 'tp', split_axis=0, concat_axis=0, tiled=True)  40.7 us
    all_to_all x3, starting transfers between devices, gather_by_exchange(): lax.all_to_all(copies, axis, split_axis=0, concat_axis=concat_axis, tiled...  20.6 us
    unnamed x33, local copies, waits for them, and re-layouts  6.55 us
  transfers between devices with their start and end apart: 3, of which 3 were waited for; matrix products, arithmetic and copies ran while one was open for 6% of the time, Pallas kernels for 0%

profile of v6, /device:TPU:6, one launch (start us, length us, event | category | flops | bytes accessed | tf_op | source)
XLA Modules:
  0.0 151.6 jit_solution(8733011837166347057)
XLA Ops:
  0.7 1.0 convert_element_type.97
  1.7 1.3 fusion.87
  3.0 0.7 slice.200
  3.6 0.7 slice_bitcast_fusion.8
  4.5 0.5 copy-done.9
  5.0 1.3 broadcast_multiply_fusion.1
  6.7 0.7 broadcast_in_dim.28
  7.4 10.1 %all-to-all-start = ((f32[16,128,26]{1,2,0:T(8,128)}), f32[16,128,26]{1,2,0:T(8,128)S(1)}, u32[]{:S(2)}, u32[]{:S(2)}) async-start(f32[16,128,26]{1,2,0:T(8,128)} %broadcast_in_dim.28), calls=%async_computation | async-start | bytes 524288 | tf_op jit(solution)/shard_map/all_to_all | solution.py:20
  17.5 0.6 slice_bitcast_fusion.4
  18.7 1.1 convolution_bitcast_fusion
  20.6 0.7 slice_bitcast_fusion.12
  21.4 6.7 %all-to-all-done = f32[16,128,26]{1,2,0:T(8,128)S(1)} async-done(((f32[16,128,26]{1,2,0:T(8,128)}), f32[16,128,26]{1,2,0:T(8,128)S(1)}, u32[]{:S(2)}, u32[]{:S(2)}) %all-to-all-start) | async-done | bytes 213024 | tf_op jit(solution)/shard_map/all_to_all | solution.py:20
  28.2 0.8 fusion.78
  29.0 0.7 convert_subtract_fusion
  30.0 0.6 multiply_reduce_fusion.2
  31.5 0.9 fusion.89
  32.5 1.2 convolution_add_fusion
  33.9 0.6 multiply_reduce_fusion
  35.2 40.7 %all_to_all.28 = bf16[32,128,128]{1,2,0:T(8,128)(2,1)S(1)} all-to-all(bf16[32,128,128]{1,2,0:T(8,128)(2,1)S(1)} %bitcast.132), channel_id=1, replica_groups=mesh['ctx'=16,'tp'=32] {'tp'}, dimensions={0} | all-to-all | bytes 2097152 | tf_op jit(solution)/shard_map/all_to_all | solution.py:150
  76.1 1.2 broadcast_in_dim_broadcast_in_dim.2
  77.3 4.0 %all-to-all-start.2 = ((bf16[32,128,1,128]{3,1,2,0:T(8,128)(2,1)}), bf16[32,128,1,128]{3,1,2,0:T(8,128)(2,1)S(1)}, u32[]{:S(2)}, u32[]{:S(2)}) async-start(bf16[32,128,1,128]{3,1,2,0:T(8,128)(2,1)} %broadcast_in_dim_broadcast_in_dim.2), calls=%async_computation.2 | async-start | bytes 2097152 | tf_op jit(solution)/shard_map/all_to_all | solution.py:20
  81.3 4.7 %copy.102 = bf16[4096,3,128]{0,2,1:T(8,128)(2,1)} copy(bf16[4096,3,128]{2,0,1:T(8,128)(2,1)} %param.15) | data formatting | bytes 6291456 | tf_op args[7]
  86.1 24.3 %all-to-all-done.2 = bf16[32,128,1,128]{3,1,2,0:T(8,128)(2,1)S(1)} async-done(((bf16[32,128,1,128]{3,1,2,0:T(8,128)(2,1)}), bf16[32,128,1,128]{3,1,2,0:T(8,128)(2,1)S(1)}, u32[]{:S(2)}, u32[]{:S(2)}) %all-to-all-start.2) | async-done | bytes 1048608 | tf_op jit(solution)/shard_map/all_to_all | solution.py:20
  110.3 0.7 copy.101
  111.0 0.6 fusion.3
  111.6 0.7 fusion.5
  112.3 0.6 copy-done.1
  112.9 1.0 fusion
  114.2 1.1 broadcast_in_dim.35
  115.3 6.5 %all-to-all-start.3 = ((bf16[16,128,256]{2,1,0:T(8,128)(2,1)}), bf16[16,128,256]{2,1,0:T(8,128)(2,1)S(1)}, u32[]{:S(2)}, u32[]{:S(2)}) async-start(bf16[16,128,256]{2,1,0:T(8,128)(2,1)} %broadcast_in_dim.35), calls=%async_computation.3 | async-start | bytes 2097152 | tf_op jit(solution)/shard_map/all_to_all | solution.py:20
  121.8 28.0 %all-to-all-done.3 = bf16[16,128,256]{2,1,0:T(8,128)(2,1)S(1)} async-done(((bf16[16,128,256]{2,1,0:T(8,128)(2,1)}), bf16[16,128,256]{2,1,0:T(8,128)(2,1)S(1)}, u32[]{:S(2)}, u32[]{:S(2)}) %all-to-all-start.3) | async-done | bytes 1048608 | tf_op jit(solution)/shard_map/all_to_all | solution.py:20
  150.6 1.0 fusion.7
  (90 shorter events, 5.3 us)
Async XLA Ops:
  0.6 33.9 %copy-start = (bf16[128,4096]{1,0:T(8,128)(2,1)S(1)}, bf16[128,4096]{1,0:T(8,128)(2,1)}, u32[]{:S(2)}) copy-start(bf16[128,4096]{1,0:T(8,128)(2,1)} %param.13) | copy-start | bytes 3145732
  4.4 0.6 copy-start.9
  4.4 0.6 copy-start.10
  4.4 1.9 %copy-start.11 = (f32[3,128]{1,0:T(4,128)}, f32[3,128]{1,0:T(4,128)S(1)}, u32[]{:S(2)}) copy-start(f32[3,128]{1,0:T(4,128)S(1)} %get-tuple-element.24) | copy-start | bytes 4612
  4.9 2.5 %copy-start.2 = (bf16[128,128]{0,1:T(8,128)(2,1)}, bf16[128,128]{0,1:T(8,128)(2,1)S(1)}, u32[]{:S(2)}) copy-start(bf16[128,128]{0,1:T(8,128)(2,1)S(1)} %fusion.96) | copy-start | bytes 98308
  7.4 20.6 %all-to-all-start = ((f32[16,128,26]{1,2,0:T(8,128)}), f32[16,128,26]{1,2,0:T(8,128)S(1)}, u32[]{:S(2)}, u32[]{:S(2)}) async-start(f32[16,128,26]{1,2,0:T(8,128)} %broadcast_in_dim.28), calls=%async_computation | async-start | bytes 524288 | tf_op jit(solution)/shard_map/all_to_all | solution.py:20
  17.5 12.3 %copy-start.4 = (f32[128,16]{0,1:T(8,128)S(1)}, f32[128,16]{0,1:T(8,128)}, u32[]{:S(2)}) copy-start(f32[128,16]{0,1:T(8,128)} %param.12) | copy-start | bytes 24580
  18.1 11.6 %copy-start.5 = (f32[128,16]{0,1:T(8,128)S(1)}, f32[128,16]{0,1:T(8,128)}, u32[]{:S(2)}) copy-start(f32[128,16]{0,1:T(8,128)} %get-tuple-element.17) | copy-start | bytes 24580
  18.1 11.6 %copy-start.6 = (f32[128,16]{0,1:T(8,128)S(1)}, f32[128,16]{0,1:T(8,128)}, u32[]{:S(2)}) copy-start(f32[128,16]{0,1:T(8,128)} %get-tuple-element.6) | copy-start | bytes 24580
  18.1 11.6 %copy-start.7 = (f32[128,16]{0,1:T(8,128)S(1)}, f32[128,16]{0,1:T(8,128)}, u32[]{:S(2)}) copy-start(f32[128,16]{0,1:T(8,128)} %get-tuple-element.7) | copy-start | bytes 24580
  18.2 11.7 %copy-start.13 = (f32[128,16]{0,1:T(8,128)S(1)}, f32[128,16]{0,1:T(8,128)}, u32[]{:S(2)}) copy-start(f32[128,16]{0,1:T(8,128)} %param.11) | copy-start | bytes 24580
  35.2 40.8 %copy-start.8 = (bf16[128,128]{1,0:T(8,128)(2,1)S(1)}, bf16[128,128]{1,0:T(8,128)(2,1)}, u32[]{:S(2)}) copy-start(bf16[128,128]{1,0:T(8,128)(2,1)} %param.8) | copy-start | bytes 98308
  76.1 9.9 %copy-start.3 = (bf16[128,128]{1,0:T(8,128)(2,1)}, bf16[128,128]{1,0:T(8,128)(2,1)S(1)}, u32[]{:S(2)}) copy-start(bf16[128,128]{1,0:T(8,128)(2,1)S(1)} %fusion.41) | copy-start | bytes 98308
  77.3 33.0 %all-to-all-start.2 = ((bf16[32,128,1,128]{3,1,2,0:T(8,128)(2,1)}), bf16[32,128,1,128]{3,1,2,0:T(8,128)(2,1)S(1)}, u32[]{:S(2)}, u32[]{:S(2)}) async-start(bf16[32,128,1,128]{3,1,2,0:T(8,128)(2,1)} %broadcast_in_dim_broadcast_in_dim.2), calls=%async_computation.2 | async-start | bytes 2097152 | tf_op jit(solution)/shard_map/all_to_all | solution.py:20
  86.0 25.5 %copy-start.12 = (f32[4096]{0:T(1024)S(1)}, f32[4096]{0:T(1024)}, u32[]{:S(2)}) copy-start(f32[4096]{0:T(1024)} %param.14) | copy-start | bytes 49156
  111.0 1.9 %copy-start.1 = (bf16[4096,3,128]{0,2,1:T(8,128)(2,1)S(1)}, bf16[4096,3,128]{0,2,1:T(8,128)(2,1)}, u32[]{:S(2)}) copy-start(bf16[4096,3,128]{0,2,1:T(8,128)(2,1)} %copy.102) | copy-start | bytes 9437188
  115.3 34.5 %all-to-all-start.3 = ((bf16[16,128,256]{2,1,0:T(8,128)(2,1)}), bf16[16,128,256]{2,1,0:T(8,128)(2,1)S(1)}, u32[]{:S(2)}, u32[]{:S(2)}) async-start(bf16[16,128,256]{2,1,0:T(8,128)(2,1)} %broadcast_in_dim.35), calls=%async_computation.3 | async-start | bytes 2097152 | tf_op jit(solution)/shard_map/all_to_all | solution.py:20

commit v7 on v6

--- a/solution.py
+++ b/solution.py
@@ -144,14 +144,24 @@
     short_query = jnp.concatenate([own_edge[:, 0], blind[2:, 0]], axis=0)
     gated = (short_query * conv_out).astype(jnp.bfloat16)
     tp_count = lax.axis_size("tp")
-    partials = lax.dot_general(
-        out_weight, gated, (((0,), (1,)), ((), ())), preferred_element_type=jnp.float32
-    ).astype(jnp.bfloat16)
-    received = lax.all_to_all(partials, "tp", split_axis=0, concat_axis=0, tiled=True)
-    own_share = jnp.sum(
-        received.reshape(tp_count, chan_count, row_count).astype(jnp.float32), axis=0
-    )
-    hyena_out = (resid_in.astype(jnp.float32) + own_share.T).astype(jnp.bfloat16)
+    pair_weight = out_weight.reshape(chan_count, tp_count // 2, 2, width_all // tp_count)
+    even_part = jnp.einsum(
+        "tc,cid->itd", gated, pair_weight[:, :, 0], preferred_element_type=jnp.float32
+    )
+    odd_part = jnp.einsum(
+        "tc,cid->itd", gated, pair_weight[:, :, 1], preferred_element_type=jnp.float32
+    )
+    is_even = lax.axis_index("tp") % 2 == 0
+    kept = jnp.where(is_even, even_part, odd_part)
+    given = jnp.where(is_even, odd_part, even_part).astype(jnp.bfloat16)
+    from_sibling = lax.ppermute(given, "tp", [(i, i ^ 1) for i in range(tp_count)])
+    chip_sum = (kept + from_sibling.astype(jnp.float32)).astype(jnp.bfloat16)
+    same_core = [[2 * i + c for i in range(tp_count // 2)] for c in range(2)]
+    received = lax.all_to_all(
+        chip_sum, "tp", split_axis=0, concat_axis=0, axis_index_groups=same_core
+    )
+    own_share = jnp.sum(received.astype(jnp.float32), axis=0)
+    hyena_out = (resid_in.astype(jnp.float32) + own_share).astype(jnp.bfloat16)
     full_rows = gather_by_exchange(hyena_out, "tp").reshape(row_count, width_all)
     wide = full_rows.astype(jnp.float32)
     mean_square = jnp.mean(wide * wide, axis=1, keepdims=True)

time: 154 us -> 153 us (level)
  blocking collectives: 40.7 us -> 28.3 us
  other arithmetic: 8.15 us -> 13.6 us
  starting transfers between devices: 20.6 us -> 24.1 us
  waiting for transfers between devices: 59 us -> 60.7 us
    all_to_all x1, blocking collectives: 40.7 us -> 28.3 us  [per_device(): lax.all_to_all(chip_sum, 'tp', split_axis=0, concat_axis=0, axis_index_gr...]
    ppermute x0 -> x1, starting transfers between devices: none -> 1.92 us  [per_device(): lax.ppermute(given, 'tp', [(i, i ^ 1) for i in range(tp_count)])]
    ppermute x0 -> x1, waiting for transfers between devices: none -> 1.88 us  [per_device(): lax.ppermute(given, 'tp', [(i, i ^ 1) for i in range(tp_count)])]
    all_to_all x1, local copies, waits for them, and re-layouts: 0.66 us -> 2.28 us  [gather_by_exchange(): lax.all_to_all(copies, axis, split_axis=0, concat_axis=concat_axis, tiled...]
    all_to_all x3, starting transfers between devices: 20.6 us -> 22.2 us  [gather_by_exchange(): lax.all_to_all(copies, axis, split_axis=0, concat_axis=concat_axis, tiled...]
    unnamed x33 -> x28, local copies, waits for them, and re-layouts: 6.55 us -> 5.1 us
  transfers between devices with their start and end apart: 3 -> 4, of which waited for: 3 -> 4; matrix products, arithmetic and copies ran while one was open for 6% -> 6% of each run, Pallas kernels for 0% -> 0%
where the time goes in v7:
time: 153 us; the launch traced here: 151 us
  waiting for transfers between devices  60.7 us (40%)
  blocking collectives  28.3 us (18%)
  starting transfers between devices  24.1 us (16%)
  local copies, waits for them, and re-layouts  16.6 us (11%)
  other arithmetic  13.6 us (9%)
  matrix products  6.26 us (4%)
    all_to_all x3, waiting for transfers between devices, gather_by_exchange(): lax.all_to_all(copies, axis, split_axis=0, concat_axis=concat_axis, tiled...  58.9 us
    all_to_all x1, blocking collectives, per_device(): lax.all_to_all(chip_sum, 'tp', split_axis=0, concat_axis=0, axis_index_gr...  28.3 us
    all_to_all x3, starting transfers between devices, gather_by_exchange(): lax.all_to_all(copies, axis, split_axis=0, concat_axis=concat_axis, tiled...  22.2 us
    unnamed x28, local copies, waits for them, and re-layouts  5.1 us
  transfers between devices with their start and end apart: 4, of which 4 were waited for; matrix products, arithmetic and copies ran while one was open for 6% of the time, Pallas kernels for 0%

profile of v7, /device:TPU:6, one launch (start us, length us, event | category | flops | bytes accessed | tf_op | source)
XLA Modules:
  0.0 150.6 jit_solution(11409610264896139303)
XLA Ops:
  0.6 0.9 convert_element_type.103
  1.6 1.3 fusion.91
  2.8 0.7 slice.208
  3.5 0.7 slice_bitcast_fusion.12
  4.9 0.7 broadcast_multiply_fusion.1
  6.0 0.7 broadcast_in_dim.28
  6.8 10.1 %all-to-all-start = ((f32[16,128,26]{1,2,0:T(8,128)}), f32[16,128,26]{1,2,0:T(8,128)S(1)}, u32[]{:S(2)}, u32[]{:S(2)}) async-start(f32[16,128,26]{1,2,0:T(8,128)} %broadcast_in_dim.28), calls=%async_computation | async-start | bytes 524288 | tf_op jit(solution)/shard_map/all_to_all | solution.py:20
  19.0 1.1 convolution_bitcast_fusion
  20.9 0.7 copy.110
  21.6 0.7 slice_bitcast_fusion.16
  22.4 5.1 %all-to-all-done = f32[16,128,26]{1,2,0:T(8,128)S(1)} async-done(((f32[16,128,26]{1,2,0:T(8,128)}), f32[16,128,26]{1,2,0:T(8,128)S(1)}, u32[]{:S(2)}, u32[]{:S(2)}) %all-to-all-start) | async-done | bytes 213024 | tf_op jit(solution)/shard_map/all_to_all | solution.py:20
  27.5 0.8 fusion.82
  28.3 1.3 convert_subtract_fusion
  30.2 0.8 fusion.41
  31.0 1.3 fusion.90
  34.0 0.9 fusion.93
  34.9 1.2 convolution_add_fusion
  37.7 1.9 %collective-permute-start = (bf16[16,128,128]{2,1,0:T(8,128)(2,1)S(1)}, bf16[16,128,128]{2,1,0:T(8,128)(2,1)S(1)}, u32[]{:S(2)}, u32[]{:S(2)}) collective-permute-start(bf16[16,128,128]{2,1,0:T(8,128)(2,1)S(1)} %fusion.15), channel_id=1, source_target_pairs={{0,1},{1,0},{2,3},{3,2},{4,5},{5,4},{6,7},{7,6},{8,9},{9,8},{10,11... | collective-permute-start | bytes 1572872 | tf_op jit(solution)/shard_map/ppermute | solution.py:157
  39.7 1.9 %collective-permute-done = bf16[16,128,128]{2,1,0:T(8,128)(2,1)S(1)} collective-permute-done((bf16[16,128,128]{2,1,0:T(8,128)(2,1)S(1)}, bf16[16,128,128]{2,1,0:T(8,128)(2,1)S(1)}, u32[]{:S(2)}, u32[]{:S(2)}) %collective-permute-start) | collective-permute-done | bytes 524320 | tf_op jit(solution)/shard_map/ppermute | solution.py:157
  41.7 28.3 %all_to_all.24 = bf16[16,128,128]{2,1,0:T(8,128)(2,1)S(1)} all-to-all(bf16[16,128,128]{2,1,0:T(8,128)(2,1)S(1)} %fusion.7), channel_id=1, replica_groups={{0,2,4,6,8,10,12,14,16,18,20,22,24,26,28,30},{1,3,5,7,9,11,13,15,17,19,..., dimensions={0} | all-to-all | bytes 1048576 | tf_op jit(solution)/shard_map/all_to_all | solution.py:160
  70.1 1.3 broadcast_in_dim_broadcast_in_dim.2
  71.4 5.6 %all-to-all-start.2 = ((bf16[32,128,1,128]{3,1,2,0:T(8,128)(2,1)}), bf16[32,128,1,128]{3,1,2,0:T(8,128)(2,1)}, u32[]{:S(2)}, u32[]{:S(2)}) async-start(bf16[32,128,1,128]{3,1,2,0:T(8,128)(2,1)} %broadcast_in_dim_broadcast_in_dim.2), calls=%async_computation.2 | async-start | bytes 2097152 | tf_op jit(solution)/shard_map/all_to_all | solution.py:20
  77.0 3.2 %copy.114 = bf16[4096,3,128]{0,2,1:T(8,128)(2,1)S(1)} copy(bf16[4096,3,128]{2,0,1:T(8,128)(2,1)} %param.15) | data formatting | bytes 6291456 | tf_op args[7]
  80.2 25.8 %all-to-all-done.2 = bf16[32,128,1,128]{3,1,2,0:T(8,128)(2,1)} async-done(((bf16[32,128,1,128]{3,1,2,0:T(8,128)(2,1)}), bf16[32,128,1,128]{3,1,2,0:T(8,128)(2,1)}, u32[]{:S(2)}, u32[]{:S(2)}) %all-to-all-start.2) | async-done | bytes 1048608 | tf_op jit(solution)/shard_map/all_to_all | solution.py:20
  106.0 2.3 %copy.113 = bf16[32,128,1,128]{1,3,0,2:T(8,128)(2,1)} copy(bf16[32,128,1,128]{3,1,2,0:T(8,128)(2,1)} %all-to-all-done.2) | data formatting | bytes 2097152 | tf_op jit(solution)/shard_map/all_to_all | solution.py:20
  108.3 1.8 %fusion.3 = f32[128]{0:T(128)S(1)} fusion(bf16[32,128,1,128]{1,3,0,2:T(8,128)(2,1)} %copy.113), kind=kLoop, calls=%fused_computation.6 | loop fusion | flops 1572736 | bytes 1049088 | tf_op jit(solution)/shard_map/reduce_sum | solution.py:167
  110.1 1.7 %fusion.5 = bf16[32,1,128,1,128]{2,4,0,3,1:T(8,128)(2,1)S(1)} fusion(bf16[32,128,1,128]{1,3,0,2:T(8,128)(2,1)} %copy.113, f32[32,128]{1,0:T(8,128)S(1)} %bitcast.150, f32[128]{0:T(128)S(1)} %add_rsqrt_fusion), kind=kLoop, calls=%fused_computation.8 | loop fusion | flops 2097152 | bytes 2114048 | tf_op jit(solution)/shard_map/convert_element_type | solution.py:168
  111.9 1.0 fusion
  113.2 1.1 broadcast_in_dim.35
  114.3 6.5 %all-to-all-start.3 = ((bf16[16,128,256]{2,1,0:T(8,128)(2,1)}), bf16[16,128,256]{2,1,0:T(8,128)(2,1)S(1)}, u32[]{:S(2)}, u32[]{:S(2)}) async-start(bf16[16,128,256]{2,1,0:T(8,128)(2,1)} %broadcast_in_dim.35), calls=%async_computation.3 | async-start | bytes 2097152 | tf_op jit(solution)/shard_map/all_to_all | solution.py:20
  120.8 28.0 %all-to-all-done.3 = bf16[16,128,256]{2,1,0:T(8,128)(2,1)S(1)} async-done(((bf16[16,128,256]{2,1,0:T(8,128)(2,1)}), bf16[16,128,256]{2,1,0:T(8,128)(2,1)S(1)}, u32[]{:S(2)}, u32[]{:S(2)}) %all-to-all-start.3) | async-done | bytes 1048608 | tf_op jit(solution)/shard_map/all_to_all | solution.py:20
  149.6 1.0 fusion.6
  (89 shorter events, 9.2 us)
Async XLA Ops:
  4.3 0.6 copy-start.4
  4.3 0.6 copy-start.5
  4.3 1.3 copy-start.6
  4.8 1.9 %copy-start.1 = (bf16[128,128]{0,1:T(8,128)(2,1)}, bf16[128,128]{0,1:T(8,128)(2,1)S(1)}, u32[]{:S(2)}) copy-start(bf16[128,128]{0,1:T(8,128)(2,1)S(1)} %fusion.98) | copy-start | bytes 98308
  6.0 14.9 %copy-start = (bf16[128,4096]{1,0:T(8,128)(2,1)S(1)}, bf16[128,4096]{1,0:T(8,128)(2,1)}, u32[]{:S(2)}) copy-start(bf16[128,4096]{1,0:T(8,128)(2,1)} %param.13) | copy-start | bytes 3145732
  6.8 20.6 %all-to-all-start = ((f32[16,128,26]{1,2,0:T(8,128)}), f32[16,128,26]{1,2,0:T(8,128)S(1)}, u32[]{:S(2)}, u32[]{:S(2)}) async-start(f32[16,128,26]{1,2,0:T(8,128)} %broadcast_in_dim.28), calls=%async_computation | async-start | bytes 524288 | tf_op jit(solution)/shard_map/all_to_all | solution.py:20
  34.0 2.4 %copy-start.8 = (f32[128,16]{0,1:T(8,128)S(1)}, f32[128,16]{0,1:T(8,128)}, u32[]{:S(2)}) copy-start(f32[128,16]{0,1:T(8,128)} %get-tuple-element.4) | copy-start | bytes 24580
  34.0 3.0 %copy-start.10 = (f32[2,128]{1,0:T(2,128)S(1)}, f32[2,128]{1,0:T(2,128)}, u32[]{:S(2)}) copy-start(f32[2,128]{1,0:T(2,128)} %convert_subtract_fusion) | copy-start | bytes 3076
  34.0 3.0 %copy-start.9 = (f32[2,128]{1,0:T(2,128)S(1)}, f32[2,128]{1,0:T(2,128)}, u32[]{:S(2)}) copy-start(f32[2,128]{1,0:T(2,128)} %slice_bitcast_fusion.13) | copy-start | bytes 3076
  37.7 32.4 %copy-start.3 = (bf16[128,128]{1,0:T(8,128)(2,1)S(1)}, bf16[128,128]{1,0:T(8,128)(2,1)}, u32[]{:S(2)}) copy-start(bf16[128,128]{1,0:T(8,128)(2,1)} %param.8) | copy-start | bytes 98308
  37.7 3.8 %collective-permute-start = (bf16[16,128,128]{2,1,0:T(8,128)(2,1)S(1)}, bf16[16,128,128]{2,1,0:T(8,128)(2,1)S(1)}, u32[]{:S(2)}, u32[]{:S(2)}) collective-permute-start(bf16[16,128,128]{2,1,0:T(8,128)(2,1)S(1)} %fusion.15), channel_id=1, source_target_pairs={{0,1},{1,0},{2,3},{3,2},{4,5},{5,4},{6,7},{7,6},{8,9},{9,8},{10,11... | collective-permute-start | bytes 1572872 | tf_op jit(solution)/shard_map/ppermute | solution.py:157
  70.1 10.1 %copy-start.2 = (bf16[128,128]{1,0:T(8,128)(2,1)}, bf16[128,128]{1,0:T(8,128)(2,1)S(1)}, u32[]{:S(2)}) copy-start(bf16[128,128]{1,0:T(8,128)(2,1)S(1)} %add_convert_fusion) | copy-start | bytes 98308
  71.4 34.6 %all-to-all-start.2 = ((bf16[32,128,1,128]{3,1,2,0:T(8,128)(2,1)}), bf16[32,128,1,128]{3,1,2,0:T(8,128)(2,1)}, u32[]{:S(2)}, u32[]{:S(2)}) async-start(bf16[32,128,1,128]{3,1,2,0:T(8,128)(2,1)} %broadcast_in_dim_broadcast_in_dim.2), calls=%async_computation.2 | async-start | bytes 2097152 | tf_op jit(solution)/shard_map/all_to_all | solution.py:20
  80.2 29.9 %copy-start.7 = (f32[4096]{0:T(1024)S(1)}, f32[4096]{0:T(1024)}, u32[]{:S(2)}) copy-start(f32[4096]{0:T(1024)} %param.14) | copy-start | bytes 49156
  114.3 34.5 %all-to-all-start.3 = ((bf16[16,128,256]{2,1,0:T(8,128)(2,1)}), bf16[16,128,256]{2,1,0:T(8,128)(2,1)S(1)}, u32[]{:S(2)}, u32[]{:S(2)}) async-start(bf16[16,128,256]{2,1,0:T(8,128)(2,1)} %broadcast_in_dim.35), calls=%async_computation.3 | async-start | bytes 2097152 | tf_op jit(solution)/shard_map/all_to_all | solution.py:20

commit v8 on v7

--- a/solution.py
+++ b/solution.py
@@ -162,13 +162,16 @@
     )
     own_share = jnp.sum(received.astype(jnp.float32), axis=0)
     hyena_out = (resid_in.astype(jnp.float32) + own_share).astype(jnp.bfloat16)
-    full_rows = gather_by_exchange(hyena_out, "tp").reshape(row_count, width_all)
-    wide = full_rows.astype(jnp.float32)
-    mean_square = jnp.mean(wide * wide, axis=1, keepdims=True)
-    normed = (wide * lax.rsqrt(mean_square + eps_norm) * norm_gain).astype(jnp.bfloat16)
-    projected = jnp.dot(
-        normed, attn_weight.reshape(width_all, 3 * chan_count), preferred_element_type=jnp.float32
-    ).reshape(row_count, 3, chan_count)
+    wide = gather_by_exchange(hyena_out, "tp", concat_axis=0).astype(jnp.float32)
+    mean_square = jnp.sum(wide * wide, axis=(0, 2), keepdims=True) / width_all
+    gain_blocks = norm_gain.reshape(tp_count, 1, chan_count)
+    normed = (wide * lax.rsqrt(mean_square + eps_norm) * gain_blocks).astype(jnp.bfloat16)
+    projected = jnp.einsum(
+        "jtc,jcpd->tpd",
+        normed,
+        attn_weight.reshape(tp_count, chan_count, 3, chan_count),
+        preferred_element_type=jnp.float32,
+    )
     head_count = chan_count // HEAD_DIM
     first_pos = ctx_index * row_count
     positions = first_pos + jnp.arange(row_count, dtype=jnp.int32)

time: 153 us -> 181 us (1.18)
  local copies, waits for them, and re-layouts: 16.6 us -> 33.6 us
  matrix products: 6.26 us -> 15.9 us
  starting transfers between devices: 24.1 us -> 27.2 us
  waiting for transfers between devices: 60.7 us -> 58.7 us
    all_to_all x3, starting transfers between devices: 22.2 us -> 25.3 us  [gather_by_exchange(): lax.all_to_all(copies, axis, split_axis=0, concat_axis=concat_axis, tiled...]
    another operation x2, local copies, waits for them, and re-layouts: 0.07 us -> 3.11 us  [toeplitz_lower(): tiled = jnp.tile(flipped, (1, block_size))]
    rev x2, local copies, waits for them, and re-layouts: 0.16 us -> 3.07 us  [toeplitz_lower(): flipped = padded[:, ::-1]]
    all_to_all x1 -> x0, local copies, waits for them, and re-layouts: 2.28 us -> none  [gather_by_exchange(): lax.all_to_all(copies, axis, split_axis=0, concat_axis=concat_axis, tiled...]
    unnamed x28 -> x49, local copies, waits for them, and re-layouts: 5.1 us -> 7.34 us
    all_to_all x3, waiting for transfers between devices: 58.9 us -> 56.8 us  [gather_by_exchange(): lax.all_to_all(copies, axis, split_axis=0, concat_axis=concat_axis, tiled...]
    dot_general x1, matrix products: 1.24 us -> 3.14 us  [modal_conv(): jnp.einsum('cnm,cmi->cni', states * weight[:, None, :], powers, precision...]
  transfers between devices with their start and end apart: 4 -> 4, of which waited for: 4 -> 3; matrix products, arithmetic and copies ran while one was open for 6% -> 9% of each run, Pallas kernels for 0% -> 0%
where the time goes in v8:
time: 181 us; the launch traced here: 178 us
  waiting for transfers between devices  58.7 us (32%)
  local copies, waits for them, and re-layouts  33.6 us (19%)
  blocking collectives  28.3 us (16%)
  starting transfers between devices  27.2 us (15%)
  matrix products  15.9 us (9%)
  other arithmetic  13 us (7%)
    all_to_all x3, waiting for transfers between devices, gather_by_exchange(): lax.all_to_all(copies, axis, split_axis=0, concat_axis=concat_axis, tiled...  56.8 us
    all_to_all x1, blocking collectives, per_device(): lax.all_to_all(chip_sum, 'tp', split_axis=0, concat_axis=0, axis_index_gr...  28.3 us
    all_to_all x3, starting transfers between devices, gather_by_exchange(): lax.all_to_all(copies, axis, split_axis=0, concat_axis=concat_axis, tiled...  25.3 us
    unnamed x49, local copies, waits for them, and re-layouts  7.34 us
  transfers between devices with their start and end apart: 4, of which 3 were waited for; matrix products, arithmetic and copies ran while one was open for 9% of the time, Pallas kernels for 0%

profile of v8, /device:TPU:6, one launch (start us, length us, event | category | flops | bytes accessed | tf_op | source)
XLA Modules:
  0.0 177.8 jit_solution(4392611151374156830)
XLA Ops:
  1.7 1.3 fusion.93
  7.9 10.1 %all-to-all-start = ((f32[16,128,26]{1,2,0:T(8,128)}), f32[16,128,26]{1,2,0:T(8,128)}, u32[]{:S(2)}, u32[]{:S(2)}) async-start(f32[16,128,26]{1,2,0:T(8,128)} %broadcast_in_dim.30), calls=%async_computation | async-start | bytes 524288 | tf_op jit(solution)/shard_map/all_to_all | solution.py:20
  22.1 2.8 %convolution_bitcast_fusion = f32[128,16,8]{1,2,0:T(8,128)} fusion(bf16[128,8,16]{2,1,0:T(8,128)(2,1)} %copy.83, f32[16]{0:T(128)S(1)} %iota_subtract_fusion.2, f32[128,16]{1,0:T(8,128)S(1)} %copy.80), kind=kOutput, calls=%fused_computation.8 | convolution fusion | flops 3178496 | bytes 106560 | tf_op jit(solution)/shard_map/cnj,cmj->cnm/dot_general | solution.py:47
  24.9 1.2 copy.115
  26.8 1.6 multiply_reduce_fusion.3
  28.5 1.9 %copy.106 = f32[128,16,8]{1,2,0:T(8,128)} copy(f32[128,16,8]{0,2,1:T(8,128)} %multiply_reduce_fusion.3) | data formatting | bytes 131072 | tf_op jit(solution)/shard_map/cmnk,ckm->cnm/dot_general | solution.py:54
  30.4 2.2 %copy.89 = bf16[128,4096]{0,1:T(8,128)(2,1)} copy(bf16[128,4096]{1,0:T(8,128)(2,1)} %param.13) | data formatting | bytes 2097152 | tf_op args[5]
  37.4 1.3 fusion.92
  40.2 1.5 rev.3
  41.7 1.5 copy.81
  43.2 1.4 tile.4
  44.7 1.7 tile.10
  46.3 1.7 slice.214
  48.0 1.7 reshape.280
  49.7 1.6 slice.215
  51.2 2.3 %copy.110 = f32[128,16,16]{2,1,0:T(8,128)} copy(f32[128,16,16]{0,2,1:T(8,128)} %slice.215) | data formatting | bytes 262144
  53.5 2.2 %fusion.95 = f32[128,8,16]{2,1,0:T(8,128)S(1)} fusion(bf16[128,8,16]{2,1,0:T(8,128)(2,1)S(1)} %copy-done.3, f32[128,16,16]{2,1,0:T(8,128)} %copy.110), kind=kOutput, calls=%fused_computation.161 | convolution fusion | flops 3145728 | bytes 229376 | tf_op jit(solution)/shard_map/cij,cnj->cni/dot_general | solution.py:45
  55.8 3.1 %convolution_add_fusion = f32[128,8,16]{2,1,0:T(8,128)} fusion(f32[128,8,16]{2,1,0:T(8,128)S(1)} %fusion.95, f32[128,16,8]{1,2,0:T(8,128)} %copy.106, f32[128,16]{1,0:T(8,128)S(1)} %copy.80, f32[128,16]{1,0:T(8,128)S(1)} %copy.79, f32[128,16]{1,0:T(8,128)} %copy.85), kind=kOutput, calls=%fused_computation.7 | convolution fusion | flops 3260416 | bytes 221184 | tf_op jit(solution)/shard_map/cnm,cmi->cni/dot_general | solution.py:60
  58.9 1.2 copy.87
  60.7 1.3 fusion.21
  62.5 1.9 %collective-permute-start = (bf16[16,128,128]{2,1,0:T(8,128)(2,1)S(1)}, bf16[16,128,128]{2,1,0:T(8,128)(2,1)S(1)}, u32[]{:S(2)}, u32[]{:S(2)}) collective-permute-start(bf16[16,128,128]{2,1,0:T(8,128)(2,1)S(1)} %fusion.17), channel_id=1, source_target_pairs={{0,1},{1,0},{2,3},{3,2},{4,5},{5,4},{6,7},{7,6},{8,9},{9,8},{10,11... | collective-permute-start | bytes 1572872 | tf_op jit(solution)/shard_map/ppermute | solution.py:157
  64.5 1.9 %collective-permute-done = bf16[16,128,128]{2,1,0:T(8,128)(2,1)S(1)} collective-permute-done((bf16[16,128,128]{2,1,0:T(8,128)(2,1)S(1)}, bf16[16,128,128]{2,1,0:T(8,128)(2,1)S(1)}, u32[]{:S(2)}, u32[]{:S(2)}) %collective-permute-start) | collective-permute-done | bytes 524320 | tf_op jit(solution)/shard_map/ppermute | solution.py:157
  66.5 28.3 %all_to_all.20 = bf16[16,128,128]{2,1,0:T(8,128)(2,1)S(1)} all-to-all(bf16[16,128,128]{2,1,0:T(8,128)(2,1)S(1)} %fusion.7), channel_id=1, replica_groups={{0,2,4,6,8,10,12,14,16,18,20,22,24,26,28,30},{1,3,5,7,9,11,13,15,17,19,..., dimensions={0} | all-to-all | bytes 1048576 | tf_op jit(solution)/shard_map/all_to_all | solution.py:160
  94.9 1.3 broadcast_in_dim.37
  96.2 5.6 %all-to-all-start.2 = ((bf16[32,128,128]{2,1,0:T(8,128)(2,1)}), bf16[32,128,128]{2,1,0:T(8,128)(2,1)}, u32[]{:S(2)}, u32[]{:S(2)}) async-start(bf16[32,128,128]{2,1,0:T(8,128)(2,1)} %broadcast_in_dim.37), calls=%async_computation.2 | async-start | bytes 2097152 | tf_op jit(solution)/shard_map/all_to_all | solution.py:20
  101.8 29.0 %all-to-all-done.2 = bf16[32,128,128]{2,1,0:T(8,128)(2,1)} async-done(((bf16[32,128,128]{2,1,0:T(8,128)(2,1)}), bf16[32,128,128]{2,1,0:T(8,128)(2,1)}, u32[]{:S(2)}, u32[]{:S(2)}) %all-to-all-start.2) | async-done | bytes 1048608 | tf_op jit(solution)/shard_map/all_to_all | solution.py:20
  130.9 1.5 fusion.1
  132.4 2.6 %convolution_bitcast_fusion.1 = f32[128,3,128]{0,2,1:T(8,128)S(1)} fusion(bf16[32,128,3,128]{3,1,0,2:T(8,128)(2,1)S(1)} %bitcast.132, bf16[32,128,128]{2,1,0:T(8,128)(2,1)} %all-to-all-done.2, f32[32,128]{1,0:T(8,128)S(1)} %bitcast.143, f32[128]{0:T(128)S(1)} %add_rsqrt_fusion), kind=kOutput, calls=%fused_computation.9 | convolution fusion | flops 404750336 | bytes 4407808 | tf_op jit(solution)/shard_map/jtc,jcpd->tpd/dot_general | solution.py:169
  136.5 9.6 %all-to-all-start.3 = ((bf16[16,128,256]{2,1,0:T(8,128)(2,1)}), bf16[16,128,256]{2,1,0:T(8,128)(2,1)}, u32[]{:S(2)}, u32[]{:S(2)}) async-start(bf16[16,128,256]{2,1,0:T(8,128)(2,1)} %broadcast_in_dim.38), calls=%async_computation.3 | async-start | bytes 2097152 | tf_op jit(solution)/shard_map/all_to_all | solution.py:20
  146.2 27.8 %all-to-all-done.3 = bf16[16,128,256]{2,1,0:T(8,128)(2,1)} async-done(((bf16[16,128,256]{2,1,0:T(8,128)(2,1)}), bf16[16,128,256]{2,1,0:T(8,128)(2,1)}, u32[]{:S(2)}, u32[]{:S(2)}) %all-to-all-start.3) | async-done | bytes 1048608 | tf_op jit(solution)/shard_map/all_to_all | solution.py:20
  173.9 1.5 fusion.94
  175.7 2.0 %fusion.4 = bf16[128,128]{1,0:T(8,128)(2,1)} fusion(f32[128,2048]{1,0:T(8,128)S(1)} %get-tuple-element.28, bf16[2048,256]{1,0:T(8,128)(2,1)} %bitcast.55, f32[128]{0:T(128)S(1)} %get-tuple-element.27, s32[128]{0:T(128)S(1)} %iota_add_fusion, f32[128]{0:T(128)S(1)} %fusion.14), kind=kOutput, calls=%fused_computation.11 | convolution fusion | flops 68190208 | bytes 1607168 | tf_op jit(solution)/shard_map/hsk,khd->hsd/dot_general | solution.py:200
  (108 shorter events, 20.0 us)
Async XLA Ops:
  0.6 131.8 %copy-start = (bf16[4096,3,128]{2,0,1:T(8,128)(2,1)S(1)}, bf16[4096,3,128]{2,0,1:T(8,128)(2,1)}, u32[]{:S(2)}) copy-start(bf16[4096,3,128]{2,0,1:T(8,128)(2,1)} %param.15) | copy-start | bytes 9437188
  4.4 0.6 copy-start.8
  4.4 0.6 copy-start.10
  4.4 1.3 copy-start.12
  6.0 1.0 copy-start.2
  7.9 25.3 %all-to-all-start = ((f32[16,128,26]{1,2,0:T(8,128)}), f32[16,128,26]{1,2,0:T(8,128)}, u32[]{:S(2)}, u32[]{:S(2)}) async-start(f32[16,128,26]{1,2,0:T(8,128)} %broadcast_in_dim.30), calls=%async_computation | async-start | bytes 524288 | tf_op jit(solution)/shard_map/all_to_all | solution.py:20
  26.1 11.3 %copy-start.6 = (f32[128,16]{0,1:T(8,128)S(1)}, f32[128,16]{0,1:T(8,128)}, u32[]{:S(2)}) copy-start(f32[128,16]{0,1:T(8,128)} %param.12) | copy-start | bytes 24580
  28.5 4.2 %copy-start.14 = (f32[3,3,128]{2,1,0:T(4,128)S(1)}, f32[3,3,128]{2,1,0:T(4,128)}, u32[]{:S(2)}) copy-start(f32[3,3,128]{2,1,0:T(4,128)} %param.10) | copy-start | bytes 13828
  28.5 5.8 %copy-start.9 = (f32[3,128]{1,0:T(4,128)S(1)}, f32[3,128]{1,0:T(4,128)}, u32[]{:S(2)}) copy-start(f32[3,128]{1,0:T(4,128)} %copy-done.8) | copy-start | bytes 4612
  28.5 5.8 %copy-start.11 = (f32[3,128]{1,0:T(4,128)S(1)}, f32[3,128]{1,0:T(4,128)}, u32[]{:S(2)}) copy-start(f32[3,128]{1,0:T(4,128)} %copy-done.10) | copy-start | bytes 4612
  28.5 5.8 %copy-start.13 = (f32[3,128]{1,0:T(4,128)S(1)}, f32[3,128]{1,0:T(4,128)}, u32[]{:S(2)}) copy-start(f32[3,128]{1,0:T(4,128)} %copy-done.12) | copy-start | bytes 4612
  28.5 5.8 %copy-start.15 = (f32[2,3,128]{2,0,1:T(2,128)S(1)}, f32[2,3,128]{2,0,1:T(2,128)}, u32[]{:S(2)}) copy-start(f32[2,3,128]{2,0,1:T(2,128)} %get-tuple-element.13) | copy-start | bytes 9220
  28.5 7.8 %copy-start.19 = (f32[16]{0:T(128)S(1)}, f32[16]{0:T(128)}, u32[]{:S(2)}) copy-start(f32[16]{0:T(128)} %fusion.86) | copy-start | bytes 196
  28.5 7.8 %copy-start.20 = (pred[16]{0:T(512)(128)(4,1)S(1)}, pred[16]{0:T(512)(128)(4,1)}, u32[]{:S(2)}) copy-start(pred[16]{0:T(512)(128)(4,1)} %fusion.87) | copy-start | bytes 52
  36.3 17.3 %copy-start.3 = (bf16[128,8,16]{2,1,0:T(8,128)(2,1)S(1)}, bf16[128,8,16]{2,1,0:T(8,128)(2,1)}, u32[]{:S(2)}) copy-start(bf16[128,8,16]{2,1,0:T(8,128)(2,1)} %copy.83) | copy-start | bytes 98308
  55.7 4.4 %copy-start.16 = (f32[128,16]{0,1:T(8,128)S(1)}, f32[128,16]{0,1:T(8,128)}, u32[]{:S(2)}) copy-start(f32[128,16]{0,1:T(8,128)} %get-tuple-element.4) | copy-start | bytes 24580
  55.7 4.9 %copy-start.18 = (f32[2,128]{1,0:T(2,128)S(1)}, f32[2,128]{1,0:T(2,128)}, u32[]{:S(2)}) copy-start(f32[2,128]{1,0:T(2,128)} %convert_subtract_fusion) | copy-start | bytes 3076
  55.7 5.0 %copy-start.4 = (f32[126,128]{1,0:T(8,128)S(1)}, f32[126,128]{1,0:T(8,128)}, u32[]{:S(2)}) copy-start(f32[126,128]{1,0:T(8,128)} %slice_bitcast_fusion.5) | copy-start | bytes 193540
  55.7 5.0 %copy-start.17 = (f32[2,128]{1,0:T(2,128)S(1)}, f32[2,128]{1,0:T(2,128)}, u32[]{:S(2)}) copy-start(f32[2,128]{1,0:T(2,128)} %slice_bitcast_fusion.13) | copy-start | bytes 3076
  60.1 2.0 %copy-start.1 = (bf16[128,4096]{0,1:T(8,128)(2,1)S(1)}, bf16[128,4096]{0,1:T(8,128)(2,1)}, u32[]{:S(2)}) copy-start(bf16[128,4096]{0,1:T(8,128)(2,1)} %copy.89) | copy-start | bytes 3145732
  62.5 32.4 %copy-start.7 = (bf16[128,128]{1,0:T(8,128)(2,1)S(1)}, bf16[128,128]{1,0:T(8,128)(2,1)}, u32[]{:S(2)}) copy-start(bf16[128,128]{1,0:T(8,128)(2,1)} %param.8) | copy-start | bytes 98308
  62.5 3.8 %collective-permute-start = (bf16[16,128,128]{2,1,0:T(8,128)(2,1)S(1)}, bf16[16,128,128]{2,1,0:T(8,128)(2,1)S(1)}, u32[]{:S(2)}, u32[]{:S(2)}) collective-permute-start(bf16[16,128,128]{2,1,0:T(8,128)(2,1)S(1)} %fusion.17), channel_id=1, source_target_pairs={{0,1},{1,0},{2,3},{3,2},{4,5},{5,4},{6,7},{7,6},{8,9},{9,8},{10,11... | collective-permute-start | bytes 1572872 | tf_op jit(solution)/shard_map/ppermute | solution.py:157
  94.9 37.5 %copy-start.5 = (bf16[128,128]{1,0:T(8,128)(2,1)}, bf16[128,128]{1,0:T(8,128)(2,1)S(1)}, u32[]{:S(2)}) copy-start(bf16[128,128]{1,0:T(8,128)(2,1)S(1)} %add_convert_fusion) | copy-start | bytes 98308
  94.9 37.5 %copy-start.21 = (f32[4096]{0:T(1024)S(1)}, f32[4096]{0:T(1024)}, u32[]{:S(2)}) copy-start(f32[4096]{0:T(1024)} %param.14) | copy-start | bytes 49156
  96.2 34.7 %all-to-all-start.2 = ((bf16[32,128,128]{2,1,0:T(8,128)(2,1)}), bf16[32,128,128]{2,1,0:T(8,128)(2,1)}, u32[]{:S(2)}, u32[]{:S(2)}) async-start(bf16[32,128,128]{2,1,0:T(8,128)(2,1)} %broadcast_in_dim.37), calls=%async_computation.2 | async-start | bytes 2097152 | tf_op jit(solution)/shard_map/all_to_all | solution.py:20
  136.5 37.4 %all-to-all-start.3 = ((bf16[16,128,256]{2,1,0:T(8,128)(2,1)}), bf16[16,128,256]{2,1,0:T(8,128)(2,1)}, u32[]{:S(2)}, u32[]{:S(2)}) async-start(bf16[16,128,256]{2,1,0:T(8,128)(2,1)} %broadcast_in_dim.38), calls=%async_computation.3 | async-start | bytes 2097152 | tf_op jit(solution)/shard_map/all_to_all | solution.py:20

commit v9 on v7

--- a/solution.py
+++ b/solution.py
@@ -99,33 +99,33 @@
         "ct,cmt->cm", blind_product[:, 2:], tail_powers[:, :, 2:], precision=highest
     )
     mode_count = late_state.shape[1]
-    head_rows = feats_wide[:2, 1:, :].reshape(4, chan_count).T
-    tail_rows = feats_wide[-2:].reshape(6, chan_count).T
-    payload = jnp.concatenate([late_state, head_rows, tail_rows], axis=1)
+    head_rows = feats_wide[:2, 1:, :].reshape(4, chan_count)
+    tail_rows = feats_wide[-2:].reshape(6, chan_count)
+    payload = jnp.concatenate([late_state.T, head_rows, tail_rows], axis=0)
     received = gather_by_exchange(payload, "ctx", concat_axis=0)
-    late_all = received[:, :, :mode_count]
-    head_all = received[:, :, mode_count : mode_count + 4].reshape(ctx_count, chan_count, 2, 2)
-    head_all = head_all.transpose(0, 2, 3, 1)
-    tail_all = received[:, :, mode_count + 4 :].reshape(ctx_count, chan_count, 2, 3)
-    tail_all = tail_all.transpose(0, 2, 3, 1)
+    late_all = received[:, :mode_count]
+    head_all = received[:, mode_count : mode_count + 4].reshape(ctx_count, 2, 2, chan_count)
+    tail_all = received[:, mode_count + 4 :].reshape(ctx_count, 2, 3, chan_count)
     prev_tail = jnp.concatenate([jnp.zeros_like(tail_all[:1]), tail_all[:-1]], axis=0)
     edge_joined = jnp.concatenate([prev_tail[:, :, 1:], head_all], axis=1)
     taps = short_filter[:, 1:, :]
     edge_short = taps[0] * edge_joined[:, 2:] + taps[1] * edge_joined[:, 1:3] + taps[2] * edge_joined[:, :2]
     edge_product = (edge_short[:, :, 0] * edge_short[:, :, 1]).astype(jnp.bfloat16).astype(jnp.float32)
+    first_powers = tail_powers[:, :, 0].T
+    second_powers = tail_powers[:, :, 1].T
     gathered_states = (
         late_all
-        + edge_product[:, 0, :, None] * tail_powers[None, :, :, 0]
-        + edge_product[:, 1, :, None] * tail_powers[None, :, :, 1]
+        + edge_product[:, 0:1, :] * first_powers[None]
+        + edge_product[:, 1:2, :] * second_powers[None]
     )
     shard_steps = jnp.arange(ctx_count, dtype=jnp.float32)
     gap_count = ctx_index.astype(jnp.float32) - 1.0 - shard_steps
     decay = jnp.where(
         (gap_count >= 0.0)[:, None, None],
-        jnp.exp(-rates[None] * row_count * jnp.maximum(gap_count, 0.0)[:, None, None]),
+        jnp.exp(-rates.T[None] * row_count * jnp.maximum(gap_count, 0.0)[:, None, None]),
         0.0,
     )
-    start_state = jnp.sum(decay * gathered_states, axis=0)
+    start_state = jnp.sum(decay * gathered_states, axis=0).T
     conv_blind = modal_conv(
         blind_product, residues, rates, jnp.zeros_like(rates), block_limit=16
     )

time: 153 us -> 153 us (level)
  no operation moved by 1% of the time
where the time goes in v9:
time: 153 us; the launch traced here: 151 us
  waiting for transfers between devices  60.7 us (40%)
  blocking collectives  28.3 us (18%)
  starting transfers between devices  24.1 us (16%)
  local copies, waits for them, and re-layouts  16.6 us (11%)
  other arithmetic  13.6 us (9%)
  matrix products  6.26 us (4%)
    all_to_all x3, waiting for transfers between devices, gather_by_exchange(): lax.all_to_all(copies, axis, split_axis=0, concat_axis=concat_axis, tiled...  58.9 us
    all_to_all x1, blocking collectives, per_device(): lax.all_to_all(chip_sum, 'tp', split_axis=0, concat_axis=0, axis_index_gr...  28.3 us
    all_to_all x3, starting transfers between devices, gather_by_exchange(): lax.all_to_all(copies, axis, split_axis=0, concat_axis=concat_axis, tiled...  22.2 us
    unnamed x28, local copies, waits for them, and re-layouts  5.1 us
  transfers between devices with their start and end apart: 4, of which 4 were waited for; matrix products, arithmetic and copies ran while one was open for 6% of the time, Pallas kernels for 0%

profile of v9, /device:TPU:6, one launch (start us, length us, event | category | flops | bytes accessed | tf_op | source)
XLA Modules:
  0.0 150.6 jit_solution(17212802934546862645)
XLA Ops:
  0.6 0.9 convert_element_type.103
  1.6 1.3 fusion.90
  2.8 0.7 slice.210
  3.5 0.7 slice_bitcast_fusion.12
  4.9 0.7 broadcast_multiply_fusion
  6.0 0.7 broadcast_in_dim.28
  6.8 10.1 %all-to-all-start = ((f32[16,26,128]{2,1,0:T(8,128)}), f32[16,26,128]{2,1,0:T(8,128)S(1)}, u32[]{:S(2)}, u32[]{:S(2)}) async-start(f32[16,26,128]{2,1,0:T(8,128)} %broadcast_in_dim.28), calls=%async_computation | async-start | bytes 524288 | tf_op jit(solution)/shard_map/all_to_all | solution.py:20
  19.0 1.1 convolution_bitcast_fusion
  20.9 0.7 copy.112
  21.6 0.7 slice_bitcast_fusion.16
  22.4 5.1 %all-to-all-done = f32[16,26,128]{2,1,0:T(8,128)S(1)} async-done(((f32[16,26,128]{2,1,0:T(8,128)}), f32[16,26,128]{2,1,0:T(8,128)S(1)}, u32[]{:S(2)}, u32[]{:S(2)}) %all-to-all-start) | async-done | bytes 213024 | tf_op jit(solution)/shard_map/all_to_all | solution.py:20
  27.5 0.8 fusion.82
  28.3 1.3 convert_subtract_fusion
  30.2 0.8 fusion.41
  31.0 1.3 bitcast_multiply_fusion
  34.0 0.9 fusion.92
  34.9 1.2 convolution_add_fusion
  37.7 1.9 %collective-permute-start = (bf16[16,128,128]{2,1,0:T(8,128)(2,1)S(1)}, bf16[16,128,128]{2,1,0:T(8,128)(2,1)S(1)}, u32[]{:S(2)}, u32[]{:S(2)}) collective-permute-start(bf16[16,128,128]{2,1,0:T(8,128)(2,1)S(1)} %fusion.15), channel_id=1, source_target_pairs={{0,1},{1,0},{2,3},{3,2},{4,5},{5,4},{6,7},{7,6},{8,9},{9,8},{10,11... | collective-permute-start | bytes 1572872 | tf_op jit(solution)/shard_map/ppermute | solution.py:157
  39.7 1.9 %collective-permute-done = bf16[16,128,128]{2,1,0:T(8,128)(2,1)S(1)} collective-permute-done((bf16[16,128,128]{2,1,0:T(8,128)(2,1)S(1)}, bf16[16,128,128]{2,1,0:T(8,128)(2,1)S(1)}, u32[]{:S(2)}, u32[]{:S(2)}) %collective-permute-start) | collective-permute-done | bytes 524320 | tf_op jit(solution)/shard_map/ppermute | solution.py:157
  41.7 28.3 %all_to_all.24 = bf16[16,128,128]{2,1,0:T(8,128)(2,1)S(1)} all-to-all(bf16[16,128,128]{2,1,0:T(8,128)(2,1)S(1)} %fusion.7), channel_id=1, replica_groups={{0,2,4,6,8,10,12,14,16,18,20,22,24,26,28,30},{1,3,5,7,9,11,13,15,17,19,..., dimensions={0} | all-to-all | bytes 1048576 | tf_op jit(solution)/shard_map/all_to_all | solution.py:160
  70.1 1.3 broadcast_in_dim_broadcast_in_dim.2
  71.4 5.6 %all-to-all-start.2 = ((bf16[32,128,1,128]{3,1,2,0:T(8,128)(2,1)}), bf16[32,128,1,128]{3,1,2,0:T(8,128)(2,1)}, u32[]{:S(2)}, u32[]{:S(2)}) async-start(bf16[32,128,1,128]{3,1,2,0:T(8,128)(2,1)} %broadcast_in_dim_broadcast_in_dim.2), calls=%async_computation.2 | async-start | bytes 2097152 | tf_op jit(solution)/shard_map/all_to_all | solution.py:20
  77.0 3.2 %copy.116 = bf16[4096,3,128]{0,2,1:T(8,128)(2,1)S(1)} copy(bf16[4096,3,128]{2,0,1:T(8,128)(2,1)} %param.15) | data formatting | bytes 6291456 | tf_op args[7]
  80.2 25.8 %all-to-all-done.2 = bf16[32,128,1,128]{3,1,2,0:T(8,128)(2,1)} async-done(((bf16[32,128,1,128]{3,1,2,0:T(8,128)(2,1)}), bf16[32,128,1,128]{3,1,2,0:T(8,128)(2,1)}, u32[]{:S(2)}, u32[]{:S(2)}) %all-to-all-start.2) | async-done | bytes 1048608 | tf_op jit(solution)/shard_map/all_to_all | solution.py:20
  106.0 2.3 %copy.115 = bf16[32,128,1,128]{1,3,0,2:T(8,128)(2,1)} copy(bf16[32,128,1,128]{3,1,2,0:T(8,128)(2,1)} %all-to-all-done.2) | data formatting | bytes 2097152 | tf_op jit(solution)/shard_map/all_to_all | solution.py:20
  108.3 1.8 %fusion.3 = f32[128]{0:T(128)S(1)} fusion(bf16[32,128,1,128]{1,3,0,2:T(8,128)(2,1)} %copy.115), kind=kLoop, calls=%fused_computation.6 | loop fusion | flops 1572736 | bytes 1049088 | tf_op jit(solution)/shard_map/reduce_sum | solution.py:167
  110.1 1.7 %fusion.5 = bf16[32,1,128,1,128]{2,4,0,3,1:T(8,128)(2,1)S(1)} fusion(bf16[32,128,1,128]{1,3,0,2:T(8,128)(2,1)} %copy.115, f32[32,128]{1,0:T(8,128)S(1)} %bitcast.152, f32[128]{0:T(128)S(1)} %add_rsqrt_fusion), kind=kLoop, calls=%fused_computation.8 | loop fusion | flops 2097152 | bytes 2114048 | tf_op jit(solution)/shard_map/convert_element_type | solution.py:168
  111.9 1.0 fusion
  113.2 1.1 broadcast_in_dim.33
  114.3 6.5 %all-to-all-start.3 = ((bf16[16,128,256]{2,1,0:T(8,128)(2,1)}), bf16[16,128,256]{2,1,0:T(8,128)(2,1)S(1)}, u32[]{:S(2)}, u32[]{:S(2)}) async-start(bf16[16,128,256]{2,1,0:T(8,128)(2,1)} %broadcast_in_dim.33), calls=%async_computation.3 | async-start | bytes 2097152 | tf_op jit(solution)/shard_map/all_to_all | solution.py:20
  120.8 28.0 %all-to-all-done.3 = bf16[16,128,256]{2,1,0:T(8,128)(2,1)S(1)} async-done(((bf16[16,128,256]{2,1,0:T(8,128)(2,1)}), bf16[16,128,256]{2,1,0:T(8,128)(2,1)S(1)}, u32[]{:S(2)}, u32[]{:S(2)}) %all-to-all-start.3) | async-done | bytes 1048608 | tf_op jit(solution)/shard_map/all_to_all | solution.py:20
  149.6 1.0 fusion.6
  (89 shorter events, 9.2 us)
Async XLA Ops:
  4.3 0.6 copy-start.4
  4.3 0.6 copy-start.5
  4.3 1.3 copy-start.6
  4.8 1.9 %copy-start.1 = (bf16[128,128]{0,1:T(8,128)(2,1)}, bf16[128,128]{0,1:T(8,128)(2,1)S(1)}, u32[]{:S(2)}) copy-start(bf16[128,128]{0,1:T(8,128)(2,1)S(1)} %fusion.97) | copy-start | bytes 98308
  6.0 14.9 %copy-start = (bf16[128,4096]{1,0:T(8,128)(2,1)S(1)}, bf16[128,4096]{1,0:T(8,128)(2,1)}, u32[]{:S(2)}) copy-start(bf16[128,4096]{1,0:T(8,128)(2,1)} %param.13) | copy-start | bytes 3145732
  6.8 20.6 %all-to-all-start = ((f32[16,26,128]{2,1,0:T(8,128)}), f32[16,26,128]{2,1,0:T(8,128)S(1)}, u32[]{:S(2)}, u32[]{:S(2)}) async-start(f32[16,26,128]{2,1,0:T(8,128)} %broadcast_in_dim.28), calls=%async_computation | async-start | bytes 524288 | tf_op jit(solution)/shard_map/all_to_all | solution.py:20
  34.0 2.4 %copy-start.8 = (f32[128,16]{0,1:T(8,128)S(1)}, f32[128,16]{0,1:T(8,128)}, u32[]{:S(2)}) copy-start(f32[128,16]{0,1:T(8,128)} %get-tuple-element.4) | copy-start | bytes 24580
  34.0 3.0 %copy-start.10 = (f32[2,128]{1,0:T(2,128)S(1)}, f32[2,128]{1,0:T(2,128)}, u32[]{:S(2)}) copy-start(f32[2,128]{1,0:T(2,128)} %convert_subtract_fusion) | copy-start | bytes 3076
  34.0 3.0 %copy-start.9 = (f32[2,128]{1,0:T(2,128)S(1)}, f32[2,128]{1,0:T(2,128)}, u32[]{:S(2)}) copy-start(f32[2,128]{1,0:T(2,128)} %slice_bitcast_fusion.13) | copy-start | bytes 3076
  37.7 32.4 %copy-start.3 = (bf16[128,128]{1,0:T(8,128)(2,1)S(1)}, bf16[128,128]{1,0:T(8,128)(2,1)}, u32[]{:S(2)}) copy-start(bf16[128,128]{1,0:T(8,128)(2,1)} %param.8) | copy-start | bytes 98308
  37.7 3.8 %collective-permute-start = (bf16[16,128,128]{2,1,0:T(8,128)(2,1)S(1)}, bf16[16,128,128]{2,1,0:T(8,128)(2,1)S(1)}, u32[]{:S(2)}, u32[]{:S(2)}) collective-permute-start(bf16[16,128,128]{2,1,0:T(8,128)(2,1)S(1)} %fusion.15), channel_id=1, source_target_pairs={{0,1},{1,0},{2,3},{3,2},{4,5},{5,4},{6,7},{7,6},{8,9},{9,8},{10,11... | collective-permute-start | bytes 1572872 | tf_op jit(solution)/shard_map/ppermute | solution.py:157
  70.1 10.1 %copy-start.2 = (bf16[128,128]{1,0:T(8,128)(2,1)}, bf16[128,128]{1,0:T(8,128)(2,1)S(1)}, u32[]{:S(2)}) copy-start(bf16[128,128]{1,0:T(8,128)(2,1)S(1)} %add_convert_fusion) | copy-start | bytes 98308
  71.4 34.6 %all-to-all-start.2 = ((bf16[32,128,1,128]{3,1,2,0:T(8,128)(2,1)}), bf16[32,128,1,128]{3,1,2,0:T(8,128)(2,1)}, u32[]{:S(2)}, u32[]{:S(2)}) async-start(bf16[32,128,1,128]{3,1,2,0:T(8,128)(2,1)} %broadcast_in_dim_broadcast_in_dim.2), calls=%async_computation.2 | async-start | bytes 2097152 | tf_op jit(solution)/shard_map/all_to_all | solution.py:20
  80.2 29.9 %copy-start.7 = (f32[4096]{0:T(1024)S(1)}, f32[4096]{0:T(1024)}, u32[]{:S(2)}) copy-start(f32[4096]{0:T(1024)} %param.14) | copy-start | bytes 49156
  114.3 34.5 %all-to-all-start.3 = ((bf16[16,128,256]{2,1,0:T(8,128)(2,1)}), bf16[16,128,256]{2,1,0:T(8,128)(2,1)S(1)}, u32[]{:S(2)}, u32[]{:S(2)}) async-start(bf16[16,128,256]{2,1,0:T(8,128)(2,1)} %broadcast_in_dim.33), calls=%async_computation.3 | async-start | bytes 2097152 | tf_op jit(solution)/shard_map/all_to_all | solution.py:20

commit v10 on v9

--- a/solution.py
+++ b/solution.py
@@ -103,6 +103,16 @@
     tail_rows = feats_wide[-2:].reshape(6, chan_count)
     payload = jnp.concatenate([late_state.T, head_rows, tail_rows], axis=0)
     received = gather_by_exchange(payload, "ctx", concat_axis=0)
+    conv_blind = modal_conv(
+        blind_product, residues, rates, jnp.zeros_like(rates), block_limit=16
+    )
+    weight = residues * jnp.sqrt(1.0 - jnp.exp(-2.0 * rates))
+    full_powers = jnp.exp(-rates[:, :, None] * lag_steps)
+    long_taps = jnp.sum(weight[:, :, None] * full_powers, axis=1)
+    later_taps = jnp.concatenate([jnp.zeros_like(long_taps[:, :1]), long_taps[:, :-1]], axis=1)
+    received, conv_blind, long_taps, later_taps, full_powers = lax.optimization_barrier(
+        (received, conv_blind, long_taps, later_taps, full_powers)
+    )
     late_all = received[:, :mode_count]
     head_all = received[:, mode_count : mode_count + 4].reshape(ctx_count, 2, 2, chan_count)
     tail_all = received[:, mode_count + 4 :].reshape(ctx_count, 2, 3, chan_count)
@@ -126,13 +136,6 @@
         0.0,
     )
     start_state = jnp.sum(decay * gathered_states, axis=0).T
-    conv_blind = modal_conv(
-        blind_product, residues, rates, jnp.zeros_like(rates), block_limit=16
-    )
-    weight = residues * jnp.sqrt(1.0 - jnp.exp(-2.0 * rates))
-    full_powers = jnp.exp(-rates[:, :, None] * lag_steps)
-    long_taps = jnp.sum(weight[:, :, None] * full_powers, axis=1)
-    later_taps = jnp.concatenate([jnp.zeros_like(long_taps[:, :1]), long_taps[:, :-1]], axis=1)
     own_prior = lax.dynamic_index_in_dim(prev_tail, ctx_index, 0, keepdims=False)
     own_edge = short_conv(jnp.concatenate([own_prior, feats_wide[:2]], axis=0), short_filter)
     own_edge_product = (own_edge[:, 1] * own_edge[:, 2]).astype(jnp.bfloat16).astype(jnp.float32)

time: 153 us -> 153 us (level)
  waiting for transfers between devices: 60.7 us -> 55.3 us
  starting transfers between devices: 24.1 us -> 27.2 us
    all_to_all x3, waiting for transfers between devices: 58.9 us -> 53.5 us  [gather_by_exchange(): lax.all_to_all(copies, axis, split_axis=0, concat_axis=concat_axis, tiled...]
    all_to_all x3, starting transfers between devices: 22.2 us -> 25.3 us  [gather_by_exchange(): lax.all_to_all(copies, axis, split_axis=0, concat_axis=concat_axis, tiled...]
    unnamed x28 -> x36, local copies, waits for them, and re-layouts: 5.1 us -> 6.18 us
  transfers between devices with their start and end apart: 4 -> 4, of which waited for: 4 -> 3; matrix products, arithmetic and copies ran while one was open for 6% -> 12% of each run, Pallas kernels for 0% -> 0%
where the time goes in v10:
time: 153 us; the launch traced here: 151 us
  waiting for transfers between devices  55.3 us (36%)
  blocking collectives  28.3 us (18%)
  starting transfers between devices  27.2 us (18%)
  local copies, waits for them, and re-layouts  17.9 us (12%)
  other arithmetic  13.9 us (9%)
  matrix products  6.88 us (4%)
    all_to_all x3, waiting for transfers between devices, gather_by_exchange(): lax.all_to_all(copies, axis, split_axis=0, concat_axis=concat_axis, tiled...  53.5 us
    all_to_all x1, blocking collectives, per_device(): lax.all_to_all(chip_sum, 'tp', split_axis=0, concat_axis=0, axis_index_gr...  28.3 us
    all_to_all x3, starting transfers between devices, gather_by_exchange(): lax.all_to_all(copies, axis, split_axis=0, concat_axis=concat_axis, tiled...  25.3 us
    unnamed x36, local copies, waits for them, and re-layouts  6.18 us
  transfers between devices with their start and end apart: 4, of which 3 were waited for; matrix products, arithmetic and copies ran while one was open for 12% of the time, Pallas kernels for 0%

profile of v10, /device:TPU:6, one launch (start us, length us, event | category | flops | bytes accessed | tf_op | source)
XLA Modules:
  0.0 150.8 jit_solution(4900222368343546530)
XLA Ops:
  0.6 0.9 convert_element_type.103
  1.6 1.3 fusion.85
  2.8 0.7 slice.210
  3.5 0.7 slice_bitcast_fusion.12
  5.0 1.3 multiply_bitcast_fusion
  7.1 0.7 broadcast_in_dim.26
  7.8 10.1 %all-to-all-start = ((f32[16,26,128]{2,1,0:T(8,128)}), f32[16,26,128]{2,1,0:T(8,128)S(1)}, u32[]{:S(2)}, u32[]{:S(2)}) async-start(f32[16,26,128]{2,1,0:T(8,128)} %broadcast_in_dim.26), calls=%async_computation | async-start | bytes 524288 | tf_op jit(solution)/shard_map/all_to_all | solution.py:20
  19.3 0.7 fusion.73
  20.0 0.7 fusion.74
  23.9 0.9 copy.88
  24.8 0.9 fusion.87
  25.8 1.7 %convolution_bitcast_fusion = f32[128,16,8]{1,2,0:T(8,128)S(1)} fusion(bf16[128,8,16]{2,1,0:T(8,128)(2,1)S(1)} %copy.88, f32[16]{0:T(128)} %iota_subtract_fusion.2, f32[128,16]{1,0:T(8,128)S(1)} %copy.85), kind=kOutput, calls=%fused_computation.10 | convolution fusion | flops 3178496 | bytes 106560 | tf_op jit(solution)/shard_map/cnj,cmj->cnm/dot_general | solution.py:47
  27.7 0.8 copy.90
  28.5 1.0 multiply_reduce_fusion.3
  29.8 1.2 convolution_add_fusion
  31.3 1.6 %copy.96 = bf16[128,4096]{0,1:T(8,128)(2,1)S(1)} copy(bf16[128,4096]{1,0:T(8,128)(2,1)} %param.13) | data formatting | bytes 2097152 | tf_op args[5]
  33.3 0.7 convert_subtract_fusion
  35.2 1.9 %collective-permute-start = (bf16[16,128,128]{2,1,0:T(8,128)(2,1)S(1)}, bf16[16,128,128]{2,1,0:T(8,128)(2,1)S(1)}, u32[]{:S(2)}, u32[]{:S(2)}) collective-permute-start(bf16[16,128,128]{2,1,0:T(8,128)(2,1)S(1)} %fusion.15), channel_id=1, source_target_pairs={{0,1},{1,0},{2,3},{3,2},{4,5},{5,4},{6,7},{7,6},{8,9},{9,8},{10,11... | collective-permute-start | bytes 1572872 | tf_op jit(solution)/shard_map/ppermute | solution.py:160
  37.1 1.9 %collective-permute-done = bf16[16,128,128]{2,1,0:T(8,128)(2,1)S(1)} collective-permute-done((bf16[16,128,128]{2,1,0:T(8,128)(2,1)S(1)}, bf16[16,128,128]{2,1,0:T(8,128)(2,1)S(1)}, u32[]{:S(2)}, u32[]{:S(2)}) %collective-permute-start) | collective-permute-done | bytes 524320 | tf_op jit(solution)/shard_map/ppermute | solution.py:160
  39.2 28.3 %all_to_all.24 = bf16[16,128,128]{2,1,0:T(8,128)(2,1)S(1)} all-to-all(bf16[16,128,128]{2,1,0:T(8,128)(2,1)S(1)} %fusion.7), channel_id=1, replica_groups={{0,2,4,6,8,10,12,14,16,18,20,22,24,26,28,30},{1,3,5,7,9,11,13,15,17,19,..., dimensions={0} | all-to-all | bytes 1048576 | tf_op jit(solution)/shard_map/all_to_all | solution.py:163
  67.6 1.3 broadcast_in_dim_broadcast_in_dim.2
  68.8 5.6 %all-to-all-start.2 = ((bf16[32,128,1,128]{3,1,2,0:T(8,128)(2,1)}), bf16[32,128,1,128]{3,1,2,0:T(8,128)(2,1)}, u32[]{:S(2)}, u32[]{:S(2)}) async-start(bf16[32,128,1,128]{3,1,2,0:T(8,128)(2,1)} %broadcast_in_dim_broadcast_in_dim.2), calls=%async_computation.2 | async-start | bytes 2097152 | tf_op jit(solution)/shard_map/all_to_all | solution.py:20
  74.4 3.2 %copy.100 = bf16[4096,3,128]{0,2,1:T(8,128)(2,1)S(1)} copy(bf16[4096,3,128]{2,0,1:T(8,128)(2,1)} %param.15) | data formatting | bytes 6291456 | tf_op args[7]
  77.7 25.8 %all-to-all-done.2 = bf16[32,128,1,128]{3,1,2,0:T(8,128)(2,1)} async-done(((bf16[32,128,1,128]{3,1,2,0:T(8,128)(2,1)}), bf16[32,128,1,128]{3,1,2,0:T(8,128)(2,1)}, u32[]{:S(2)}, u32[]{:S(2)}) %all-to-all-start.2) | async-done | bytes 1048608 | tf_op jit(solution)/shard_map/all_to_all | solution.py:20
  103.5 2.3 %copy.99 = bf16[32,128,1,128]{1,3,0,2:T(8,128)(2,1)} copy(bf16[32,128,1,128]{3,1,2,0:T(8,128)(2,1)} %all-to-all-done.2) | data formatting | bytes 2097152 | tf_op jit(solution)/shard_map/all_to_all | solution.py:20
  105.7 1.8 %fusion.3 = f32[128]{0:T(128)S(1)} fusion(bf16[32,128,1,128]{1,3,0,2:T(8,128)(2,1)} %copy.99), kind=kLoop, calls=%fused_computation.6 | loop fusion | flops 1572736 | bytes 1049088 | tf_op jit(solution)/shard_map/reduce_sum | solution.py:170
  107.5 1.7 %fusion.5 = bf16[32,1,128,1,128]{2,4,0,3,1:T(8,128)(2,1)S(1)} fusion(bf16[32,128,1,128]{1,3,0,2:T(8,128)(2,1)} %copy.99, f32[32,128]{1,0:T(8,128)S(1)} %bitcast.146, f32[128]{0:T(128)S(1)} %add_rsqrt_fusion), kind=kLoop, calls=%fused_computation.8 | loop fusion | flops 2097152 | bytes 2114048 | tf_op jit(solution)/shard_map/convert_element_type | solution.py:171
  109.3 1.0 fusion
  110.6 1.1 broadcast_in_dim.31
  111.7 9.6 %all-to-all-start.3 = ((bf16[16,128,256]{2,1,0:T(8,128)(2,1)}), bf16[16,128,256]{2,1,0:T(8,128)(2,1)S(1)}, u32[]{:S(2)}, u32[]{:S(2)}) async-start(bf16[16,128,256]{2,1,0:T(8,128)(2,1)} %broadcast_in_dim.31), calls=%async_computation.3 | async-start | bytes 2097152 | tf_op jit(solution)/shard_map/all_to_all | solution.py:20
  121.3 27.7 %all-to-all-done.3 = bf16[16,128,256]{2,1,0:T(8,128)(2,1)S(1)} async-done(((bf16[16,128,256]{2,1,0:T(8,128)(2,1)}), bf16[16,128,256]{2,1,0:T(8,128)(2,1)S(1)}, u32[]{:S(2)}, u32[]{:S(2)}) %all-to-all-start.3) | async-done | bytes 1048608 | tf_op jit(solution)/shard_map/all_to_all | solution.py:20
  149.8 1.0 fusion.6
  (99 shorter events, 9.5 us)
Async XLA Ops:
  4.2 0.7 copy-start.5
  4.3 0.7 copy-start.7
  4.3 0.7 copy-start.9
  4.3 0.6 copy-start
  7.8 25.1 %all-to-all-start = ((f32[16,26,128]{2,1,0:T(8,128)}), f32[16,26,128]{2,1,0:T(8,128)S(1)}, u32[]{:S(2)}, u32[]{:S(2)}) async-start(f32[16,26,128]{2,1,0:T(8,128)} %broadcast_in_dim.26), calls=%async_computation | async-start | bytes 524288 | tf_op jit(solution)/shard_map/all_to_all | solution.py:20
  29.8 3.2 %copy-start.12 = (f32[3,3,128]{2,1,0:T(4,128)S(1)}, f32[3,3,128]{2,1,0:T(4,128)}, u32[]{:S(2)}) copy-start(f32[3,3,128]{2,1,0:T(4,128)} %param.10) | copy-start | bytes 13828
  31.0 2.2 %copy-start.6 = (f32[3,128]{1,0:T(4,128)S(1)}, f32[3,128]{1,0:T(4,128)}, u32[]{:S(2)}) copy-start(f32[3,128]{1,0:T(4,128)} %copy-done.5) | copy-start | bytes 4612
  31.0 2.2 %copy-start.8 = (f32[3,128]{1,0:T(4,128)S(1)}, f32[3,128]{1,0:T(4,128)}, u32[]{:S(2)}) copy-start(f32[3,128]{1,0:T(4,128)} %copy-done.7) | copy-start | bytes 4612
  31.0 2.2 %copy-start.10 = (f32[3,128]{1,0:T(4,128)S(1)}, f32[3,128]{1,0:T(4,128)}, u32[]{:S(2)}) copy-start(f32[3,128]{1,0:T(4,128)} %copy-done.9) | copy-start | bytes 4612
  31.0 2.2 %copy-start.13 = (f32[2,3,128]{2,0,1:T(2,128)S(1)}, f32[2,3,128]{2,0,1:T(2,128)}, u32[]{:S(2)}) copy-start(f32[2,3,128]{2,0,1:T(2,128)} %get-tuple-element.19) | copy-start | bytes 9220
  31.1 3.0 %copy-start.2 = (f32[16,128]{1,0:T(8,128)S(1)}, f32[16,128]{1,0:T(8,128)}, u32[]{:S(2)}) copy-start(f32[16,128]{1,0:T(8,128)} %get-tuple-element.12) | copy-start | bytes 24580
  31.1 3.0 %copy-start.3 = (f32[16,128]{1,0:T(8,128)S(1)}, f32[16,128]{1,0:T(8,128)}, u32[]{:S(2)}) copy-start(f32[16,128]{1,0:T(8,128)} %get-tuple-element.13) | copy-start | bytes 24580
  31.1 3.0 %copy-start.14 = (f32[16]{0:T(128)S(1)}, f32[16]{0:T(128)}, u32[]{:S(2)}) copy-start(f32[16]{0:T(128)} %fusion.79) | copy-start | bytes 196
  31.1 3.0 %copy-start.15 = (pred[16]{0:T(512)(128)(4,1)S(1)}, pred[16]{0:T(512)(128)(4,1)}, u32[]{:S(2)}) copy-start(pred[16]{0:T(512)(128)(4,1)} %fusion.80) | copy-start | bytes 52
  35.2 32.4 %copy-start.4 = (bf16[128,128]{1,0:T(8,128)(2,1)S(1)}, bf16[128,128]{1,0:T(8,128)(2,1)}, u32[]{:S(2)}) copy-start(bf16[128,128]{1,0:T(8,128)(2,1)} %param.8) | copy-start | bytes 98308
  35.2 3.8 %collective-permute-start = (bf16[16,128,128]{2,1,0:T(8,128)(2,1)S(1)}, bf16[16,128,128]{2,1,0:T(8,128)(2,1)S(1)}, u32[]{:S(2)}, u32[]{:S(2)}) collective-permute-start(bf16[16,128,128]{2,1,0:T(8,128)(2,1)S(1)} %fusion.15), channel_id=1, source_target_pairs={{0,1},{1,0},{2,3},{3,2},{4,5},{5,4},{6,7},{7,6},{8,9},{9,8},{10,11... | collective-permute-start | bytes 1572872 | tf_op jit(solution)/shard_map/ppermute | solution.py:160
  67.6 10.1 %copy-start.1 = (bf16[128,128]{1,0:T(8,128)(2,1)}, bf16[128,128]{1,0:T(8,128)(2,1)S(1)}, u32[]{:S(2)}) copy-start(bf16[128,128]{1,0:T(8,128)(2,1)S(1)} %add_convert_fusion) | copy-start | bytes 98308
  68.8 34.6 %all-to-all-start.2 = ((bf16[32,128,1,128]{3,1,2,0:T(8,128)(2,1)}), bf16[32,128,1,128]{3,1,2,0:T(8,128)(2,1)}, u32[]{:S(2)}, u32[]{:S(2)}) async-start(bf16[32,128,1,128]{3,1,2,0:T(8,128)(2,1)} %broadcast_in_dim_broadcast_in_dim.2), calls=%async_computation.2 | async-start | bytes 2097152 | tf_op jit(solution)/shard_map/all_to_all | solution.py:20
  77.6 29.9 %copy-start.11 = (f32[4096]{0:T(1024)S(1)}, f32[4096]{0:T(1024)}, u32[]{:S(2)}) copy-start(f32[4096]{0:T(1024)} %param.14) | copy-start | bytes 49156
  111.7 37.3 %all-to-all-start.3 = ((bf16[16,128,256]{2,1,0:T(8,128)(2,1)}), bf16[16,128,256]{2,1,0:T(8,128)(2,1)S(1)}, u32[]{:S(2)}, u32[]{:S(2)}) async-start(bf16[16,128,256]{2,1,0:T(8,128)(2,1)} %broadcast_in_dim.31), calls=%async_computation.3 | async-start | bytes 2097152 | tf_op jit(solution)/shard_map/all_to_all | solution.py:20

commit v11 on v10

--- a/solution.py
+++ b/solution.py
@@ -168,9 +168,12 @@
     full_rows = gather_by_exchange(hyena_out, "tp").reshape(row_count, width_all)
     wide = full_rows.astype(jnp.float32)
     mean_square = jnp.mean(wide * wide, axis=1, keepdims=True)
-    normed = (wide * lax.rsqrt(mean_square + eps_norm) * norm_gain).astype(jnp.bfloat16)
-    projected = jnp.dot(
-        normed, attn_weight.reshape(width_all, 3 * chan_count), preferred_element_type=jnp.float32
+    scaled = (wide * norm_gain).astype(jnp.bfloat16)
+    projected = (
+        jnp.dot(
+            scaled, attn_weight.reshape(width_all, 3 * chan_count), preferred_element_type=jnp.float32
+        )
+        * lax.rsqrt(mean_square + eps_norm)
     ).reshape(row_count, 3, chan_count)
     head_count = chan_count // HEAD_DIM
     first_pos = ctx_index * row_count

time: 153 us -> 150 us (0.980)
  local copies, waits for them, and re-layouts: 17.9 us -> 16.1 us
  other arithmetic: 13.9 us -> 12.3 us
    all_to_all x1 -> x0, local copies, waits for them, and re-layouts: 2.26 us -> none  [gather_by_exchange(): lax.all_to_all(copies, axis, split_axis=0, concat_axis=concat_axis, tiled...]
    convert_element_type x1 -> x0, other arithmetic: 1.75 us -> none  [per_device(): (wide * lax.rsqrt(mean_square + eps_norm) * norm_gain).astype(jnp.bfloat16)]
where the time goes in v11:
time: 150 us; the launch traced here: 148 us
  waiting for transfers between devices  55.3 us (37%)
  blocking collectives  28.3 us (19%)
  starting transfers between devices  27.2 us (18%)
  local copies, waits for them, and re-layouts  16.1 us (11%)
  other arithmetic  12.3 us (8%)
  matrix products  7.05 us (5%)
    all_to_all x3, waiting for transfers between devices, gather_by_exchange(): lax.all_to_all(copies, axis, split_axis=0, concat_axis=concat_axis, tiled...  53.5 us
    all_to_all x1, blocking collectives, per_device(): lax.all_to_all(chip_sum, 'tp', split_axis=0, concat_axis=0, axis_index_gr...  28.3 us
    all_to_all x3, starting transfers between devices, gather_by_exchange(): lax.all_to_all(copies, axis, split_axis=0, concat_axis=concat_axis, tiled...  25.3 us
    unnamed x36, local copies, waits for them, and re-layouts  6.18 us
  transfers between devices with their start and end apart: 4, of which 3 were waited for; matrix products, arithmetic and copies ran while one was open for 12% of the time, Pallas kernels for 0%

profile of v11, /device:TPU:6, one launch (start us, length us, event | category | flops | bytes accessed | tf_op | source)
XLA Modules:
  0.0 147.5 jit_solution(12531978118506730506)
XLA Ops:
  0.6 0.9 convert_element_type.103
  1.6 1.3 fusion.81
  2.9 0.7 slice.210
  3.5 0.7 slice_bitcast_fusion.12
  5.0 1.3 multiply_bitcast_fusion
  7.1 0.7 broadcast_in_dim.26
  7.9 10.1 %all-to-all-start = ((f32[16,26,128]{2,1,0:T(8,128)}), f32[16,26,128]{2,1,0:T(8,128)S(1)}, u32[]{:S(2)}, u32[]{:S(2)}) async-start(f32[16,26,128]{2,1,0:T(8,128)} %broadcast_in_dim.26), calls=%async_computation | async-start | bytes 524288 | tf_op jit(solution)/shard_map/all_to_all | solution.py:20
  18.1 0.6 fusion.36
  19.4 0.7 fusion.69
  20.0 0.7 fusion.70
  22.4 0.6 multiply_reduce_fusion.2
  23.9 0.9 copy.78
  24.9 0.9 fusion.83
  25.8 1.8 %convolution_bitcast_fusion = f32[128,16,8]{1,2,0:T(8,128)S(1)} fusion(bf16[128,8,16]{2,1,0:T(8,128)(2,1)S(1)} %copy.78, f32[16]{0:T(128)} %iota_subtract_fusion.2, f32[128,16]{1,0:T(8,128)S(1)} %copy.75), kind=kOutput, calls=%fused_computation.7 | convolution fusion | flops 3178496 | bytes 106560 | tf_op jit(solution)/shard_map/cnj,cmj->cnm/dot_general | solution.py:47
  27.8 0.8 copy.80
  28.6 1.0 multiply_reduce_fusion.3
  29.9 1.2 convolution_add_fusion
  31.4 1.6 %copy.86 = bf16[128,4096]{0,1:T(8,128)(2,1)S(1)} copy(bf16[128,4096]{1,0:T(8,128)(2,1)} %param.13) | data formatting | bytes 2097152 | tf_op args[5]
  33.3 0.7 convert_subtract_fusion
  35.2 1.9 %collective-permute-start = (bf16[16,128,128]{2,1,0:T(8,128)(2,1)S(1)}, bf16[16,128,128]{2,1,0:T(8,128)(2,1)S(1)}, u32[]{:S(2)}, u32[]{:S(2)}) collective-permute-start(bf16[16,128,128]{2,1,0:T(8,128)(2,1)S(1)} %fusion.12), channel_id=1, source_target_pairs={{0,1},{1,0},{2,3},{3,2},{4,5},{5,4},{6,7},{7,6},{8,9},{9,8},{10,11... | collective-permute-start | bytes 1572872 | tf_op jit(solution)/shard_map/ppermute | solution.py:160
  37.2 1.9 %collective-permute-done = bf16[16,128,128]{2,1,0:T(8,128)(2,1)S(1)} collective-permute-done((bf16[16,128,128]{2,1,0:T(8,128)(2,1)S(1)}, bf16[16,128,128]{2,1,0:T(8,128)(2,1)S(1)}, u32[]{:S(2)}, u32[]{:S(2)}) %collective-permute-start) | collective-permute-done | bytes 524320 | tf_op jit(solution)/shard_map/ppermute | solution.py:160
  39.2 28.3 %all_to_all.24 = bf16[16,128,128]{2,1,0:T(8,128)(2,1)S(1)} all-to-all(bf16[16,128,128]{2,1,0:T(8,128)(2,1)S(1)} %fusion.4), channel_id=1, replica_groups={{0,2,4,6,8,10,12,14,16,18,20,22,24,26,28,30},{1,3,5,7,9,11,13,15,17,19,..., dimensions={0} | all-to-all | bytes 1048576 | tf_op jit(solution)/shard_map/all_to_all | solution.py:163
  67.7 1.3 broadcast_in_dim_broadcast_in_dim.2
  69.0 5.6 %all-to-all-start.2 = ((bf16[32,128,1,128]{1,3,2,0:T(8,128)(2,1)}), bf16[32,128,1,128]{1,3,2,0:T(8,128)(2,1)}, u32[]{:S(2)}, u32[]{:S(2)}) async-start(bf16[32,128,1,128]{1,3,2,0:T(8,128)(2,1)} %broadcast_in_dim_broadcast_in_dim.2), calls=%async_computation.2 | async-start | bytes 2097152 | tf_op jit(solution)/shard_map/all_to_all | solution.py:20
  74.6 3.2 %copy.91 = bf16[4096,3,128]{0,2,1:T(8,128)(2,1)S(1)} copy(bf16[4096,3,128]{2,0,1:T(8,128)(2,1)} %param.15) | data formatting | bytes 6291456 | tf_op args[7]
  77.8 25.8 %all-to-all-done.2 = bf16[32,128,1,128]{1,3,2,0:T(8,128)(2,1)} async-done(((bf16[32,128,1,128]{1,3,2,0:T(8,128)(2,1)}), bf16[32,128,1,128]{1,3,2,0:T(8,128)(2,1)}, u32[]{:S(2)}, u32[]{:S(2)}) %all-to-all-start.2) | async-done | bytes 1048608 | tf_op jit(solution)/shard_map/all_to_all | solution.py:20
  103.7 1.8 %fusion.2 = (f32[128]{0:T(128)S(1)}, bf16[32,1,128,1,128]{2,4,0,3,1:T(8,128)(2,1)S(1)}) fusion(bf16[32,128,1,128]{1,3,2,0:T(8,128)(2,1)} %all-to-all-done.2, f32[32,128]{1,0:T(8,128)S(1)} %bitcast.145), kind=kLoop, calls=%fused_computation.5 | loop fusion | flops 2621312 | bytes 2114048 | tf_op jit(solution)/shard_map/reduce_sum | solution.py:170
  105.4 1.1 convolution_multiply_fusion.1
  107.4 1.1 broadcast_in_dim.31
  108.5 9.6 %all-to-all-start.3 = ((bf16[16,128,256]{2,1,0:T(8,128)(2,1)}), bf16[16,128,256]{2,1,0:T(8,128)(2,1)S(1)}, u32[]{:S(2)}, u32[]{:S(2)}) async-start(bf16[16,128,256]{2,1,0:T(8,128)(2,1)} %broadcast_in_dim.31), calls=%async_computation.3 | async-start | bytes 2097152 | tf_op jit(solution)/shard_map/all_to_all | solution.py:20
  118.1 27.7 %all-to-all-done.3 = bf16[16,128,256]{2,1,0:T(8,128)(2,1)S(1)} async-done(((bf16[16,128,256]{2,1,0:T(8,128)(2,1)}), bf16[16,128,256]{2,1,0:T(8,128)(2,1)S(1)}, u32[]{:S(2)}, u32[]{:S(2)}) %all-to-all-start.3) | async-done | bytes 1048608 | tf_op jit(solution)/shard_map/all_to_all | solution.py:20
  146.5 1.0 fusion.3
  (101 shorter events, 8.8 us)
Async XLA Ops:
  4.3 0.7 copy-start.5
  4.3 0.7 copy-start.7
  4.3 0.7 copy-start.9
  4.3 0.6 copy-start
  7.9 25.2 %all-to-all-start = ((f32[16,26,128]{2,1,0:T(8,128)}), f32[16,26,128]{2,1,0:T(8,128)S(1)}, u32[]{:S(2)}, u32[]{:S(2)}) async-start(f32[16,26,128]{2,1,0:T(8,128)} %broadcast_in_dim.26), calls=%async_computation | async-start | bytes 524288 | tf_op jit(solution)/shard_map/all_to_all | solution.py:20
  27.6 5.4 %copy-start.12 = (f32[3,3,128]{2,1,0:T(4,128)S(1)}, f32[3,3,128]{2,1,0:T(4,128)}, u32[]{:S(2)}) copy-start(f32[3,3,128]{2,1,0:T(4,128)} %param.10) | copy-start | bytes 13828
  28.6 4.7 %copy-start.6 = (f32[3,128]{1,0:T(4,128)S(1)}, f32[3,128]{1,0:T(4,128)}, u32[]{:S(2)}) copy-start(f32[3,128]{1,0:T(4,128)} %copy-done.5) | copy-start | bytes 4612
  28.6 4.7 %copy-start.8 = (f32[3,128]{1,0:T(4,128)S(1)}, f32[3,128]{1,0:T(4,128)}, u32[]{:S(2)}) copy-start(f32[3,128]{1,0:T(4,128)} %copy-done.7) | copy-start | bytes 4612
  28.6 4.7 %copy-start.10 = (f32[3,128]{1,0:T(4,128)S(1)}, f32[3,128]{1,0:T(4,128)}, u32[]{:S(2)}) copy-start(f32[3,128]{1,0:T(4,128)} %copy-done.9) | copy-start | bytes 4612
  28.6 4.7 %copy-start.13 = (f32[2,3,128]{2,0,1:T(2,128)S(1)}, f32[2,3,128]{2,0,1:T(2,128)}, u32[]{:S(2)}) copy-start(f32[2,3,128]{2,0,1:T(2,128)} %get-tuple-element.21) | copy-start | bytes 9220
  29.6 4.4 %copy-start.2 = (f32[16,128]{1,0:T(8,128)S(1)}, f32[16,128]{1,0:T(8,128)}, u32[]{:S(2)}) copy-start(f32[16,128]{1,0:T(8,128)} %get-tuple-element.14) | copy-start | bytes 24580
  29.6 4.4 %copy-start.3 = (f32[16,128]{1,0:T(8,128)S(1)}, f32[16,128]{1,0:T(8,128)}, u32[]{:S(2)}) copy-start(f32[16,128]{1,0:T(8,128)} %get-tuple-element.15) | copy-start | bytes 24580
  29.6 4.4 %copy-start.14 = (f32[16]{0:T(128)S(1)}, f32[16]{0:T(128)}, u32[]{:S(2)}) copy-start(f32[16]{0:T(128)} %fusion.75) | copy-start | bytes 196
  29.6 4.4 %copy-start.15 = (pred[16]{0:T(512)(128)(4,1)S(1)}, pred[16]{0:T(512)(128)(4,1)}, u32[]{:S(2)}) copy-start(pred[16]{0:T(512)(128)(4,1)} %fusion.76) | copy-start | bytes 52
  35.1 32.5 %copy-start.4 = (bf16[128,128]{1,0:T(8,128)(2,1)S(1)}, bf16[128,128]{1,0:T(8,128)(2,1)}, u32[]{:S(2)}) copy-start(bf16[128,128]{1,0:T(8,128)(2,1)} %param.8) | copy-start | bytes 98308
  35.2 3.8 %collective-permute-start = (bf16[16,128,128]{2,1,0:T(8,128)(2,1)S(1)}, bf16[16,128,128]{2,1,0:T(8,128)(2,1)S(1)}, u32[]{:S(2)}, u32[]{:S(2)}) collective-permute-start(bf16[16,128,128]{2,1,0:T(8,128)(2,1)S(1)} %fusion.12), channel_id=1, source_target_pairs={{0,1},{1,0},{2,3},{3,2},{4,5},{5,4},{6,7},{7,6},{8,9},{9,8},{10,11... | collective-permute-start | bytes 1572872 | tf_op jit(solution)/shard_map/ppermute | solution.py:160
  67.6 10.2 %copy-start.1 = (bf16[128,128]{1,0:T(8,128)(2,1)}, bf16[128,128]{1,0:T(8,128)(2,1)S(1)}, u32[]{:S(2)}) copy-start(bf16[128,128]{1,0:T(8,128)(2,1)S(1)} %add_convert_fusion) | copy-start | bytes 98308
  69.0 34.7 %all-to-all-start.2 = ((bf16[32,128,1,128]{1,3,2,0:T(8,128)(2,1)}), bf16[32,128,1,128]{1,3,2,0:T(8,128)(2,1)}, u32[]{:S(2)}, u32[]{:S(2)}) async-start(bf16[32,128,1,128]{1,3,2,0:T(8,128)(2,1)} %broadcast_in_dim_broadcast_in_dim.2), calls=%async_computation.2 | async-start | bytes 2097152 | tf_op jit(solution)/shard_map/all_to_all | solution.py:20
  74.6 29.1 %copy-start.11 = (f32[4096]{0:T(1024)S(1)}, f32[4096]{0:T(1024)}, u32[]{:S(2)}) copy-start(f32[4096]{0:T(1024)} %param.14) | copy-start | bytes 49156
  108.5 37.3 %all-to-all-start.3 = ((bf16[16,128,256]{2,1,0:T(8,128)(2,1)}), bf16[16,128,256]{2,1,0:T(8,128)(2,1)S(1)}, u32[]{:S(2)}, u32[]{:S(2)}) async-start(bf16[16,128,256]{2,1,0:T(8,128)(2,1)} %broadcast_in_dim.31), calls=%async_computation.3 | async-start | bytes 2097152 | tf_op jit(solution)/shard_map/all_to_all | solution.py:20

commit v12 on v11

--- a/solution.py
+++ b/solution.py
@@ -32,31 +32,25 @@
     return window.reshape(chan_count, block_size, 2 * block_size - 2)[:, :, :block_size]
 
 
-def modal_conv(signal, residues, rates, start_state, block_limit=128):
+def modal_conv(signal, weight, rates, full_powers, block_size):
     chan_count, length = signal.shape
-    block_size = math.gcd(length, block_limit)
     block_count = length // block_size
-    weight = residues * jnp.sqrt(1.0 - jnp.exp(-2.0 * rates))
-    lag_steps = jnp.arange(block_size, dtype=jnp.float32)
-    powers = jnp.exp(-rates[:, :, None] * lag_steps)
+    powers = full_powers[:, :, :block_size]
     filter_taps = jnp.sum(weight[:, :, None] * powers, axis=1)
     toeplitz = toeplitz_lower(filter_taps)
     blocks = signal.reshape(chan_count, block_count, block_size)
     inner_part = jnp.einsum("cij,cnj->cni", toeplitz, blocks, precision=highest)
-    tail_powers = jnp.exp(-rates[:, :, None] * (block_size - lag_steps))
+    tail_powers = full_powers[:, :, block_size:0:-1]
     end_states = jnp.einsum("cnj,cmj->cnm", blocks, tail_powers, precision=highest)
     block_steps = jnp.arange(block_count, dtype=jnp.float32)
     gap_count = block_steps[:, None] - 1.0 - block_steps[None, :]
     live_mask = gap_count >= 0.0
     carry_mat = jnp.where(
-        live_mask, jnp.exp(-rates[:, :, None, None] * block_size * jnp.maximum(gap_count, 0.0)), 0.0
+        live_mask,
+        jnp.exp(-rates[:, :, None, None] * block_size * jnp.maximum(gap_count, 0.0)),
+        0.0,
     )
     states = jnp.einsum("cmnk,ckm->cnm", carry_mat, end_states, precision=highest)
-    states = (
-        states
-        + jnp.exp(-rates[:, None, :] * block_size * block_steps[None, :, None])
-        * start_state[:, None, :]
-    )
     cross_part = jnp.einsum("cnm,cmi->cni", states * weight[:, None, :], powers, precision=highest)
     return (inner_part + cross_part).reshape(chan_count, length)
 
@@ -91,7 +85,9 @@
     ctx_count = lax.axis_size("ctx")
     ctx_index = lax.axis_index("ctx")
     lag_steps = jnp.arange(row_count, dtype=jnp.float32)
-    tail_powers = jnp.exp(-rates[:, :, None] * (row_count - lag_steps))
+    weight = residues * jnp.sqrt(1.0 - jnp.exp(-2.0 * rates))
+    full_powers = jnp.exp(-rates[:, :, None] * lag_steps)
+    tail_powers = full_powers[:, :, ::-1] * jnp.exp(-rates)[:, :, None]
     no_prior = jnp.zeros((2,) + feats_wide.shape[1:], jnp.float32)
     blind = short_conv(jnp.concatenate([no_prior, feats_wide], axis=0), short_filter)
     blind_product = (blind[:, 1] * blind[:, 2]).astype(jnp.bfloat16).T.astype(jnp.float32)
@@ -103,11 +99,7 @@
     tail_rows = feats_wide[-2:].reshape(6, chan_count)
     payload = jnp.concatenate([late_state.T, head_rows, tail_rows], axis=0)
     received = gather_by_exchange(payload, "ctx", concat_axis=0)
-    conv_blind = modal_conv(
-        blind_product, residues, rates, jnp.zeros_like(rates), block_limit=16
-    )
-    weight = residues * jnp.sqrt(1.0 - jnp.exp(-2.0 * rates))
-    full_powers = jnp.exp(-rates[:, :, None] * lag_steps)
+    conv_blind = modal_conv(blind_product, weight, rates, full_powers, 16)
     long_taps = jnp.sum(weight[:, :, None] * full_powers, axis=1)
     later_taps = jnp.concatenate([jnp.zeros_like(long_taps[:, :1]), long_taps[:, :-1]], axis=1)
     received, conv_blind, long_taps, later_taps, full_powers = lax.optimization_barrier(

time: 150 us -> 165 us (1.10)
  local copies, waits for them, and re-layouts: 16.1 us -> 28.4 us
  other arithmetic: 12.3 us -> 14 us
    slice x0 -> x6, local copies, waits for them, and re-layouts: none -> 4.1 us  [the longest x2 3.32 us: per_device(): first_powers = tail_powers[:, :, 0].T]
    add x2 -> x3, other arithmetic: 0.08 us -> 1.83 us  [short_conv(): short_filter[0] * joined[2:] + short_filter[1] * joined[1:row_count + 1]]
    unnamed x36 -> x33, local copies, waits for them, and re-layouts: 6.18 us -> 7.31 us
  transfers between devices with their start and end apart: 4 -> 4, of which waited for: 3 -> 3; matrix products, arithmetic and copies ran while one was open for 12% -> 15% of each run, Pallas kernels for 0% -> 0%
where the time goes in v12:
time: 165 us; the launch traced here: 163 us
  waiting for transfers between devices  55.3 us (34%)
  local copies, waits for them, and re-layouts  28.4 us (17%)
  blocking collectives  28.3 us (17%)
  starting transfers between devices  27.2 us (16%)
  other arithmetic  14 us (8%)
  matrix products  8.13 us (5%)
    all_to_all x3, waiting for transfers between devices, gather_by_exchange(): lax.all_to_all(copies, axis, split_axis=0, concat_axis=concat_axis, tiled...  53.5 us
    all_to_all x1, blocking collectives, per_device(): lax.all_to_all(chip_sum, 'tp', split_axis=0, concat_axis=0, axis_index_gr...  28.3 us
    all_to_all x3, starting transfers between devices, gather_by_exchange(): lax.all_to_all(copies, axis, split_axis=0, concat_axis=concat_axis, tiled...  25.3 us
    unnamed x33, local copies, waits for them, and re-layouts  7.31 us
    slice x2, local copies, waits for them, and re-layouts, per_device(): first_powers = tail_powers[:, :, 0].T  3.32 us
  transfers between devices with their start and end apart: 4, of which 3 were waited for; matrix products, arithmetic and copies ran while one was open for 15% of the time, Pallas kernels for 0%

profile of v12, /device:TPU:6, one launch (start us, length us, event | category | flops | bytes accessed | tf_op | source)
XLA Modules:
  0.0 162.6 jit_solution(15017801418254980022)
XLA Ops:
  0.6 1.0 copy.155
  3.1 1.3 multiply_bitcast_fusion
  8.3 1.2 broadcast_multiply_fusion
  9.5 1.0 fusion.4
  10.7 1.0 copy.160
  12.5 10.1 %all-to-all-start = ((f32[16,26,128]{2,1,0:T(8,128)}), f32[16,26,128]{2,1,0:T(8,128)}, u32[]{:S(2)}, u32[]{:S(2)}) async-start(f32[16,26,128]{2,1,0:T(8,128)} %broadcast_in_dim.26), calls=%async_computation | async-start | bytes 524288 | tf_op jit(solution)/shard_map/all_to_all | solution.py:20
  22.6 1.2 fusion.72
  25.8 1.7 %fusion.71 = (f32[128,16,1]{2,1,0:T(8,128)}, f32[128,16,1]{2,1,0:T(8,128)}) fusion(f32[128,16,128]{2,1,0:T(8,128)S(1)} %broadcast_multiply_fusion), kind=kLoop, calls=%fused_computation.133 | loop fusion | bytes 32768 | tf_op jit(solution)/shard_map/slice | solution.py:116
  29.1 0.9 copy.166
  30.0 0.9 convolution_bitcast_fusion
  31.2 1.0 multiply_reduce_fusion.3
  32.2 1.0 copy.203
  33.2 0.9 concatenate.50
  34.9 0.9 fusion.75
  35.9 2.1 %convolution_add_fusion = f32[128,8,16]{2,1,0:T(8,128)S(1)} fusion(f32[128,8,16]{2,1,0:T(8,128)S(1)} %fusion.75, f32[128,16,128]{2,1,0:T(8,128)S(1)} %get-tuple-element.9, f32[128,16,8]{1,2,0:T(8,128)} %copy.203, f32[128,16]{1,0:T(8,128)S(1)} %copy.163), kind=kOutput, calls=%fused_computation.6 | convolution fusion | flops 3178496 | bytes 1253376 | tf_op jit(solution)/shard_map/cnm,cmi->cni/dot_general | solution.py:54
  39.5 1.6 %copy.178 = f32[128,16,1]{0,1,2:T(8,128)S(1)} copy(f32[128,16,1]{2,1,0:T(8,128)} %get-tuple-element.16) | data formatting | bytes 16384 | tf_op jit(solution)/shard_map/slice | solution.py:116
  41.7 1.7 %copy.182 = bf16[128,4096]{0,1:T(8,128)(2,1)S(1)} copy(bf16[128,4096]{1,0:T(8,128)(2,1)} %param.13) | data formatting | bytes 2097152 | tf_op args[5]
  44.4 1.1 copy.171
  47.5 1.0 multiply_reduce_fusion.4
  50.2 1.9 %collective-permute-start = (bf16[16,128,128]{2,1,0:T(8,128)(2,1)S(1)}, bf16[16,128,128]{2,1,0:T(8,128)(2,1)S(1)}, u32[]{:S(2)}, u32[]{:S(2)}) collective-permute-start(bf16[16,128,128]{2,1,0:T(8,128)(2,1)S(1)} %fusion.11), channel_id=1, source_target_pairs={{0,1},{1,0},{2,3},{3,2},{4,5},{5,4},{6,7},{7,6},{8,9},{9,8},{10,11... | collective-permute-start | bytes 1572872 | tf_op jit(solution)/shard_map/ppermute | solution.py:152
  52.1 1.9 %collective-permute-done = bf16[16,128,128]{2,1,0:T(8,128)(2,1)S(1)} collective-permute-done((bf16[16,128,128]{2,1,0:T(8,128)(2,1)S(1)}, bf16[16,128,128]{2,1,0:T(8,128)(2,1)S(1)}, u32[]{:S(2)}, u32[]{:S(2)}) %collective-permute-start) | collective-permute-done | bytes 524320 | tf_op jit(solution)/shard_map/ppermute | solution.py:152
  54.2 28.3 %all_to_all.24 = bf16[16,128,128]{2,1,0:T(8,128)(2,1)S(1)} all-to-all(bf16[16,128,128]{2,1,0:T(8,128)(2,1)S(1)} %fusion.6), channel_id=1, replica_groups={{0,2,4,6,8,10,12,14,16,18,20,22,24,26,28,30},{1,3,5,7,9,11,13,15,17,19,..., dimensions={0} | all-to-all | bytes 1048576 | tf_op jit(solution)/shard_map/all_to_all | solution.py:155
  82.7 1.3 broadcast_in_dim_broadcast_in_dim.2
  84.0 5.6 %all-to-all-start.2 = ((bf16[32,128,1,128]{1,3,2,0:T(8,128)(2,1)}), bf16[32,128,1,128]{1,3,2,0:T(8,128)(2,1)}, u32[]{:S(2)}, u32[]{:S(2)}) async-start(bf16[32,128,1,128]{1,3,2,0:T(8,128)(2,1)} %broadcast_in_dim_broadcast_in_dim.2), calls=%async_computation.2 | async-start | bytes 2097152 | tf_op jit(solution)/shard_map/all_to_all | solution.py:20
  89.6 3.2 %copy.189 = bf16[4096,3,128]{0,2,1:T(8,128)(2,1)S(1)} copy(bf16[4096,3,128]{2,0,1:T(8,128)(2,1)} %param.15) | data formatting | bytes 6291456 | tf_op args[7]
  92.8 25.8 %all-to-all-done.2 = bf16[32,128,1,128]{1,3,2,0:T(8,128)(2,1)} async-done(((bf16[32,128,1,128]{1,3,2,0:T(8,128)(2,1)}), bf16[32,128,1,128]{1,3,2,0:T(8,128)(2,1)}, u32[]{:S(2)}, u32[]{:S(2)}) %all-to-all-start.2) | async-done | bytes 1048608 | tf_op jit(solution)/shard_map/all_to_all | solution.py:20
  118.7 1.8 %fusion.2 = (f32[128]{0:T(128)S(1)}, bf16[32,1,128,1,128]{2,4,0,3,1:T(8,128)(2,1)S(1)}) fusion(bf16[32,128,1,128]{1,3,2,0:T(8,128)(2,1)} %all-to-all-done.2, f32[32,128]{1,0:T(8,128)S(1)} %bitcast.137), kind=kLoop, calls=%fused_computation.5 | loop fusion | flops 2621312 | bytes 2114048 | tf_op jit(solution)/shard_map/reduce_sum | solution.py:162
  120.4 1.1 convolution_multiply_fusion.1
  122.4 1.1 broadcast_in_dim.35
  123.5 9.6 %all-to-all-start.3 = ((bf16[16,128,256]{2,1,0:T(8,128)(2,1)}), bf16[16,128,256]{2,1,0:T(8,128)(2,1)S(1)}, u32[]{:S(2)}, u32[]{:S(2)}) async-start(bf16[16,128,256]{2,1,0:T(8,128)(2,1)} %broadcast_in_dim.35), calls=%async_computation.3 | async-start | bytes 2097152 | tf_op jit(solution)/shard_map/all_to_all | solution.py:20
  133.1 27.7 %all-to-all-done.3 = bf16[16,128,256]{2,1,0:T(8,128)(2,1)S(1)} async-done(((bf16[16,128,256]{2,1,0:T(8,128)(2,1)}), bf16[16,128,256]{2,1,0:T(8,128)(2,1)S(1)}, u32[]{:S(2)}, u32[]{:S(2)}) %all-to-all-start.3) | async-done | bytes 1048608 | tf_op jit(solution)/shard_map/all_to_all | solution.py:20
  161.6 1.0 fusion.3
  (108 shorter events, 19.4 us)
Async XLA Ops:
  5.3 2.2 %copy-start.9 = (f32[3,128]{1,0:T(4,128)}, f32[3,128]{1,0:T(4,128)S(1)}, u32[]{:S(2)}) copy-start(f32[3,128]{1,0:T(4,128)S(1)} %get-tuple-element.39) | copy-start | bytes 4612
  5.3 2.2 %copy-start.10 = (f32[3,128]{1,0:T(4,128)}, f32[3,128]{1,0:T(4,128)S(1)}, u32[]{:S(2)}) copy-start(f32[3,128]{1,0:T(4,128)S(1)} %get-tuple-element.38) | copy-start | bytes 4612
  5.3 2.2 %copy-start.11 = (f32[3,128]{1,0:T(4,128)}, f32[3,128]{1,0:T(4,128)S(1)}, u32[]{:S(2)}) copy-start(f32[3,128]{1,0:T(4,128)S(1)} %get-tuple-element.40) | copy-start | bytes 4612
  5.6 0.7 copy-start.1
  6.3 17.5 %copy-start.3 = (bf16[128,128]{1,0:T(8,128)(2,1)}, bf16[128,128]{1,0:T(8,128)(2,1)S(1)}, u32[]{:S(2)}) copy-start(bf16[128,128]{1,0:T(8,128)(2,1)S(1)} %fusion.45) | copy-start | bytes 98308
  12.5 31.9 %all-to-all-start = ((f32[16,26,128]{2,1,0:T(8,128)}), f32[16,26,128]{2,1,0:T(8,128)}, u32[]{:S(2)}, u32[]{:S(2)}) async-start(f32[16,26,128]{2,1,0:T(8,128)} %broadcast_in_dim.26), calls=%async_computation | async-start | bytes 524288 | tf_op jit(solution)/shard_map/all_to_all | solution.py:20
  34.9 6.3 %copy-start = (f32[128,16,1]{2,1,0:T(8,128)S(1)}, f32[128,16,1]{2,1,0:T(8,128)}, u32[]{:S(2)}) copy-start(f32[128,16,1]{2,1,0:T(8,128)} %get-tuple-element.17) | copy-start | bytes 24580
  35.9 5.8 %copy-start.2 = (f32[2,3,128]{0,2,1:T(8,128)S(1)}, f32[2,3,128]{0,2,1:T(8,128)}, u32[]{:S(2)}) copy-start(f32[2,3,128]{0,2,1:T(8,128)} %get-tuple-element.25) | copy-start | bytes 9220
  38.0 5.4 %copy-start.13 = (f32[3,3,128]{2,1,0:T(4,128)S(1)}, f32[3,3,128]{2,1,0:T(4,128)}, u32[]{:S(2)}) copy-start(f32[3,3,128]{2,1,0:T(4,128)} %param.10) | copy-start | bytes 13828
  39.5 7.9 %copy-start.4 = (bf16[128,128]{1,0:T(8,128)(2,1)S(1)}, bf16[128,128]{1,0:T(8,128)(2,1)}, u32[]{:S(2)}) copy-start(bf16[128,128]{1,0:T(8,128)(2,1)} %copy-done.3) | copy-start | bytes 98308
  41.6 7.2 %copy-start.5 = (f32[128,8,16]{0,2,1:T(8,128)S(1)}, f32[128,8,16]{0,2,1:T(8,128)}, u32[]{:S(2)}) copy-start(f32[128,8,16]{0,2,1:T(8,128)} %copy.169) | copy-start | bytes 196612
  41.7 7.6 %copy-start.6 = (f32[128,128]{1,0:T(8,128)S(1)}, f32[128,128]{1,0:T(8,128)}, u32[]{:S(2)}) copy-start(f32[128,128]{1,0:T(8,128)} %concatenate.51) | copy-start | bytes 196612
  50.1 32.5 %copy-start.8 = (bf16[128,128]{1,0:T(8,128)(2,1)S(1)}, bf16[128,128]{1,0:T(8,128)(2,1)}, u32[]{:S(2)}) copy-start(bf16[128,128]{1,0:T(8,128)(2,1)} %param.8) | copy-start | bytes 98308
  50.2 3.8 %collective-permute-start = (bf16[16,128,128]{2,1,0:T(8,128)(2,1)S(1)}, bf16[16,128,128]{2,1,0:T(8,128)(2,1)S(1)}, u32[]{:S(2)}, u32[]{:S(2)}) collective-permute-start(bf16[16,128,128]{2,1,0:T(8,128)(2,1)S(1)} %fusion.11), channel_id=1, source_target_pairs={{0,1},{1,0},{2,3},{3,2},{4,5},{5,4},{6,7},{7,6},{8,9},{9,8},{10,11... | collective-permute-start | bytes 1572872 | tf_op jit(solution)/shard_map/ppermute | solution.py:152
  82.6 10.2 %copy-start.7 = (bf16[128,128]{1,0:T(8,128)(2,1)}, bf16[128,128]{1,0:T(8,128)(2,1)S(1)}, u32[]{:S(2)}) copy-start(bf16[128,128]{1,0:T(8,128)(2,1)S(1)} %add_convert_fusion) | copy-start | bytes 98308
  84.0 34.7 %all-to-all-start.2 = ((bf16[32,128,1,128]{1,3,2,0:T(8,128)(2,1)}), bf16[32,128,1,128]{1,3,2,0:T(8,128)(2,1)}, u32[]{:S(2)}, u32[]{:S(2)}) async-start(bf16[32,128,1,128]{1,3,2,0:T(8,128)(2,1)} %broadcast_in_dim_broadcast_in_dim.2), calls=%async_computation.2 | async-start | bytes 2097152 | tf_op jit(solution)/shard_map/all_to_all | solution.py:20
  89.6 29.1 %copy-start.12 = (f32[4096]{0:T(1024)S(1)}, f32[4096]{0:T(1024)}, u32[]{:S(2)}) copy-start(f32[4096]{0:T(1024)} %param.14) | copy-start | bytes 49156
  123.5 37.3 %all-to-all-start.3 = ((bf16[16,128,256]{2,1,0:T(8,128)(2,1)}), bf16[16,128,256]{2,1,0:T(8,128)(2,1)S(1)}, u32[]{:S(2)}, u32[]{:S(2)}) async-start(bf16[16,128,256]{2,1,0:T(8,128)(2,1)} %broadcast_in_dim.35), calls=%async_computation.3 | async-start | bytes 2097152 | tf_op jit(solution)/shard_map/all_to_all | solution.py:20

commit v13 on v11

--- a/solution.py
+++ b/solution.py
@@ -42,22 +42,22 @@
     filter_taps = jnp.sum(weight[:, :, None] * powers, axis=1)
     toeplitz = toeplitz_lower(filter_taps)
     blocks = signal.reshape(chan_count, block_count, block_size)
-    inner_part = jnp.einsum("cij,cnj->cni", toeplitz, blocks, precision=highest)
+    inner_part = jnp.sum(toeplitz[:, None, :, :] * blocks[:, :, None, :], axis=3)
     tail_powers = jnp.exp(-rates[:, :, None] * (block_size - lag_steps))
-    end_states = jnp.einsum("cnj,cmj->cnm", blocks, tail_powers, precision=highest)
+    end_states = jnp.sum(blocks[:, :, None, :] * tail_powers[:, None, :, :], axis=3)
     block_steps = jnp.arange(block_count, dtype=jnp.float32)
     gap_count = block_steps[:, None] - 1.0 - block_steps[None, :]
     live_mask = gap_count >= 0.0
     carry_mat = jnp.where(
         live_mask, jnp.exp(-rates[:, :, None, None] * block_size * jnp.maximum(gap_count, 0.0)), 0.0
     )
-    states = jnp.einsum("cmnk,ckm->cnm", carry_mat, end_states, precision=highest)
+    states = jnp.sum(carry_mat * end_states.transpose(0, 2, 1)[:, :, None, :], axis=3).transpose(0, 2, 1)
     states = (
         states
         + jnp.exp(-rates[:, None, :] * block_size * block_steps[None, :, None])
         * start_state[:, None, :]
     )
-    cross_part = jnp.einsum("cnm,cmi->cni", states * weight[:, None, :], powers, precision=highest)
+    cross_part = jnp.sum((states * weight[:, None, :])[:, :, :, None] * powers[:, None, :, :], axis=2)
     return (inner_part + cross_part).reshape(chan_count, length)
 
 

time: 150 us -> 150 us (level)
  other arithmetic: 12.3 us -> 18.5 us
  matrix products: 7.05 us -> 3.12 us
  local copies, waits for them, and re-layouts: 16.1 us -> 14 us
    dot_general x3 -> x0, matrix products: 3.94 us -> none  [the longest x1 1.77 us: modal_conv(): jnp.einsum('cnj,cmj->cnm', blocks, tail_powers, precision=highest)]
    reduce_sum x1 -> x3, other arithmetic: 0.62 us -> 3.09 us  [the longest x1 1.11 us: modal_conv(): jnp.sum(blocks[:, :, None, :] * tail_powers[:, None, :, :], axis=3)]
    unnamed x36 -> x20, local copies, waits for them, and re-layouts: 6.18 us -> 3.9 us
  transfers between devices with their start and end apart: 4 -> 4, of which waited for: 3 -> 3; matrix products, arithmetic and copies ran while one was open for 12% -> 11% of each run, Pallas kernels for 0% -> 0%
where the time goes in v13:
time: 150 us; the launch traced here: 148 us
  waiting for transfers between devices  55.3 us (37%)
  blocking collectives  28.3 us (19%)
  starting transfers between devices  27.2 us (18%)
  other arithmetic  18.5 us (12%)
  local copies, waits for them, and re-layouts  14 us (9%)
  matrix products  3.12 us (2%)
    all_to_all x3, waiting for transfers between devices, gather_by_exchange(): lax.all_to_all(copies, axis, split_axis=0, concat_axis=concat_axis, tiled...  53.5 us
    all_to_all x1, blocking collectives, per_device(): lax.all_to_all(chip_sum, 'tp', split_axis=0, concat_axis=0, axis_index_gr...  28.3 us
    all_to_all x3, starting transfers between devices, gather_by_exchange(): lax.all_to_all(copies, axis, split_axis=0, concat_axis=concat_axis, tiled...  25.3 us
    unnamed x20, local copies, waits for them, and re-layouts  3.9 us
  transfers between devices with their start and end apart: 4, of which 3 were waited for; matrix products, arithmetic and copies ran while one was open for 11% of the time, Pallas kernels for 0%

profile of v13, /device:TPU:6, one launch (start us, length us, event | category | flops | bytes accessed | tf_op | source)
XLA Modules:
  0.0 147.6 jit_solution(2147937619981893136)
XLA Ops:
  0.6 0.9 convert_element_type.105
  1.6 1.3 fusion.71
  2.8 0.7 slice.209
  3.5 0.7 slice_bitcast_fusion.12
  4.3 0.7 fusion.20
  5.0 0.9 fusion.69
  6.0 1.3 multiply_bitcast_fusion
  8.1 0.7 broadcast_in_dim.26
  8.8 10.1 %all-to-all-start = ((f32[16,26,128]{2,1,0:T(8,128)}), f32[16,26,128]{2,1,0:T(8,128)S(1)}, u32[]{:S(2)}, u32[]{:S(2)}) async-start(f32[16,26,128]{2,1,0:T(8,128)} %broadcast_in_dim.26), calls=%async_computation | async-start | bytes 524288 | tf_op jit(solution)/shard_map/all_to_all | solution.py:20
  22.5 1.3 multiply_exponential_fusion.3
  24.0 1.1 multiply_reduce_fusion.3
  25.1 1.0 multiply_reduce_fusion.5
  28.1 1.0 multiply_reduce_fusion.2
  29.1 0.8 add.106
  30.0 0.7 slice_bitcast_fusion.17
  30.7 0.8 slice_bitcast_fusion.5
  31.7 0.8 fusion.61
  32.6 0.8 multiply_reduce_fusion.6
  33.7 0.9 fusion.23
  35.3 1.9 %collective-permute-start = (bf16[16,128,128]{2,1,0:T(8,128)(2,1)S(1)}, bf16[16,128,128]{2,1,0:T(8,128)(2,1)S(1)}, u32[]{:S(2)}, u32[]{:S(2)}) collective-permute-start(bf16[16,128,128]{2,1,0:T(8,128)(2,1)S(1)} %fusion.10), channel_id=1, source_target_pairs={{0,1},{1,0},{2,3},{3,2},{4,5},{5,4},{6,7},{7,6},{8,9},{9,8},{10,11... | collective-permute-start | bytes 1572872 | tf_op jit(solution)/shard_map/ppermute | solution.py:160
  37.2 1.9 %collective-permute-done = bf16[16,128,128]{2,1,0:T(8,128)(2,1)S(1)} collective-permute-done((bf16[16,128,128]{2,1,0:T(8,128)(2,1)S(1)}, bf16[16,128,128]{2,1,0:T(8,128)(2,1)S(1)}, u32[]{:S(2)}, u32[]{:S(2)}) %collective-permute-start) | collective-permute-done | bytes 524320 | tf_op jit(solution)/shard_map/ppermute | solution.py:160
  39.3 28.3 %all_to_all.24 = bf16[16,128,128]{2,1,0:T(8,128)(2,1)S(1)} all-to-all(bf16[16,128,128]{2,1,0:T(8,128)(2,1)S(1)} %fusion.4), channel_id=1, replica_groups={{0,2,4,6,8,10,12,14,16,18,20,22,24,26,28,30},{1,3,5,7,9,11,13,15,17,19,..., dimensions={0} | all-to-all | bytes 1048576 | tf_op jit(solution)/shard_map/all_to_all | solution.py:163
  67.8 1.3 broadcast_in_dim_broadcast_in_dim.2
  69.1 5.6 %all-to-all-start.2 = ((bf16[32,128,1,128]{1,3,2,0:T(8,128)(2,1)}), bf16[32,128,1,128]{1,3,2,0:T(8,128)(2,1)}, u32[]{:S(2)}, u32[]{:S(2)}) async-start(bf16[32,128,1,128]{1,3,2,0:T(8,128)(2,1)} %broadcast_in_dim_broadcast_in_dim.2), calls=%async_computation.2 | async-start | bytes 2097152 | tf_op jit(solution)/shard_map/all_to_all | solution.py:20
  74.7 3.2 %copy.101 = bf16[4096,3,128]{0,2,1:T(8,128)(2,1)S(1)} copy(bf16[4096,3,128]{2,0,1:T(8,128)(2,1)} %param.15) | data formatting | bytes 6291456 | tf_op args[7]
  77.9 25.8 %all-to-all-done.2 = bf16[32,128,1,128]{1,3,2,0:T(8,128)(2,1)} async-done(((bf16[32,128,1,128]{1,3,2,0:T(8,128)(2,1)}), bf16[32,128,1,128]{1,3,2,0:T(8,128)(2,1)}, u32[]{:S(2)}, u32[]{:S(2)}) %all-to-all-start.2) | async-done | bytes 1048608 | tf_op jit(solution)/shard_map/all_to_all | solution.py:20
  103.7 1.8 %fusion.2 = (f32[128]{0:T(128)S(1)}, bf16[32,1,128,1,128]{2,4,0,3,1:T(8,128)(2,1)S(1)}) fusion(bf16[32,128,1,128]{1,3,2,0:T(8,128)(2,1)} %all-to-all-done.2, f32[32,128]{1,0:T(8,128)S(1)} %bitcast.141), kind=kLoop, calls=%fused_computation.5 | loop fusion | flops 2621312 | bytes 2114048 | tf_op jit(solution)/shard_map/reduce_sum | solution.py:170
  105.5 1.1 convolution_multiply_fusion.1
  107.5 1.1 broadcast_in_dim.31
  108.5 9.6 %all-to-all-start.3 = ((bf16[16,128,256]{2,1,0:T(8,128)(2,1)}), bf16[16,128,256]{2,1,0:T(8,128)(2,1)S(1)}, u32[]{:S(2)}, u32[]{:S(2)}) async-start(bf16[16,128,256]{2,1,0:T(8,128)(2,1)} %broadcast_in_dim.31), calls=%async_computation.3 | async-start | bytes 2097152 | tf_op jit(solution)/shard_map/all_to_all | solution.py:20
  118.2 27.7 %all-to-all-done.3 = bf16[16,128,256]{2,1,0:T(8,128)(2,1)S(1)} async-done(((bf16[16,128,256]{2,1,0:T(8,128)(2,1)}), bf16[16,128,256]{2,1,0:T(8,128)(2,1)S(1)}, u32[]{:S(2)}, u32[]{:S(2)}) %all-to-all-start.3) | async-done | bytes 1048608 | tf_op jit(solution)/shard_map/all_to_all | solution.py:20
  146.6 1.0 fusion.3
  (80 shorter events, 9.7 us)
Async XLA Ops:
  4.2 1.7 %copy-start.5 = (f32[3,128]{1,0:T(4,128)}, f32[3,128]{1,0:T(4,128)S(1)}, u32[]{:S(2)}) copy-start(f32[3,128]{1,0:T(4,128)S(1)} %get-tuple-element.41) | copy-start | bytes 4612
  4.2 1.7 %copy-start.6 = (f32[3,128]{1,0:T(4,128)}, f32[3,128]{1,0:T(4,128)S(1)}, u32[]{:S(2)}) copy-start(f32[3,128]{1,0:T(4,128)S(1)} %get-tuple-element.42) | copy-start | bytes 4612
  4.3 1.7 %copy-start.7 = (f32[3,128]{1,0:T(4,128)}, f32[3,128]{1,0:T(4,128)S(1)}, u32[]{:S(2)}) copy-start(f32[3,128]{1,0:T(4,128)S(1)} %get-tuple-element.43) | copy-start | bytes 4612
  7.8 19.6 %copy-start = (bf16[128,4096]{1,0:T(8,128)(2,1)S(1)}, bf16[128,4096]{1,0:T(8,128)(2,1)}, u32[]{:S(2)}) copy-start(bf16[128,4096]{1,0:T(8,128)(2,1)} %param.13) | copy-start | bytes 3145732
  8.8 22.7 %all-to-all-start = ((f32[16,26,128]{2,1,0:T(8,128)}), f32[16,26,128]{2,1,0:T(8,128)S(1)}, u32[]{:S(2)}, u32[]{:S(2)}) async-start(f32[16,26,128]{2,1,0:T(8,128)} %broadcast_in_dim.26), calls=%async_computation | async-start | bytes 524288 | tf_op jit(solution)/shard_map/all_to_all | solution.py:20
  21.4 4.7 %copy-start.3 = (f32[128,16]{0,1:T(8,128)S(1)}, f32[128,16]{0,1:T(8,128)}, u32[]{:S(2)}) copy-start(f32[128,16]{0,1:T(8,128)} %get-tuple-element.29) | copy-start | bytes 24580
  23.9 8.7 %copy-start.2 = (f32[16,128]{1,0:T(8,128)S(1)}, f32[16,128]{1,0:T(8,128)}, u32[]{:S(2)}) copy-start(f32[16,128]{1,0:T(8,128)} %get-tuple-element.28) | copy-start | bytes 24580
  35.1 32.5 %copy-start.4 = (bf16[128,128]{1,0:T(8,128)(2,1)S(1)}, bf16[128,128]{1,0:T(8,128)(2,1)}, u32[]{:S(2)}) copy-start(bf16[128,128]{1,0:T(8,128)(2,1)} %param.8) | copy-start | bytes 98308
  35.3 3.8 %collective-permute-start = (bf16[16,128,128]{2,1,0:T(8,128)(2,1)S(1)}, bf16[16,128,128]{2,1,0:T(8,128)(2,1)S(1)}, u32[]{:S(2)}, u32[]{:S(2)}) collective-permute-start(bf16[16,128,128]{2,1,0:T(8,128)(2,1)S(1)} %fusion.10), channel_id=1, source_target_pairs={{0,1},{1,0},{2,3},{3,2},{4,5},{5,4},{6,7},{7,6},{8,9},{9,8},{10,11... | collective-permute-start | bytes 1572872 | tf_op jit(solution)/shard_map/ppermute | solution.py:160
  67.7 10.2 %copy-start.1 = (bf16[128,128]{1,0:T(8,128)(2,1)}, bf16[128,128]{1,0:T(8,128)(2,1)S(1)}, u32[]{:S(2)}) copy-start(bf16[128,128]{1,0:T(8,128)(2,1)S(1)} %add_convert_fusion) | copy-start | bytes 98308
  69.1 34.7 %all-to-all-start.2 = ((bf16[32,128,1,128]{1,3,2,0:T(8,128)(2,1)}), bf16[32,128,1,128]{1,3,2,0:T(8,128)(2,1)}, u32[]{:S(2)}, u32[]{:S(2)}) async-start(bf16[32,128,1,128]{1,3,2,0:T(8,128)(2,1)} %broadcast_in_dim_broadcast_in_dim.2), calls=%async_computation.2 | async-start | bytes 2097152 | tf_op jit(solution)/shard_map/all_to_all | solution.py:20
  74.6 29.1 %copy-start.8 = (f32[4096]{0:T(1024)S(1)}, f32[4096]{0:T(1024)}, u32[]{:S(2)}) copy-start(f32[4096]{0:T(1024)} %param.14) | copy-start | bytes 49156
  108.5 37.3 %all-to-all-start.3 = ((bf16[16,128,256]{2,1,0:T(8,128)(2,1)}), bf16[16,128,256]{2,1,0:T(8,128)(2,1)S(1)}, u32[]{:S(2)}, u32[]{:S(2)}) async-start(bf16[16,128,256]{2,1,0:T(8,128)(2,1)} %broadcast_in_dim.31), calls=%async_computation.3 | async-start | bytes 2097152 | tf_op jit(solution)/shard_map/all_to_all | solution.py:20

commit v14 on v11

--- a/solution.py
+++ b/solution.py
@@ -52,11 +52,6 @@
         live_mask, jnp.exp(-rates[:, :, None, None] * block_size * jnp.maximum(gap_count, 0.0)), 0.0
     )
     states = jnp.einsum("cmnk,ckm->cnm", carry_mat, end_states, precision=highest)
-    states = (
-        states
-        + jnp.exp(-rates[:, None, :] * block_size * block_steps[None, :, None])
-        * start_state[:, None, :]
-    )
     cross_part = jnp.einsum("cnm,cmi->cni", states * weight[:, None, :], powers, precision=highest)
     return (inner_part + cross_part).reshape(chan_count, length)
 

time: 150 us -> 150 us (level)
    unnamed x36 -> x20, local copies, waits for them, and re-layouts: 6.18 us -> 6.14 us
where the time goes in v14:
time: 150 us; the launch traced here: 148 us
  waiting for transfers between devices  55.4 us (37%)
  blocking collectives  28.3 us (19%)
  starting transfers between devices  27.2 us (18%)
  local copies, waits for them, and re-layouts  15.3 us (10%)
  other arithmetic  13.7 us (9%)
  matrix products  6.9 us (5%)
    all_to_all x3, waiting for transfers between devices, gather_by_exchange(): lax.all_to_all(copies, axis, split_axis=0, concat_axis=concat_axis, tiled...  53.5 us
    all_to_all x1, blocking collectives, per_device(): lax.all_to_all(chip_sum, 'tp', split_axis=0, concat_axis=0, axis_index_gr...  28.3 us
    all_to_all x3, starting transfers between devices, gather_by_exchange(): lax.all_to_all(copies, axis, split_axis=0, concat_axis=concat_axis, tiled...  25.3 us
    unnamed x20, local copies, waits for them, and re-layouts  6.14 us
  transfers between devices with their start and end apart: 4, of which 3 were waited for; matrix products, arithmetic and copies ran while one was open for 12% of the time, Pallas kernels for 0%

profile of v14, /device:TPU:6, one launch (start us, length us, event | category | flops | bytes accessed | tf_op | source)
XLA Modules:
  0.0 147.9 jit_solution(12687678274211357386)
XLA Ops:
  0.6 0.9 convert_element_type.103
  1.6 1.3 fusion.73
  2.9 0.7 slice.210
  3.5 0.7 slice_bitcast_fusion.12
  5.0 1.3 multiply_bitcast_fusion
  7.2 0.7 broadcast_in_dim.26
  7.9 10.1 %all-to-all-start = ((f32[16,26,128]{2,1,0:T(8,128)}), f32[16,26,128]{2,1,0:T(8,128)S(1)}, u32[]{:S(2)}, u32[]{:S(2)}) async-start(f32[16,26,128]{2,1,0:T(8,128)} %broadcast_in_dim.26), calls=%async_computation | async-start | bytes 524288 | tf_op jit(solution)/shard_map/all_to_all | solution.py:20
  18.2 0.6 fusion.29
  19.3 0.7 fusion.62
  20.0 0.6 fusion.63
  23.9 0.9 copy.75
  24.8 0.9 fusion.75
  25.7 1.7 %convolution_bitcast_fusion = f32[128,16,8]{1,2,0:T(8,128)S(1)} fusion(bf16[128,8,16]{2,1,0:T(8,128)(2,1)S(1)} %copy.75, f32[16]{0:T(128)} %iota_subtract_fusion.2, f32[128,16]{1,0:T(8,128)S(1)} %copy.72), kind=kOutput, calls=%fused_computation.7 | convolution fusion | flops 3178496 | bytes 106560 | tf_op jit(solution)/shard_map/cnj,cmj->cnm/dot_general | solution.py:47
  27.6 1.0 multiply_reduce_fusion.3
  28.9 1.2 convolution_add_fusion
  30.3 1.6 %copy.82 = bf16[128,4096]{0,1:T(8,128)(2,1)S(1)} copy(bf16[128,4096]{1,0:T(8,128)(2,1)} %param.13) | data formatting | bytes 2097152 | tf_op args[5]
  32.2 0.8 fusion.66
  33.0 0.7 convert_subtract_fusion
  33.7 0.8 multiply_reduce_fusion.4
  35.6 1.9 %collective-permute-start = (bf16[16,128,128]{2,1,0:T(8,128)(2,1)S(1)}, bf16[16,128,128]{2,1,0:T(8,128)(2,1)S(1)}, u32[]{:S(2)}, u32[]{:S(2)}) collective-permute-start(bf16[16,128,128]{2,1,0:T(8,128)(2,1)S(1)} %fusion.12), channel_id=1, source_target_pairs={{0,1},{1,0},{2,3},{3,2},{4,5},{5,4},{6,7},{7,6},{8,9},{9,8},{10,11... | collective-permute-start | bytes 1572872 | tf_op jit(solution)/shard_map/ppermute | solution.py:155
  37.5 1.9 %collective-permute-done = bf16[16,128,128]{2,1,0:T(8,128)(2,1)S(1)} collective-permute-done((bf16[16,128,128]{2,1,0:T(8,128)(2,1)S(1)}, bf16[16,128,128]{2,1,0:T(8,128)(2,1)S(1)}, u32[]{:S(2)}, u32[]{:S(2)}) %collective-permute-start) | collective-permute-done | bytes 524320 | tf_op jit(solution)/shard_map/ppermute | solution.py:155
  39.5 28.3 %all_to_all.24 = bf16[16,128,128]{2,1,0:T(8,128)(2,1)S(1)} all-to-all(bf16[16,128,128]{2,1,0:T(8,128)(2,1)S(1)} %fusion.4), channel_id=1, replica_groups={{0,2,4,6,8,10,12,14,16,18,20,22,24,26,28,30},{1,3,5,7,9,11,13,15,17,19,..., dimensions={0} | all-to-all | bytes 1048576 | tf_op jit(solution)/shard_map/all_to_all | solution.py:158
  68.1 1.3 broadcast_in_dim_broadcast_in_dim.2
  69.3 5.6 %all-to-all-start.2 = ((bf16[32,128,1,128]{1,3,2,0:T(8,128)(2,1)}), bf16[32,128,1,128]{1,3,2,0:T(8,128)(2,1)}, u32[]{:S(2)}, u32[]{:S(2)}) async-start(bf16[32,128,1,128]{1,3,2,0:T(8,128)(2,1)} %broadcast_in_dim_broadcast_in_dim.2), calls=%async_computation.2 | async-start | bytes 2097152 | tf_op jit(solution)/shard_map/all_to_all | solution.py:20
  74.9 3.2 %copy.87 = bf16[4096,3,128]{0,2,1:T(8,128)(2,1)S(1)} copy(bf16[4096,3,128]{2,0,1:T(8,128)(2,1)} %param.15) | data formatting | bytes 6291456 | tf_op args[7]
  78.2 25.8 %all-to-all-done.2 = bf16[32,128,1,128]{1,3,2,0:T(8,128)(2,1)} async-done(((bf16[32,128,1,128]{1,3,2,0:T(8,128)(2,1)}), bf16[32,128,1,128]{1,3,2,0:T(8,128)(2,1)}, u32[]{:S(2)}, u32[]{:S(2)}) %all-to-all-start.2) | async-done | bytes 1048608 | tf_op jit(solution)/shard_map/all_to_all | solution.py:20
  104.0 1.8 %fusion.2 = (f32[128]{0:T(128)S(1)}, bf16[32,1,128,1,128]{2,4,0,3,1:T(8,128)(2,1)S(1)}) fusion(bf16[32,128,1,128]{1,3,2,0:T(8,128)(2,1)} %all-to-all-done.2, f32[32,128]{1,0:T(8,128)S(1)} %bitcast.140), kind=kLoop, calls=%fused_computation.5 | loop fusion | flops 2621312 | bytes 2114048 | tf_op jit(solution)/shard_map/reduce_sum | solution.py:165
  105.8 1.1 convolution_multiply_fusion.1
  107.7 1.1 broadcast_in_dim.31
  108.8 9.6 %all-to-all-start.3 = ((bf16[16,128,256]{2,1,0:T(8,128)(2,1)}), bf16[16,128,256]{2,1,0:T(8,128)(2,1)S(1)}, u32[]{:S(2)}, u32[]{:S(2)}) async-start(bf16[16,128,256]{2,1,0:T(8,128)(2,1)} %broadcast_in_dim.31), calls=%async_computation.3 | async-start | bytes 2097152 | tf_op jit(solution)/shard_map/all_to_all | solution.py:20
  118.5 27.7 %all-to-all-done.3 = bf16[16,128,256]{2,1,0:T(8,128)(2,1)S(1)} async-done(((bf16[16,128,256]{2,1,0:T(8,128)(2,1)}), bf16[16,128,256]{2,1,0:T(8,128)(2,1)S(1)}, u32[]{:S(2)}, u32[]{:S(2)}) %all-to-all-start.3) | async-done | bytes 1048608 | tf_op jit(solution)/shard_map/all_to_all | solution.py:20
  146.9 1.0 fusion.3
  (84 shorter events, 9.2 us)
Async XLA Ops:
  4.3 0.7 copy-start.3
  4.3 0.7 copy-start.4
  4.3 0.7 copy-start.5
  4.4 0.6 copy-start
  7.9 24.1 %all-to-all-start = ((f32[16,26,128]{2,1,0:T(8,128)}), f32[16,26,128]{2,1,0:T(8,128)S(1)}, u32[]{:S(2)}, u32[]{:S(2)}) async-start(f32[16,26,128]{2,1,0:T(8,128)} %broadcast_in_dim.26), calls=%async_computation | async-start | bytes 524288 | tf_op jit(solution)/shard_map/all_to_all | solution.py:20
  27.4 4.5 %copy-start.7 = (f32[3,3,128]{2,1,0:T(4,128)S(1)}, f32[3,3,128]{2,1,0:T(4,128)}, u32[]{:S(2)}) copy-start(f32[3,3,128]{2,1,0:T(4,128)} %param.10) | copy-start | bytes 13828
  35.4 32.5 %copy-start.2 = (bf16[128,128]{1,0:T(8,128)(2,1)S(1)}, bf16[128,128]{1,0:T(8,128)(2,1)}, u32[]{:S(2)}) copy-start(bf16[128,128]{1,0:T(8,128)(2,1)} %param.8) | copy-start | bytes 98308
  35.6 3.8 %collective-permute-start = (bf16[16,128,128]{2,1,0:T(8,128)(2,1)S(1)}, bf16[16,128,128]{2,1,0:T(8,128)(2,1)S(1)}, u32[]{:S(2)}, u32[]{:S(2)}) collective-permute-start(bf16[16,128,128]{2,1,0:T(8,128)(2,1)S(1)} %fusion.12), channel_id=1, source_target_pairs={{0,1},{1,0},{2,3},{3,2},{4,5},{5,4},{6,7},{7,6},{8,9},{9,8},{10,11... | collective-permute-start | bytes 1572872 | tf_op jit(solution)/shard_map/ppermute | solution.py:155
  67.9 10.2 %copy-start.1 = (bf16[128,128]{1,0:T(8,128)(2,1)}, bf16[128,128]{1,0:T(8,128)(2,1)S(1)}, u32[]{:S(2)}) copy-start(bf16[128,128]{1,0:T(8,128)(2,1)S(1)} %add_convert_fusion) | copy-start | bytes 98308
  69.3 34.6 %all-to-all-start.2 = ((bf16[32,128,1,128]{1,3,2,0:T(8,128)(2,1)}), bf16[32,128,1,128]{1,3,2,0:T(8,128)(2,1)}, u32[]{:S(2)}, u32[]{:S(2)}) async-start(bf16[32,128,1,128]{1,3,2,0:T(8,128)(2,1)} %broadcast_in_dim_broadcast_in_dim.2), calls=%async_computation.2 | async-start | bytes 2097152 | tf_op jit(solution)/shard_map/all_to_all | solution.py:20
  74.9 29.1 %copy-start.6 = (f32[4096]{0:T(1024)S(1)}, f32[4096]{0:T(1024)}, u32[]{:S(2)}) copy-start(f32[4096]{0:T(1024)} %param.14) | copy-start | bytes 49156
  108.8 37.3 %all-to-all-start.3 = ((bf16[16,128,256]{2,1,0:T(8,128)(2,1)}), bf16[16,128,256]{2,1,0:T(8,128)(2,1)S(1)}, u32[]{:S(2)}, u32[]{:S(2)}) async-start(bf16[16,128,256]{2,1,0:T(8,128)(2,1)} %broadcast_in_dim.31), calls=%async_computation.3 | async-start | bytes 2097152 | tf_op jit(solution)/shard_map/all_to_all | solution.py:20
